TPU v7x, 256 devices: a whole 4x4x8 slice. The times are simulated.
256 devices in a mesh: seq: 64 (over x, z, core), batch: 4 (over y).
Axes of the slice: x: 4, y: 4, z: 8, core: 2. Of those that a mesh axis runs over, the one named last changes fastest.
Arguments:
- token_ids: int32 [4, 16384], P('batch', 'seq'), may hold values from 0 to 15
- input_table: bfloat16 [16, 3840], replicated, may hold values from -6 to 6
- gate_table: bfloat16 [16, 3584], replicated, may hold values from -6 to 6
- step_table: float32 [16, 56], replicated, may hold values from -4.5 to -1.5
- decay_log: float32 [56], replicated, may hold values from -12 to 0
- conv_weight: float32 [4, 3840], replicated, may hold values from -3 to 3
- conv_bias: float32 [3840], replicated, may hold values from -3 to 3
- skip_gain: float32 [56], replicated, may hold values from 0.25 to 1.75
- norm_gain: float32 [3584], replicated, may hold values from 0.5 to 1.5
- cotangent: bfloat16 [4, 16384, 3584], P('batch', 'seq'), may hold values from -1 to 1
Outputs:
- layer_out: bfloat16 [4, 16384, 3584], P('batch', 'seq')
- input_grad: float32 [16, 3840], replicated
- gate_grad: float32 [16, 3584], replicated
- step_grad: float32 [16, 56], replicated
- decay_grad: float32 [56], replicated
- conv_weight_grad: float32 [4, 3840], replicated
- conv_bias_grad: float32 [3840], replicated
- skip_grad: float32 [56], replicated
- norm_grad: float32 [3584], replicated
All inputs are finite; a program needn't handle non-finite values.
Results may differ from a plain program's by a relative error of at most 0.014.
Values sent between devices are 32-bit elements; how exact they have to be, the bound alone decides.
No kernel may reach another device: no remote copies, remote signals or barrier semaphores. Data moves between devices by JAX's collectives and lax.ppermute only.
A program may use at most 320 MiB of HBM per device.

v0:
```python
from functools import partial

import jax
import jax.numpy as jnp
from jax import lax
from jax.sharding import PartitionSpec as P

BLOCK = 128


EPS = 1e-05
HIGH = lax.Precision.HIGHEST


def shifted(value, axis, steps):
    count = lax.axis_size(axis)
    leading, last = (max(0, -steps), min(count, count - steps))
    return lax.ppermute(value, axis, [(source, source + steps) for source in range(leading, last)])


def indicator(labels, vocab, kind):
    return (labels[:, None] == jnp.arange(vocab, dtype=jnp.int32)[None, :]).astype(kind)


def prepare(raw_rows, step_rows, decay_log, conv_weight, conv_bias, inner, heads):
    width = conv_weight.shape[0]
    tokens = raw_rows.shape[0] - width + 1
    state = (raw_rows.shape[1] - inner) // 2
    convolved = conv_bias[None, :] + conv_weight[0][None, :] * raw_rows[0:tokens]
    for offset in range(1, width):
        convolved = convolved + conv_weight[offset][None, :] * raw_rows[offset : offset + tokens]
    active = jax.nn.silu(convolved)
    values = active[:, :inner].astype(jnp.bfloat16).reshape(tokens, heads, inner // heads)
    write_keys = active[:, inner : inner + state].astype(jnp.bfloat16)
    read_keys = active[:, inner + state :].astype(jnp.bfloat16)
    steps = jax.nn.softplus(step_rows)
    log_decay = -jnp.exp(decay_log)[None, :] * steps
    return (values, write_keys, read_keys, steps, log_decay)


def group_states(values, write_keys, steps, log_decay):
    tokens, heads, head = values.shape
    count = tokens // BLOCK
    cum = jnp.cumsum(log_decay.reshape(count, BLOCK, heads), axis=1)
    factor = jnp.exp(cum[:, -1:, :] - cum) * steps.reshape(count, BLOCK, heads)
    weighted = (values.reshape(count, BLOCK, heads, head) * factor[..., None]).astype(jnp.bfloat16)
    return jnp.einsum(
        "cshp,csn->chpn",
        weighted,
        write_keys.reshape(count, BLOCK, -1),
        preferred_element_type=jnp.float32,
    )


def local_states(pieces, log_decay):
    count = pieces.shape[0]
    block_total = jnp.sum(log_decay.reshape(count, BLOCK, -1), axis=1)

    def advance(carried, item):
        piece, total = item
        return (jnp.exp(total)[:, None, None] * carried + piece, carried)

    final, entering = lax.scan(
        advance, jnp.zeros_like(pieces[0]), (pieces, block_total), unroll=True
    )
    return (entering, final, jnp.sum(block_total, axis=0))


def intra(values, write_keys, read_keys, steps, log_decay):
    tokens, heads, head = values.shape
    count = tokens // BLOCK
    cum = jnp.cumsum(log_decay.reshape(count, BLOCK, heads), axis=1)
    writes = write_keys.reshape(count, BLOCK, -1)
    reads = read_keys.reshape(count, BLOCK, -1)
    scores = jnp.einsum("ctn,csn->cts", reads, writes, preferred_element_type=jnp.float32)
    lower = (
        lax.broadcasted_iota(jnp.int32, (BLOCK, BLOCK), 0)
        >= lax.broadcasted_iota(jnp.int32, (BLOCK, BLOCK), 1)
    )[None, None]
    track = jnp.transpose(cum, (0, 2, 1))
    power = track[:, :, :, None] - track[:, :, None, :]
    fade = jnp.where(lower, jnp.exp(jnp.where(lower, power, 0.0)), 0.0)
    widths = jnp.transpose(steps.reshape(count, BLOCK, heads), (0, 2, 1))
    mixing = (scores[:, None] * fade * widths[:, :, None, :]).astype(jnp.bfloat16)
    blocked = values.reshape(count, BLOCK, heads, head)
    return jnp.einsum("chts,cshp->cthp", mixing, blocked, preferred_element_type=jnp.float32)


def mixer_output(
    values,
    read_keys,
    log_decay,
    entering,
    carried,
    within,
    gate_rows,
    skip_gain,
    norm_gain,
):
    tokens, heads, head = values.shape
    count = tokens // BLOCK
    cum = jnp.cumsum(log_decay.reshape(count, BLOCK, heads), axis=1)
    block_total = cum[:, -1, :]
    before = jnp.cumsum(block_total, axis=0) - block_total
    states = entering + jnp.exp(before)[:, :, None, None] * carried[None]
    reads = read_keys.reshape(count, BLOCK, -1)
    blocked = values.reshape(count, BLOCK, heads, head)
    across = jnp.exp(cum)[..., None] * jnp.einsum(
        "ctn,chpn->cthp", reads, states.astype(jnp.bfloat16), preferred_element_type=jnp.float32
    )
    mixed = within + across + skip_gain[None, None, :, None] * blocked
    gated = mixed.reshape(tokens, heads * head) * jax.nn.silu(gate_rows)
    scale = lax.rsqrt(jnp.mean(gated * gated, axis=1, keepdims=True) + EPS)
    return (gated * scale * norm_gain[None, :]).astype(jnp.bfloat16)


def carry_weights(logs, backward):
    parts = logs.shape[1]
    inclusive = jnp.cumsum(logs, axis=1)
    exclusive = inclusive - logs
    rows = lax.broadcasted_iota(jnp.int32, (parts, parts), 0)
    cols = lax.broadcasted_iota(jnp.int32, (parts, parts), 1)
    if backward:
        keep = (cols > rows)[None]
        power = exclusive[:, None, :] - inclusive[:, :, None]
    else:
        keep = (cols < rows)[None]
        power = exclusive[:, :, None] - inclusive[:, None, :]
    return jnp.where(keep, jnp.exp(jnp.where(keep, power, 0.0)), 0.0)


def settle_forward(pieces):
    states_in, totals_in = pieces
    weights = carry_weights(totals_in[:, :, 0], False)
    settled = jnp.einsum("hij,hjw->hiw", weights, states_in, precision=HIGH)
    return lax.all_to_all(settled, "seq", split_axis=1, concat_axis=1, tiled=True)


def settle_backward(pieces):
    states_in, totals_in = pieces
    weights = carry_weights(totals_in[:, :, 0], True)
    settled = jnp.einsum("hij,hjw->hiw", weights, states_in, precision=HIGH)
    return lax.all_to_all(settled, "seq", split_axis=1, concat_axis=1, tiled=True)


def spread_sum(flat, axes):
    count = 1
    for axis in axes:
        count *= lax.axis_size(axis)
    size = flat.shape[0]
    chunk = -(-size // count)
    padded = jnp.pad(flat, (0, chunk * count - size)).reshape(count, chunk)
    gathered = lax.all_to_all(padded, axes, split_axis=0, concat_axis=0, tiled=True)
    reduced = jnp.sum(gathered, axis=0, keepdims=True)
    spread = jnp.broadcast_to(reduced, (count, chunk))
    whole = lax.all_to_all(spread, axes, split_axis=0, concat_axis=0, tiled=True)
    return whole.reshape(-1)[:size]


def local(
    token_ids,
    input_table,
    gate_table,
    step_table,
    decay_log,
    conv_weight,
    conv_bias,
    skip_gain,
    norm_gain,
    cotangent,
):
    labels = token_ids[0]
    tokens = labels.shape[0]
    width = conv_weight.shape[0]
    vocab = input_table.shape[0]
    inner = gate_table.shape[1]
    heads = step_table.shape[1]
    rim = shifted(labels[tokens - width + 1 :] + 1, "seq", 1) - 1
    extended = jnp.concatenate([rim, labels])
    wide_hot = indicator(extended, vocab, jnp.bfloat16)
    own_hot = wide_hot[width - 1 :]
    raw_rows = jnp.dot(wide_hot, input_table, preferred_element_type=jnp.float32)
    gate_rows = jnp.dot(own_hot, gate_table, preferred_element_type=jnp.float32)
    step_rows = jnp.dot(own_hot.astype(jnp.float32), step_table, precision=HIGH)
    features, pull_prepare = jax.vjp(
        partial(prepare, inner=inner, heads=heads),
        raw_rows,
        step_rows,
        decay_log,
        conv_weight,
        conv_bias,
    )
    values, write_keys, read_keys, steps, log_decay = features
    pieces, pull_groups = jax.vjp(group_states, values, write_keys, steps, log_decay)
    (entering, final, total), pull_local = jax.vjp(local_states, pieces, log_decay)
    flat = final.reshape(heads, -1)
    parts = lax.axis_size("seq")
    span = flat.shape[1] // parts
    total_row = jnp.zeros((1, parts, span), jnp.float32).at[0, :, :heads].set(
        jnp.broadcast_to(total[None, :], (parts, heads))
    )
    outgoing = jnp.concatenate([flat.reshape(heads, parts, span), total_row], axis=0)
    within, pull_intra = jax.vjp(intra, values, write_keys, read_keys, steps, log_decay)
    incoming = lax.all_to_all(outgoing, "seq", split_axis=1, concat_axis=1, tiled=True)
    incoming, within = lax.optimization_barrier((incoming, within))
    totals = jnp.transpose(incoming[heads, :, :heads])[:, :, None]
    carried = settle_forward((incoming[:heads], totals))
    layer_out, pull_out = jax.vjp(
        mixer_output,
        values,
        read_keys,
        log_decay,
        entering,
        carried,
        within,
        gate_rows,
        skip_gain,
        norm_gain,
    )
    d_values, d_read, d_log, d_entering, d_carried, d_within, d_gate, d_skip, d_norm = pull_out(
        cotangent[0]
    )
    back_flat = d_carried.reshape(heads, -1)
    back_incoming = lax.all_to_all(
        back_flat.reshape(heads, parts, span), "seq", split_axis=1, concat_axis=1, tiled=True
    )
    d_intra = pull_intra(d_within)
    back_incoming, d_intra = lax.optimization_barrier((back_incoming, d_intra))
    later = settle_backward((back_incoming, totals))
    d_total = jnp.exp(total) * jnp.sum(later * carried, axis=(1, 2))
    d_pieces, d_log_local = pull_local((d_entering, later, d_total))
    d_values_state, d_write_state, d_steps_state, d_log_state = pull_groups(d_pieces)
    d_raw, d_step_rows, d_decay, d_taps, d_shift = pull_prepare(
        (
            d_values + d_intra[0] + d_values_state,
            d_intra[1] + d_write_state,
            d_read + d_intra[2],
            d_intra[3] + d_steps_state,
            d_log + d_intra[4] + d_log_state + d_log_local,
        )
    )
    wide_float = wide_hot.astype(jnp.float32)
    own_float = wide_float[width - 1 :]
    parts_list = (
        jnp.dot(wide_float.T, d_raw, precision=HIGH),
        jnp.dot(own_float.T, d_gate, precision=HIGH),
        jnp.dot(own_float.T, d_step_rows, precision=HIGH),
        d_decay,
        d_taps,
        d_shift,
        d_skip,
        d_norm,
    )
    packed = jnp.concatenate([part.reshape(-1) for part in parts_list])
    packed = spread_sum(packed, ("seq", "batch"))
    sums = []
    offset = 0
    for part in parts_list:
        sums.append(packed[offset : offset + part.size].reshape(part.shape))
        offset += part.size
    return (layer_out[None], sums[0], sums[1], sums[2], sums[3], sums[4], sums[5], sums[6], sums[7])


def solution(mesh):
    return jax.shard_map(
        local,
        mesh=mesh,
        in_specs=(
            P("batch", "seq"),
            P(),
            P(),
            P(),
            P(),
            P(),
            P(),
            P(),
            P(),
            P("batch", "seq", None),
        ),
        out_specs=(P("batch", "seq", None), P(), P(), P(), P(), P(), P(), P(), P()),
        check_vma=False,
    )
```

profile of v0, /device:TPU:1, one launch (start us, length us, event | category | flops | bytes accessed | tf_op | source)
XLA Modules:
  0.0 437.7 jit_solution(4301305758779537066)
XLA Ops:
  1.4 4.9 %collective-permute-start = (s32[3]{0:T(128)S(1)}, s32[3]{0:T(128)S(1)}, u32[]{:S(2)}, u32[]{:S(2)}) collective-permute-start(s32[3]{0:T(128)S(1)} %add_bitcast_fusion.1), channel_id=1, source_target_pairs={{0,4},{4,8},{8,12},{12,16},{16,20},{20,24},{24,28},{28,32},{32,36}... | collective-permute-start | bytes 44 | tf_op jit(solution)/shard_map/ppermute | solution.py:18
  9.8 3.9 multiply_convert_fusion.1
  16.5 3.5 reshape.377
  20.0 5.8 %copy.295 = bf16[2,128,56,64]{1,3,2,0:T(8,128)(2,1)S(1)} copy(bf16[2,128,56,64]{3,2,1,0:T(8,128)(2,1)} %reshape.377) | data formatting | bytes 3670016 | tf_op jit(solution)/shard_map/jvp()/reshape;jvp()/reshape | solution.py:46
  28.3 2.4 copy.299
  30.7 12.7 %all-to-all-start = ((f32[57,64,128]{2,0,1:T(8,128)}), f32[57,64,128]{2,0,1:T(8,128)S(1)}, u32[]{:S(2)}, u32[]{:S(2)}) async-start(f32[57,64,128]{2,0,1:T(8,128)} %copy.299), calls=%async_computation | async-start | bytes 4194304 | tf_op jit(solution)/shard_map/all_to_all | solution.py:204
  43.7 5.7 %fusion.49 = f32[2,128,56,64]{1,3,2,0:T(8,128)} fusion(bf16[2,128,56,64]{1,3,2,0:T(8,128)(2,1)} %copy-done.8, f32[2,56,128]{2,1,0:T(8,128)S(1)} %copy.302, f32[2,56,128]{2,1,0:T(8,128)S(1)} %copy.300, f32[2,128,128]{2,1,0:T(8,128)S(1)} %fusion.148, pred[128,128]{1,0:T(8,128)(4,1)S(1)} %iota_compare_fusion.3), kind=kOutput, calls=%fused_computation.77 | convolution fusion | flops 245891072 | bytes 5767168 | tf_op jit(solution)/shard_map/jvp(chts,cshp->cthp)/dot_general | solution.py:86
  49.5 45.1 %all-to-all-done = f32[57,64,128]{2,0,1:T(8,128)S(1)} async-done(((f32[57,64,128]{2,0,1:T(8,128)}), f32[57,64,128]{2,0,1:T(8,128)S(1)}, u32[]{:S(2)}, u32[]{:S(2)}) %all-to-all-start) | async-done | bytes 1867808 | tf_op jit(solution)/shard_map/all_to_all | solution.py:204
  94.6 2.3 copy.306
  96.9 2.6 copy.305
  101.2 3.8 fusion.55
  105.0 2.3 copy.307
  107.3 6.6 %all-to-all-start.1 = ((f32[56,64,128]{2,0,1:T(8,128)}), f32[56,64,128]{2,0,1:T(8,128)}, u32[]{:S(2)}, u32[]{:S(2)}) async-start(f32[56,64,128]{2,0,1:T(8,128)} %copy.307), calls=%async_computation.1 | async-start | bytes 3670016 | tf_op jit(solution)/shard_map/all_to_all | solution.py:136
  114.1 2.9 slice_add_fusion
  117.0 42.1 %all-to-all-done.1 = f32[56,64,128]{2,0,1:T(8,128)} async-done(((f32[56,64,128]{2,0,1:T(8,128)}), f32[56,64,128]{2,0,1:T(8,128)}, u32[]{:S(2)}, u32[]{:S(2)}) %all-to-all-start.1) | async-done | bytes 1835040 | tf_op jit(solution)/shard_map/all_to_all | solution.py:136
  161.2 5.5 %fusion.27 = (f32[2,128,56,64]{1,3,2,0:T(8,128)}, f32[2,128,56,64]{1,3,2,0:T(8,128)}) fusion(bf16[2,128,56,64]{1,3,2,0:T(8,128)(2,1)} %copy-done.8, f32[2,128,56,64]{1,3,2,0:T(8,128)} %fusion.49, f32[56]{0:T(128)S(1)} %copy-done.19, f32[2,128,56]{1,2,0:T(8,128)S(1)} %copy.304, bf16[2,128,128,1]{2,1,3,0:T(8,128)(2,1)S(1)} %bitcast.153, ...), kind=kOutput, calls=%fused_computation.47 | convolution fusion | flops 242221056 | bytes 16638624 | tf_op jit(solution)/shard_map/jvp(ctn,chpn->cthp)/dot_general | solution.py:108
  166.7 8.9 %copy.355 = f32[2,128,56,64]{3,2,1,0:T(8,128)} copy(f32[2,128,56,64]{1,3,2,0:T(8,128)} %get-tuple-element.90) | data formatting | bytes 7340032 | tf_op jit(solution)/shard_map/jvp()/reshape | solution.py:112
  175.6 6.9 %reshape.378 = f32[256,3584]{1,0:T(8,128)} reshape(f32[2,128,56,64]{3,2,1,0:T(8,128)} %copy.355) | data formatting | bytes 7340032 | tf_op jit(solution)/shard_map/jvp()/reshape | solution.py:112
  182.5 3.5 multiply_reduce_fusion.8
  189.1 3.9 multiply_reduce_fusion.4
  193.0 5.1 %copy.311 = f32[256,3584]{0,1:T(8,128)} copy(f32[256,3584]{1,0:T(8,128)} %get-tuple-element.57) | data formatting | bytes 7340032 | tf_op jit(solution)/shard_map/transpose(jvp())/mul | solution.py:112
  198.2 5.4 %reshape.345 = f32[2,128,56,64]{1,0,3,2:T(2,128)} reshape(f32[256,3584]{0,1:T(8,128)} %copy.311) | data formatting | bytes 7340032 | tf_op jit(solution)/shard_map/transpose(jvp())/reshape | solution.py:112
  203.5 4.6 %multiply_reduce_fusion.5 = (f32[2,56]{1,0:T(2,128)S(1)}, f32[56,64,128]{2,1,0:T(8,128)S(1)}, bf16[2,56,64,128]{3,2,1,0:T(8,128)(2,1)}) fusion(f32[56,64,128]{2,1,0:T(8,128)S(1)} %copy.308, f32[2,56]{1,0:T(2,128)S(1)} %subtract_exponential_fusion.1, bf16[2,128,128,1]{2,1,3,0:T(8,128)(2,1)S(1)} %bitcast.154, f32[2,128,56,64]{1,0,3,2:T(2,128)} %reshape.345, ...), kind=kOutput, calls=%fused_computation.54 | convolution fusion | flops 240844688 | bytes 9298816 | tf_op jit(solution)/shard_map/transpose(jvp(ctn,chpn->cthp))/dot_general | solution.py:108
  208.1 2.3 copy.313
  210.4 6.4 %all-to-all-start.2 = ((f32[56,64,128]{2,0,1:T(8,128)}), f32[56,64,128]{2,0,1:T(8,128)}, u32[]{:S(2)}, u32[]{:S(2)}) async-start(f32[56,64,128]{2,0,1:T(8,128)} %copy.313), calls=%async_computation.2 | async-start | bytes 3670016 | tf_op jit(solution)/shard_map/all_to_all | solution.py:224
  216.9 9.2 %fusion.10 = (f32[2,56,128]{2,1,0:T(8,128)S(1)}, f32[2,56,128]{2,1,0:T(8,128)S(1)}, f32[2,56,128]{2,1,0:T(8,128)S(1)}, bf16[2,128,128]{2,1,0:T(8,128)(2,1)S(1)}) fusion(f32[2,56,128]{2,1,0:T(8,128)S(1)} %copy.302, f32[2,56,128]{2,1,0:T(8,128)S(1)} %copy.300, f32[2,128,128]{2,1,0:T(8,128)S(1)} %fusion.148, pred[128,128]{1,0:T(8,128)(4,1)S(1)} %iota_compare_fusion.3, ...), kind=kOutput, calls=%fused_computation.15 | convolution fusion | flops 264165376 | bytes 6004736 | tf_op jit(solution)/shard_map/transpose(jvp(chts,cshp->cthp))/dot_general | solution.py:86
  226.2 2.2 reduce_window_sum.75
  228.6 4.5 %convert_bitcast_fusion = bf16[2,56,8,8,128]{4,3,2,1,0:T(8,128)(2,1)S(1)} fusion(f32[2,56,128]{2,1,0:T(8,128)S(1)} %copy.302, f32[2,56,128]{2,1,0:T(8,128)S(1)} %copy.300, f32[2,128,128]{2,1,0:T(8,128)S(1)} %fusion.148, pred[128,128]{1,0:T(8,128)(4,1)S(1)} %iota_compare_fusion.3, f32[2,56,64,128]{3,0,2,1:T(2,128)} %bitcast.147), kind=kOutput, calls=%fused_computation.104 | convolution fusion | flops 245891072 | bytes 5767168 | tf_op jit(solution)/shard_map/transpose(jvp(chts,cshp->cthp))/dot_general | solution.py:86
  235.0 27.1 %all-to-all-done.2 = f32[56,64,128]{2,0,1:T(8,128)} async-done(((f32[56,64,128]{2,0,1:T(8,128)}), f32[56,64,128]{2,0,1:T(8,128)}, u32[]{:S(2)}, u32[]{:S(2)}) %all-to-all-start.2) | async-done | bytes 1835040 | tf_op jit(solution)/shard_map/all_to_all | solution.py:224
  262.1 3.9 fusion.58
  266.0 2.3 copy.323
  268.3 6.5 %all-to-all-start.3 = ((f32[56,64,128]{2,0,1:T(8,128)}), f32[56,64,128]{2,0,1:T(8,128)}, u32[]{:S(2)}, u32[]{:S(2)}) async-start(f32[56,64,128]{2,0,1:T(8,128)} %copy.323), calls=%async_computation.3 | async-start | bytes 3670016 | tf_op jit(solution)/shard_map/all_to_all | solution.py:143
  274.8 6.4 %fusion.31 = f32[16,3584]{1,0:T(8,128)S(1)} fusion(f32[256,3584]{1,0:T(8,128)} %copy-done.16, f32[256,3584]{1,0:T(8,128)} %reshape.378, f32[256,3584]{1,0:T(8,128)} %copy-done.12, bf16[1,256,3584]{2,1,0:T(8,128)(2,1)} %param.21, f32[256]{0:T(256)S(1)} %multiply_multiply_fusion.1, f32[3584]{0:T(1024)S(1)} %copy-done.17, f32[256]{0:T(256)S(1)} %fusion.124, ...), kind=kOutput, calls=%fused_computation.51 | convolution fusion | flops 190840832 | bytes 13125632 | tf_op jit(solution)/shard_map/dot_general | solution.py:246
  282.1 3.9 multiply_reduce_fusion.6
  286.1 3.9 convert_element_type.91
  291.4 28.5 %all-to-all-done.3 = f32[56,64,128]{2,0,1:T(8,128)} async-done(((f32[56,64,128]{2,0,1:T(8,128)}), f32[56,64,128]{2,0,1:T(8,128)}, u32[]{:S(2)}, u32[]{:S(2)}) %all-to-all-start.3) | async-done | bytes 1835040 | tf_op jit(solution)/shard_map/all_to_all | solution.py:143
  320.0 3.4 fusion.111
  326.6 3.0 multiply_reduce_fusion.11
  329.6 3.2 multiply_reduce_fusion.10
  332.9 4.5 %fusion.52 = bf16[256,56,64]{0,2,1:T(8,128)(2,1)} fusion(bf16[256,56,64]{0,2,1:T(8,128)(2,1)S(1)} %bitcast.149, f32[256,56,64]{0,2,1:T(8,128)} %bitcast.148, bf16[2,56,8,8,128]{4,3,2,1,0:T(8,128)(2,1)} %get-tuple-element.77, f32[56]{0:T(128)S(1)} %copy-done.19), kind=kLoop, calls=%fused_computation.85 | loop fusion | flops 3670016 | bytes 9175264 | tf_op jit(solution)/shard_map/add | solution.py:235
  337.4 2.8 copy.328
  340.2 10.8 %multiply_reduce_fusion.3 = (f32[3840]{0:T(1024)S(1)}, f32[3840]{0:T(1024)S(1)}, f32[3840]{0:T(1024)S(1)}, f32[3840]{0:T(1024)S(1)}, f32[3840]{0:T(1024)S(1)}, /*index=5*/f32[256,3840]{1,0:T(8,128)}) fusion(f32[259,3840]{1,0:T(8,128)} %copy-done.2, f32[256,3840]{1,0:T(8,128)} %get-tuple-element.68, bf16[256,3584]{1,0:T(8,128)(2,1)S(1)} %copy.328, ...), kind=kLoop, calls=%fused_computation.39 | loop fusion | flops 22590720 | bytes 25635840 | tf_op jit(solution)/shard_map/transpose(jvp())/reduce_sum | solution.py:31
  351.4 2.2 reduce_window_sum.79
  356.7 3.3 broadcast_multiply_fusion
  360.0 2.7 fusion.13
  362.7 3.9 concatenate.25
  367.7 32.5 %all_to_all.36 = f32[256,1,557]{2,1,0:T(1,128)S(1)} all-to-all(f32[256,1,557]{2,1,0:T(1,128)S(1)} %all_to_all.29), channel_id=1, replica_groups=mesh['seq'=64,'batch'=4] {'seq','batch'}, dimensions={0} | all-to-all | bytes 1140736 | tf_op jit(solution)/shard_map/all_to_all | solution.py:153
  401.0 29.6 %all_to_all.37 = f32[256,1,557]{2,1,0:T(1,128)S(1)} all-to-all(f32[256,1,557]{2,1,0:T(1,128)S(1)} %broadcast_in_dim.128), channel_id=1, replica_groups=mesh['seq'=64,'batch'=4] {'seq','batch'}, dimensions={0} | all-to-all | bytes 1140736 | tf_op jit(solution)/shard_map/all_to_all | solution.py:156
  (153 shorter events, 36.4 us)
Async XLA Ops:
  0.6 8.4 %copy-start = (bf16[16,3840]{1,0:T(8,128)(2,1)S(1)}, bf16[16,3840]{1,0:T(8,128)(2,1)}, u32[]{:S(2)}) copy-start(bf16[16,3840]{1,0:T(8,128)(2,1)} %param.13) | copy-start | bytes 368644
  1.4 6.7 %collective-permute-start = (s32[3]{0:T(128)S(1)}, s32[3]{0:T(128)S(1)}, u32[]{:S(2)}, u32[]{:S(2)}) collective-permute-start(s32[3]{0:T(128)S(1)} %add_bitcast_fusion.1), channel_id=1, source_target_pairs={{0,4},{4,8},{8,12},{12,16},{16,20},{20,24},{24,28},{28,32},{32,36}... | collective-permute-start | bytes 44 | tf_op jit(solution)/shard_map/ppermute | solution.py:18
  7.0 8.1 %copy-start.23 = (f32[56]{0:T(128)}, f32[56]{0:T(128)S(1)}, u32[]{:S(2)}) copy-start(f32[56]{0:T(128)S(1)} %exponential_negate_fusion) | copy-start | bytes 676
  9.1 0.8 copy-start.18
  9.8 3.9 copy-start.2
  13.7 1.3 copy-start.6
  13.7 1.4 copy-start.21
  25.8 1.2 copy-start.8
  26.5 1.8 copy-start.4
  30.7 63.9 %all-to-all-start = ((f32[57,64,128]{2,0,1:T(8,128)}), f32[57,64,128]{2,0,1:T(8,128)S(1)}, u32[]{:S(2)}, u32[]{:S(2)}) async-start(f32[57,64,128]{2,0,1:T(8,128)} %copy.299), calls=%async_computation | async-start | bytes 4194304 | tf_op jit(solution)/shard_map/all_to_all | solution.py:204
  107.3 51.8 %all-to-all-start.1 = ((f32[56,64,128]{2,0,1:T(8,128)}), f32[56,64,128]{2,0,1:T(8,128)}, u32[]{:S(2)}, u32[]{:S(2)}) async-start(f32[56,64,128]{2,0,1:T(8,128)} %copy.307), calls=%async_computation.1 | async-start | bytes 3670016 | tf_op jit(solution)/shard_map/all_to_all | solution.py:136
  114.1 47.1 %copy-start.19 = (f32[56]{0:T(128)S(1)}, f32[56]{0:T(128)}, u32[]{:S(2)}) copy-start(f32[56]{0:T(128)} %param.19) | copy-start | bytes 676
  159.1 2.1 copy-start.10
  175.6 6.9 %copy-start.20 = (bf16[16,3584]{1,0:T(8,128)(2,1)S(1)}, bf16[16,3584]{1,0:T(8,128)(2,1)}, u32[]{:S(2)}) copy-start(bf16[16,3584]{1,0:T(8,128)(2,1)} %param.14) | copy-start | bytes 344068
  182.5 3.6 copy-start.14
  182.5 3.6 copy-start.17
  186.0 7.0 %copy-start.12 = (f32[256,3584]{1,0:T(8,128)}, f32[256,3584]{1,0:T(8,128)S(1)}, u32[]{:S(2)}) copy-start(f32[256,3584]{1,0:T(8,128)S(1)} %get-tuple-element.64) | copy-start | bytes 11010052
  186.1 7.0 %copy-start.16 = (f32[256,3584]{1,0:T(8,128)}, f32[256,3584]{1,0:T(8,128)S(1)}, u32[]{:S(2)}) copy-start(f32[256,3584]{1,0:T(8,128)S(1)} %get-tuple-element.92) | copy-start | bytes 11010052
  186.1 3.0 copy-start.7
  210.4 51.7 %all-to-all-start.2 = ((f32[56,64,128]{2,0,1:T(8,128)}), f32[56,64,128]{2,0,1:T(8,128)}, u32[]{:S(2)}, u32[]{:S(2)}) async-start(f32[56,64,128]{2,0,1:T(8,128)} %copy.313), calls=%async_computation.2 | async-start | bytes 3670016 | tf_op jit(solution)/shard_map/all_to_all | solution.py:224
  268.3 51.7 %all-to-all-start.3 = ((f32[56,64,128]{2,0,1:T(8,128)}), f32[56,64,128]{2,0,1:T(8,128)}, u32[]{:S(2)}, u32[]{:S(2)}) async-start(f32[56,64,128]{2,0,1:T(8,128)} %copy.323), calls=%async_computation.3 | async-start | bytes 3670016 | tf_op jit(solution)/shard_map/all_to_all | solution.py:143
  286.1 3.9 copy-start.3
  286.1 3.9 copy-start.11
  291.4 32.0 %copy-start.9 = (bf16[2,128,56,64]{1,3,2,0:T(8,128)(2,1)S(1)}, bf16[2,128,56,64]{1,3,2,0:T(8,128)(2,1)}, u32[]{:S(2)}) copy-start(bf16[2,128,56,64]{1,3,2,0:T(8,128)(2,1)} %copy-done.8) | copy-start | bytes 5505028
  324.4 5.2 %copy-start.5 = (f32[2,56,64,128]{3,2,1,0:T(8,128)S(1)}, f32[2,56,64,128]{3,2,1,0:T(8,128)}, u32[]{:S(2)}) copy-start(f32[2,56,64,128]{3,2,1,0:T(8,128)} %copy-done.4) | copy-start | bytes 11010052
  324.4 5.2 %copy-start.13 = (f32[2,56,64,128]{3,2,1,0:T(8,128)S(1)}, f32[2,56,64,128]{3,2,1,0:T(8,128)}, u32[]{:S(2)}) copy-start(f32[2,56,64,128]{3,2,1,0:T(8,128)} %convert_element_type.91) | copy-start | bytes 11010052
  329.6 3.4 copy-start.15
  340.2 16.2 %copy-start.24 = (f32[56]{0:T(128)S(1)}, f32[56]{0:T(128)}, u32[]{:S(2)}) copy-start(f32[56]{0:T(128)} %copy-done.23) | copy-start | bytes 676
  351.0 5.7 %copy-start.22 = (f32[56]{0:T(128)S(1)}, f32[56]{0:T(128)}, u32[]{:S(2)}) copy-start(f32[56]{0:T(128)} %param.16) | copy-start | bytes 676
  367.7 69.8 %copy-start.1 = (bf16[16,3840]{1,0:T(8,128)(2,1)S(1)}, bf16[16,3840]{1,0:T(8,128)(2,1)}, u32[]{:S(2)}) copy-start(bf16[16,3840]{1,0:T(8,128)(2,1)} %param.13) | copy-start | bytes 368644
where the time goes:
time: 445 us; the launch traced here: 438 us
  waiting for transfers between devices  143 us (32%)
  local copies, waits for them, and re-layouts  75.4 us (17%)
  blocking collectives  62.1 us (14%)
  other arithmetic  61.8 us (14%)
  matrix products  56.7 us (13%)
  starting transfers between devices  37.2 us (8%)
    all_to_all x1, waiting for transfers between devices, local(): lax.all_to_all(outgoing, 'seq', split_axis=1, concat_axis=1, tiled=True)  45.1 us
    all_to_all x1, waiting for transfers between devices, settle_forward(): lax.all_to_all(settled, 'seq', split_axis=1, concat_axis=1, tiled=True)  42.1 us
    all_to_all x1, blocking collectives, spread_sum(): lax.all_to_all(padded, axes, split_axis=0, concat_axis=0, tiled=True)  32.5 us
    all_to_all x1, blocking collectives, spread_sum(): lax.all_to_all(spread, axes, split_axis=0, concat_axis=0, tiled=True)  29.6 us
    all_to_all x1, waiting for transfers between devices, settle_backward(): lax.all_to_all(settled, 'seq', split_axis=1, concat_axis=1, tiled=True)  28.5 us
    all_to_all x1, waiting for transfers between devices, local(): lax.all_to_all(back_flat.reshape(heads, parts, span), 'seq', split_axis=1...  27.1 us
    reshape x3, local copies, waits for them, and re-layouts, mixer_output(): gated = mixed.reshape(tokens, heads * head) * jax.nn.silu(gate_rows)  21.2 us
    dot_general x3, matrix products, intra(): jnp.einsum('chts,cshp->cthp', mixing, blocked, preferred_element_type=jnp...  19.5 us
  transfers between devices with their start and end apart: 5, of which 4 were waited for; matrix products, arithmetic and copies ran while one was open for 10% of the time, Pallas kernels for 0%

commit v1 on v0

--- a/solution.py
+++ b/solution.py
@@ -109,9 +109,9 @@
         "ctn,chpn->cthp", reads, states.astype(jnp.bfloat16), preferred_element_type=jnp.float32
     )
     mixed = within + across + skip_gain[None, None, :, None] * blocked
-    gated = mixed.reshape(tokens, heads * head) * jax.nn.silu(gate_rows)
-    scale = lax.rsqrt(jnp.mean(gated * gated, axis=1, keepdims=True) + EPS)
-    return (gated * scale * norm_gain[None, :]).astype(jnp.bfloat16)
+    gated = mixed * jax.nn.silu(gate_rows)
+    scale = lax.rsqrt(jnp.mean(gated * gated, axis=(2, 3), keepdims=True) + EPS)
+    return (gated * scale * norm_gain.reshape(heads, head)[None, None]).astype(jnp.bfloat16)
 
 
 def carry_weights(logs, backward):
@@ -202,7 +202,13 @@
     outgoing = jnp.concatenate([flat.reshape(heads, parts, span), total_row], axis=0)
     within, pull_intra = jax.vjp(intra, values, write_keys, read_keys, steps, log_decay)
     incoming = lax.all_to_all(outgoing, "seq", split_axis=1, concat_axis=1, tiled=True)
-    incoming, within = lax.optimization_barrier((incoming, within))
+    count = tokens // BLOCK
+    head = inner // heads
+    gate_view = gate_rows.reshape(count, BLOCK, heads, head)
+    cot_view = cotangent[0].reshape(count, BLOCK, heads, head)
+    incoming, within, gate_view, cot_view = lax.optimization_barrier(
+        (incoming, within, gate_view, cot_view)
+    )
     totals = jnp.transpose(incoming[heads, :, :heads])[:, :, None]
     carried = settle_forward((incoming[:heads], totals))
     layer_out, pull_out = jax.vjp(
@@ -213,13 +219,14 @@
         entering,
         carried,
         within,
-        gate_rows,
+        gate_view,
         skip_gain,
         norm_gain,
     )
     d_values, d_read, d_log, d_entering, d_carried, d_within, d_gate, d_skip, d_norm = pull_out(
-        cotangent[0]
-    )
+        cot_view
+    )
+    d_gate = d_gate.reshape(tokens, inner)
     back_flat = d_carried.reshape(heads, -1)
     back_incoming = lax.all_to_all(
         back_flat.reshape(heads, parts, span), "seq", split_axis=1, concat_axis=1, tiled=True
@@ -258,7 +265,7 @@
     for part in parts_list:
         sums.append(packed[offset : offset + part.size].reshape(part.shape))
         offset += part.size
-    return (layer_out[None], sums[0], sums[1], sums[2], sums[3], sums[4], sums[5], sums[6], sums[7])
+    return (layer_out.reshape(1, tokens, inner), sums[0], sums[1], sums[2], sums[3], sums[4], sums[5], sums[6], sums[7])
 
 
 def solution(mesh):

time: 445 us -> 418 us (0.939)
  blocking collectives: 62.1 us -> 32.5 us
  local copies, waits for them, and re-layouts: 75.4 us -> 86.5 us
  other arithmetic: 61.8 us -> 53.7 us
  matrix products: 56.7 us -> 50.5 us
  starting transfers between devices: 37.2 us -> 42.8 us
    all_to_all x1 -> x0, blocking collectives: 29.6 us -> none  [spread_sum(): lax.all_to_all(spread, axes, split_axis=0, concat_axis=0, tiled=True)]
    unnamed x52 -> x55, local copies, waits for them, and re-layouts: 4.28 us -> 21.3 us
    reshape x3 -> x2, local copies, waits for them, and re-layouts: 21.2 us -> 5.48 us  [the longest x1 5.4 us: local(): gate_view = gate_rows.reshape(count, BLOCK, heads, head)]
    all_to_all x1, waiting for transfers between devices: 45.1 us -> 30 us  [local(): lax.all_to_all(outgoing, 'seq', split_axis=1, concat_axis=1, tiled=True)]
    all_to_all x0 -> x1, waiting for transfers between devices: none -> 11.7 us  [spread_sum(): lax.all_to_all(spread, axes, split_axis=0, concat_axis=0, tiled=True)]
    reduce_sum x4 -> x1, other arithmetic: 9.54 us -> 1.77 us  [mixer_output(): gated * scale * norm_gain.reshape(heads, head)[None, None]]
    all_to_all x0 -> x1, starting transfers between devices: none -> 5.7 us  [spread_sum(): lax.all_to_all(spread, axes, split_axis=0, concat_axis=0, tiled=True)]
    unnamed x0 -> x1, other arithmetic: none -> 5.49 us
  transfers between devices with their start and end apart: 5 -> 6, of which waited for: 4 -> 5; matrix products, arithmetic and copies ran while one was open for 10% -> 17% of each run, Pallas kernels for 0% -> 0%
where the time goes in v1:
time: 418 us; the launch traced here: 410 us
  waiting for transfers between devices  143 us (34%)
  local copies, waits for them, and re-layouts  86.5 us (21%)
  other arithmetic  53.7 us (13%)
  matrix products  50.5 us (12%)
  starting transfers between devices  42.8 us (10%)
  blocking collectives  32.5 us (8%)
    all_to_all x1, waiting for transfers between devices, settle_forward(): lax.all_to_all(settled, 'seq', split_axis=1, concat_axis=1, tiled=True)  42.1 us
    all_to_all x1, blocking collectives, spread_sum(): lax.all_to_all(padded, axes, split_axis=0, concat_axis=0, tiled=True)  32.5 us
    all_to_all x1, waiting for transfers between devices, settle_backward(): lax.all_to_all(settled, 'seq', split_axis=1, concat_axis=1, tiled=True)  31.2 us
    all_to_all x1, waiting for transfers between devices, local(): lax.all_to_all(outgoing, 'seq', split_axis=1, concat_axis=1, tiled=True)  30 us
    all_to_all x1, waiting for transfers between devices, local(): lax.all_to_all(back_flat.reshape(heads, parts, span), 'seq', split_axis=1...  27.8 us
    unnamed x55, local copies, waits for them, and re-layouts  21.3 us
    dot_general x3, matrix products, intra(): jnp.einsum('chts,cshp->cthp', mixing, blocked, preferred_element_type=jnp...  17.4 us
    all_to_all x1, starting transfers between devices, local(): lax.all_to_all(outgoing, 'seq', split_axis=1, concat_axis=1, tiled=True)  12.9 us
  transfers between devices with their start and end apart: 6, of which 5 were waited for; matrix products, arithmetic and copies ran while one was open for 17% of the time, Pallas kernels for 0%

profile of v1, /device:TPU:1, one launch (start us, length us, event | category | flops | bytes accessed | tf_op | source)
XLA Modules:
  0.0 410.5 jit_solution(13858696267668599020)
XLA Ops:
  1.4 4.9 %collective-permute-start = (s32[3]{0:T(128)S(1)}, s32[3]{0:T(128)S(1)}, u32[]{:S(2)}, u32[]{:S(2)}) collective-permute-start(s32[3]{0:T(128)S(1)} %add_bitcast_fusion.1), channel_id=1, source_target_pairs={{0,4},{4,8},{8,12},{12,16},{16,20},{20,24},{24,28},{28,32},{32,36}... | collective-permute-start | bytes 44 | tf_op jit(solution)/shard_map/ppermute | solution.py:18
  9.8 3.8 multiply_convert_fusion.1
  15.7 3.6 reshape.383
  19.3 5.8 %copy.241 = bf16[2,128,56,64]{1,3,2,0:T(8,128)(2,1)S(1)} copy(bf16[2,128,56,64]{3,2,1,0:T(8,128)(2,1)} %reshape.383) | data formatting | bytes 3670016 | tf_op jit(solution)/shard_map/jvp()/reshape;jvp()/reshape | solution.py:46
  27.7 2.5 copy.245
  30.2 12.9 %all-to-all-start = ((f32[57,64,128]{2,0,1:T(8,128)}), f32[57,64,128]{2,0,1:T(8,128)}, u32[]{:S(2)}, u32[]{:S(2)}) async-start(f32[57,64,128]{2,0,1:T(8,128)} %copy.245), calls=%async_computation | async-start | bytes 4194304 | tf_op jit(solution)/shard_map/all_to_all | solution.py:204
  43.1 3.8 copy.251
  46.9 4.6 %reshape_squeeze.3 = bf16[2,128,56,64]{1,0,3,2:T(2,128)(2,1)} reshape(bf16[1,256,3584]{1,2,0:T(8,128)(2,1)} %copy.251) | data formatting | bytes 3670016 | tf_op jit(solution)/shard_map/reshape;squeeze | solution.py:208
  51.6 2.5 fusion.119
  54.2 5.4 %reshape.348 = f32[2,128,56,64]{1,0,3,2:T(2,128)} reshape(f32[256,3584]{0,1:T(8,128)} %fusion.119) | data formatting | bytes 7340032 | tf_op jit(solution)/shard_map/reshape | solution.py:207
  59.8 4.4 %fusion.50 = f32[2,128,56,64]{1,3,2,0:T(8,128)} fusion(bf16[2,128,56,64]{1,3,2,0:T(8,128)(2,1)S(1)} %copy.241, f32[2,56,128]{2,1,0:T(8,128)S(1)} %copy.248, f32[2,56,128]{2,1,0:T(8,128)S(1)} %copy.246, f32[2,128,128]{2,1,0:T(8,128)S(1)} %fusion.158, pred[128,128]{1,0:T(8,128)(4,1)S(1)} %iota_compare_fusion.3), kind=kOutput, calls=%fused_computation.78 | convolution fusion | flops 245891072 | bytes 5767168 | tf_op jit(solution)/shard_map/jvp(chts,cshp->cthp)/dot_general | solution.py:86
  64.1 30.0 %all-to-all-done = f32[57,64,128]{2,0,1:T(8,128)} async-done(((f32[57,64,128]{2,0,1:T(8,128)}), f32[57,64,128]{2,0,1:T(8,128)}, u32[]{:S(2)}, u32[]{:S(2)}) %all-to-all-start) | async-done | bytes 1867808 | tf_op jit(solution)/shard_map/all_to_all | solution.py:204
  94.1 4.0 copy.254
  98.1 3.7 copy.253
  103.5 3.8 fusion.54
  107.3 2.3 copy.255
  109.6 6.4 %all-to-all-start.1 = ((f32[56,64,128]{2,0,1:T(8,128)}), f32[56,64,128]{2,0,1:T(8,128)}, u32[]{:S(2)}, u32[]{:S(2)}) async-start(f32[56,64,128]{2,0,1:T(8,128)} %copy.255), calls=%async_computation.1 | async-start | bytes 3670016 | tf_op jit(solution)/shard_map/all_to_all | solution.py:136
  116.2 2.9 slice_add_fusion
  119.1 42.1 %all-to-all-done.1 = f32[56,64,128]{2,0,1:T(8,128)} async-done(((f32[56,64,128]{2,0,1:T(8,128)}), f32[56,64,128]{2,0,1:T(8,128)}, u32[]{:S(2)}, u32[]{:S(2)}) %all-to-all-start.1) | async-done | bytes 1835040 | tf_op jit(solution)/shard_map/all_to_all | solution.py:136
  163.7 5.0 %multiply_reduce_fusion.7 = (f32[2,128]{1,0:T(2,128)S(1)}, f32[2,128,56,64]{1,3,2,0:T(8,128)S(1)}, f32[2,128,56,64]{1,3,2,0:T(8,128)S(1)}) fusion(f32[2,128,56,64]{1,0,3,2:T(2,128)S(1)} %copy-done.13, bf16[2,128,56,64]{1,3,2,0:T(8,128)(2,1)S(1)} %copy.241, f32[56]{0:T(128)S(1)} %copy-done.22, f32[2,128,56,64]{1,3,2,0:T(8,128)} %fusion.50, ...), kind=kOutput, calls=%fused_computation.66 | convolution fusion | flops 248643328 | bytes 20309664 | tf_op jit(solution)/shard_map/jvp(ctn,chpn->cthp)/dot_general | solution.py:108
  172.1 5.5 %fusion.51 = (bf16[2,56,8,8,128]{4,3,2,1,0:T(8,128)(2,1)}, f32[2,128,56,64]{1,3,2,0:T(8,128)S(1)}, f32[2,128,56,64]{1,3,2,0:T(8,128)}, bf16[2,128,56,64]{1,3,2,0:T(8,128)(2,1)}) fusion(f32[56]{0:T(128)S(1)} %copy-done.22, f32[2,128,56,64]{1,0,3,2:T(2,128)S(1)} %copy-done.13, f32[2,128,56,64]{1,3,2,0:T(8,128)S(1)} %get-tuple-element.116, ...), kind=kLoop, calls=%fused_computation.84 | loop fusion | flops 25690112 | bytes 29434080
  177.6 2.5 multiply_reduce_fusion.4
  180.2 2.3 copy.261
  182.5 6.8 %all-to-all-start.2 = ((f32[56,64,128]{2,0,1:T(8,128)}), f32[56,64,128]{2,0,1:T(8,128)}, u32[]{:S(2)}, u32[]{:S(2)}) async-start(f32[56,64,128]{2,0,1:T(8,128)} %copy.261), calls=%async_computation.2 | async-start | bytes 3670016 | tf_op jit(solution)/shard_map/all_to_all | solution.py:231
  189.2 8.5 %fusion.10 = (f32[2,56,128]{2,1,0:T(8,128)S(1)}, f32[2,56,128]{2,1,0:T(8,128)S(1)}, f32[2,56,128]{2,1,0:T(8,128)S(1)}, bf16[2,128,128]{2,1,0:T(8,128)(2,1)S(1)}) fusion(f32[2,56,128]{2,1,0:T(8,128)S(1)} %copy.248, f32[2,56,128]{2,1,0:T(8,128)S(1)} %copy.246, f32[2,128,128]{2,1,0:T(8,128)S(1)} %fusion.158, pred[128,128]{1,0:T(8,128)(4,1)S(1)} %iota_compare_fusion.3, ...), kind=kOutput, calls=%fused_computation.19 | convolution fusion | flops 264165376 | bytes 6004736 | tf_op jit(solution)/shard_map/transpose(jvp(chts,cshp->cthp))/dot_general | solution.py:86
  197.9 2.2 reduce_window_sum.75
  200.2 4.5 %convert_bitcast_fusion = bf16[2,56,8,8,128]{4,3,2,1,0:T(8,128)(2,1)S(1)} fusion(f32[2,56,128]{2,1,0:T(8,128)S(1)} %copy.248, f32[2,56,128]{2,1,0:T(8,128)S(1)} %copy.246, f32[2,128,128]{2,1,0:T(8,128)S(1)} %fusion.158, pred[128,128]{1,0:T(8,128)(4,1)S(1)} %iota_compare_fusion.3, f32[2,128,56,64]{1,3,2,0:T(8,128)} %copy-done.3), kind=kOutput, calls=%fused_computation.105 | convolution fusion | flops 245891072 | bytes 5767168 | tf_op jit(solution)/shard_map/transpose(jvp(chts,cshp->cthp))/dot_general | solution.py:86
  206.7 27.8 %all-to-all-done.2 = f32[56,64,128]{2,0,1:T(8,128)} async-done(((f32[56,64,128]{2,0,1:T(8,128)}), f32[56,64,128]{2,0,1:T(8,128)}, u32[]{:S(2)}, u32[]{:S(2)}) %all-to-all-start.2) | async-done | bytes 1835040 | tf_op jit(solution)/shard_map/all_to_all | solution.py:231
  234.4 3.9 fusion.57
  238.3 2.3 copy.269
  240.6 6.2 %all-to-all-start.3 = ((f32[56,64,128]{2,0,1:T(8,128)}), f32[56,64,128]{2,0,1:T(8,128)S(1)}, u32[]{:S(2)}, u32[]{:S(2)}) async-start(f32[56,64,128]{2,0,1:T(8,128)} %copy.269), calls=%async_computation.3 | async-start | bytes 3670016 | tf_op jit(solution)/shard_map/all_to_all | solution.py:143
  246.9 4.0 convert_element_type.83
  250.9 3.3 copy.276
  256.7 4.2 %fusion.85 = bf16[2,128,128]{2,1,0:T(8,128)(2,1)S(1)} fusion(f32[2,128,56,64]{1,3,2,0:T(8,128)} %copy-done.3, f32[2,128,56]{1,2,0:T(8,128)S(1)} %copy.252, f32[1,56,64,128]{3,2,1,0:T(8,128)} %slice_add_fusion, f32[56,64,128]{2,1,0:T(8,128)} %copy-done.7, f32[2,56]{1,0:T(2,128)S(1)} %subtract_exponential_fusion.1), kind=kOutput, calls=%fused_computation.120 | convolution fusion | flops 238583808 | bytes 7463360 | tf_op jit(solution)/shard_map/transpose(jvp(ctn,chpn->cthp))/dot_general | solution.py:108
  261.0 31.2 %all-to-all-done.3 = f32[56,64,128]{2,0,1:T(8,128)S(1)} async-done(((f32[56,64,128]{2,0,1:T(8,128)}), f32[56,64,128]{2,0,1:T(8,128)S(1)}, u32[]{:S(2)}, u32[]{:S(2)}) %all-to-all-start.3) | async-done | bytes 1835040 | tf_op jit(solution)/shard_map/all_to_all | solution.py:143
  292.1 2.5 fusion.116
  295.3 3.3 fusion.31
  303.3 3.9 copy.274
  307.2 11.2 %multiply_reduce_fusion.3 = (f32[3840]{0:T(1024)S(1)}, f32[3840]{0:T(1024)S(1)}, f32[3840]{0:T(1024)S(1)}, f32[3840]{0:T(1024)S(1)}, f32[3840]{0:T(1024)S(1)}, /*index=5*/f32[256,3840]{1,0:T(8,128)}) fusion(f32[259,3840]{1,0:T(8,128)} %copy-done.2, f32[256,3840]{1,0:T(8,128)} %get-tuple-element.118, bf16[256,3584]{1,0:T(8,128)(2,1)} %copy.274, ...), kind=kLoop, calls=%fused_computation.40 | loop fusion | flops 22590720 | bytes 25635840 | tf_op jit(solution)/shard_map/transpose(jvp())/reduce_sum | solution.py:31
  320.6 2.2 reduce_window_sum.79
  325.9 3.3 broadcast_multiply_fusion
  329.3 2.7 fusion.13
  332.0 4.1 %concatenate.25 = f32[142576]{0:T(1024)S(1)} concatenate(f32[61440]{0:T(1024)S(1)} %reshape.359, f32[57344]{0:T(1024)} %reshape.361, f32[896]{0:T(1024)S(1)} %reshape.366, f32[56]{0:T(128)S(1)} %negate_multiply_fusion, f32[15360]{0:T(1024)S(1)} %reshape.371, f32[3840]{0:T(1024)S(1)} %get-tuple-element.92, f32[56]{0:T(128)S(1)} %get-tuple-element.97, f32[3584]{0:T(1024)S(1)} %reshape.372), dimensions={0} | concatenate | bytes 1140608 | tf_op jit(solution)/shard_map/concatenate | solution.py:261
  339.0 32.5 %all_to_all.36 = f32[256,1,557]{2,1,0:T(1,128)S(1)} all-to-all(f32[256,1,557]{2,1,0:T(1,128)S(1)} %all_to_all.29), channel_id=1, replica_groups=mesh['seq'=64,'batch'=4] {'seq','batch'}, dimensions={0} | all-to-all | bytes 1140736 | tf_op jit(solution)/shard_map/all_to_all | solution.py:153
  373.2 5.7 %all-to-all-start.5 = ((f32[256,1,557]{2,1,0:T(1,128)}), f32[256,1,557]{2,1,0:T(1,128)S(1)}, u32[]{:S(2)}, u32[]{:S(2)}) async-start(f32[256,1,557]{2,1,0:T(1,128)} %broadcast_in_dim.123), calls=%async_computation.5 | async-start | bytes 1310720 | tf_op jit(solution)/shard_map/all_to_all | solution.py:156
  378.9 6.7 %copy.297 = bf16[2,128,56,64]{3,2,1,0:T(8,128)(2,1)} copy(bf16[2,128,56,64]{1,3,2,0:T(8,128)(2,1)S(1)} %copy-done.17) | data formatting | bytes 3670016
  385.6 5.8 %reshape.382 = bf16[1,256,3584]{2,1,0:T(8,128)(2,1)} reshape(bf16[2,128,56,64]{3,2,1,0:T(8,128)(2,1)} %copy.297) | data formatting | bytes 3670016
  391.4 11.7 %all-to-all-done.5 = f32[256,1,557]{2,1,0:T(1,128)S(1)} async-done(((f32[256,1,557]{2,1,0:T(1,128)}), f32[256,1,557]{2,1,0:T(1,128)S(1)}, u32[]{:S(2)}, u32[]{:S(2)}) %all-to-all-start.5) | async-done | bytes 570400 | tf_op jit(solution)/shard_map/all_to_all | solution.py:156
  (155 shorter events, 43.6 us)
Async XLA Ops:
  0.6 8.4 %copy-start = (bf16[16,3840]{1,0:T(8,128)(2,1)S(1)}, bf16[16,3840]{1,0:T(8,128)(2,1)}, u32[]{:S(2)}) copy-start(bf16[16,3840]{1,0:T(8,128)(2,1)} %param.13) | copy-start | bytes 368644
  1.4 6.7 %collective-permute-start = (s32[3]{0:T(128)S(1)}, s32[3]{0:T(128)S(1)}, u32[]{:S(2)}, u32[]{:S(2)}) collective-permute-start(s32[3]{0:T(128)S(1)} %add_bitcast_fusion.1), channel_id=1, source_target_pairs={{0,4},{4,8},{8,12},{12,16},{16,20},{20,24},{24,28},{28,32},{32,36}... | collective-permute-start | bytes 44 | tf_op jit(solution)/shard_map/ppermute | solution.py:18
  9.1 0.8 copy-start.20
  9.8 3.8 copy-start.2
  13.6 0.7 copy-start.23
  25.1 164.1 %copy-start.8 = (bf16[2,128,56,64]{1,3,2,0:T(8,128)(2,1)}, bf16[2,128,56,64]{1,3,2,0:T(8,128)(2,1)S(1)}, u32[]{:S(2)}) copy-start(bf16[2,128,56,64]{1,3,2,0:T(8,128)(2,1)S(1)} %copy.241) | copy-start | bytes 5505028
  25.8 1.9 copy-start.5
  30.2 63.9 %all-to-all-start = ((f32[57,64,128]{2,0,1:T(8,128)}), f32[57,64,128]{2,0,1:T(8,128)}, u32[]{:S(2)}, u32[]{:S(2)}) async-start(f32[57,64,128]{2,0,1:T(8,128)} %copy.245), calls=%async_computation | async-start | bytes 4194304 | tf_op jit(solution)/shard_map/all_to_all | solution.py:204
  43.1 8.5 %copy-start.19 = (bf16[16,3584]{1,0:T(8,128)(2,1)S(1)}, bf16[16,3584]{1,0:T(8,128)(2,1)}, u32[]{:S(2)}) copy-start(bf16[16,3584]{1,0:T(8,128)(2,1)} %param.14) | copy-start | bytes 344068
  107.2 8.7 %copy-start.21 = (f32[3584]{0:T(1024)S(1)}, f32[3584]{0:T(1024)}, u32[]{:S(2)}) copy-start(f32[3584]{0:T(1024)} %param.20) | copy-start | bytes 43012
  109.6 51.6 %all-to-all-start.1 = ((f32[56,64,128]{2,0,1:T(8,128)}), f32[56,64,128]{2,0,1:T(8,128)}, u32[]{:S(2)}, u32[]{:S(2)}) async-start(f32[56,64,128]{2,0,1:T(8,128)} %copy.255), calls=%async_computation.1 | async-start | bytes 3670016 | tf_op jit(solution)/shard_map/all_to_all | solution.py:136
  116.1 47.0 %copy-start.22 = (f32[56]{0:T(128)S(1)}, f32[56]{0:T(128)}, u32[]{:S(2)}) copy-start(f32[56]{0:T(128)} %param.19) | copy-start | bytes 676
  161.1 2.6 copy-start.13
  163.1 14.5 %copy-start.7 = (f32[56,64,128]{2,1,0:T(8,128)}, f32[56,64,128]{2,1,0:T(8,128)S(1)}, u32[]{:S(2)}) copy-start(f32[56,64,128]{2,1,0:T(8,128)S(1)} %copy.256) | copy-start | bytes 5505028
  163.7 5.1 %copy-start.10 = (bf16[2,128,56,64]{1,0,3,2:T(2,128)(2,1)S(1)}, bf16[2,128,56,64]{1,0,3,2:T(2,128)(2,1)}, u32[]{:S(2)}) copy-start(bf16[2,128,56,64]{1,0,3,2:T(2,128)(2,1)} %reshape_squeeze.3) | copy-start | bytes 5505028
  168.8 8.9 %copy-start.14 = (f32[2,128,56,64]{1,3,2,0:T(8,128)}, f32[2,128,56,64]{1,3,2,0:T(8,128)S(1)}, u32[]{:S(2)}) copy-start(f32[2,128,56,64]{1,3,2,0:T(8,128)S(1)} %get-tuple-element.142) | copy-start | bytes 11010052
  168.8 3.4 copy-start.18
  177.6 2.5 copy-start.3
  182.5 52.0 %all-to-all-start.2 = ((f32[56,64,128]{2,0,1:T(8,128)}), f32[56,64,128]{2,0,1:T(8,128)}, u32[]{:S(2)}, u32[]{:S(2)}) async-start(f32[56,64,128]{2,0,1:T(8,128)} %copy.261), calls=%async_computation.2 | async-start | bytes 3670016 | tf_op jit(solution)/shard_map/all_to_all | solution.py:231
  240.6 51.5 %all-to-all-start.3 = ((f32[56,64,128]{2,0,1:T(8,128)}), f32[56,64,128]{2,0,1:T(8,128)S(1)}, u32[]{:S(2)}, u32[]{:S(2)}) async-start(f32[56,64,128]{2,0,1:T(8,128)} %copy.269), calls=%async_computation.3 | async-start | bytes 3670016 | tf_op jit(solution)/shard_map/all_to_all | solution.py:143
  246.9 4.0 copy-start.12
  292.1 2.6 copy-start.4
  292.1 3.2 copy-start.9
  298.6 3.0 copy-start.15
  298.6 3.0 copy-start.16
  307.2 11.3 %copy-start.6 = (f32[2,56,64,128]{3,2,1,0:T(8,128)S(1)}, f32[2,56,64,128]{3,2,1,0:T(8,128)}, u32[]{:S(2)}) copy-start(f32[2,56,64,128]{3,2,1,0:T(8,128)} %copy-done.5) | copy-start | bytes 11010052
  307.2 11.3 %copy-start.11 = (f32[2,56,64,128]{3,2,1,0:T(8,128)S(1)}, f32[2,56,64,128]{3,2,1,0:T(8,128)}, u32[]{:S(2)}) copy-start(f32[2,56,64,128]{3,2,1,0:T(8,128)} %convert_element_type.83) | copy-start | bytes 11010052
  318.5 7.4 %copy-start.24 = (f32[56]{0:T(128)S(1)}, f32[56]{0:T(128)}, u32[]{:S(2)}) copy-start(f32[56]{0:T(128)} %param.16) | copy-start | bytes 676
  332.0 47.0 %copy-start.17 = (bf16[2,128,56,64]{1,3,2,0:T(8,128)(2,1)S(1)}, bf16[2,128,56,64]{1,3,2,0:T(8,128)(2,1)}, u32[]{:S(2)}) copy-start(bf16[2,128,56,64]{1,3,2,0:T(8,128)(2,1)} %get-tuple-element.126) | copy-start | bytes 5505028
  373.2 29.9 %all-to-all-start.5 = ((f32[256,1,557]{2,1,0:T(1,128)}), f32[256,1,557]{2,1,0:T(1,128)S(1)}, u32[]{:S(2)}, u32[]{:S(2)}) async-start(f32[256,1,557]{2,1,0:T(1,128)} %broadcast_in_dim.123), calls=%async_computation.5 | async-start | bytes 1310720 | tf_op jit(solution)/shard_map/all_to_all | solution.py:156
  385.6 24.4 %copy-start.1 = (bf16[16,3840]{1,0:T(8,128)(2,1)S(1)}, bf16[16,3840]{1,0:T(8,128)(2,1)}, u32[]{:S(2)}) copy-start(bf16[16,3840]{1,0:T(8,128)(2,1)} %param.13) | copy-start | bytes 368644

commit v2 on v1

--- a/solution.py
+++ b/solution.py
@@ -22,13 +22,18 @@
     return (labels[:, None] == jnp.arange(vocab, dtype=jnp.int32)[None, :]).astype(kind)
 
 
-def prepare(raw_rows, step_rows, decay_log, conv_weight, conv_bias, inner, heads):
+def convolve(raw_rows, conv_weight, conv_bias):
     width = conv_weight.shape[0]
     tokens = raw_rows.shape[0] - width + 1
-    state = (raw_rows.shape[1] - inner) // 2
     convolved = conv_bias[None, :] + conv_weight[0][None, :] * raw_rows[0:tokens]
     for offset in range(1, width):
         convolved = convolved + conv_weight[offset][None, :] * raw_rows[offset : offset + tokens]
+    return convolved
+
+
+def prepare(convolved, step_rows, decay_log, inner, heads):
+    tokens = convolved.shape[0]
+    state = (convolved.shape[1] - inner) // 2
     active = jax.nn.silu(convolved)
     values = active[:, :inner].astype(jnp.bfloat16).reshape(tokens, heads, inner // heads)
     write_keys = active[:, inner : inner + state].astype(jnp.bfloat16)
@@ -182,13 +187,12 @@
     raw_rows = jnp.dot(wide_hot, input_table, preferred_element_type=jnp.float32)
     gate_rows = jnp.dot(own_hot, gate_table, preferred_element_type=jnp.float32)
     step_rows = jnp.dot(own_hot.astype(jnp.float32), step_table, precision=HIGH)
+    convolved = convolve(raw_rows, conv_weight, conv_bias)
     features, pull_prepare = jax.vjp(
         partial(prepare, inner=inner, heads=heads),
-        raw_rows,
+        convolved,
         step_rows,
         decay_log,
-        conv_weight,
-        conv_bias,
     )
     values, write_keys, read_keys, steps, log_decay = features
     pieces, pull_groups = jax.vjp(group_states, values, write_keys, steps, log_decay)
@@ -237,7 +241,7 @@
     d_total = jnp.exp(total) * jnp.sum(later * carried, axis=(1, 2))
     d_pieces, d_log_local = pull_local((d_entering, later, d_total))
     d_values_state, d_write_state, d_steps_state, d_log_state = pull_groups(d_pieces)
-    d_raw, d_step_rows, d_decay, d_taps, d_shift = pull_prepare(
+    d_conv, d_step_rows, d_decay = pull_prepare(
         (
             d_values + d_intra[0] + d_values_state,
             d_intra[1] + d_write_state,
@@ -248,8 +252,15 @@
     )
     wide_float = wide_hot.astype(jnp.float32)
     own_float = wide_float[width - 1 :]
+    shifted_hot = jnp.concatenate(
+        [wide_float[offset : offset + tokens].T for offset in range(width)], axis=0
+    )
+    per_tap = jnp.dot(shifted_hot, d_conv, precision=HIGH).reshape(width, vocab, -1)
+    table_grad = jnp.sum(conv_weight[:, None, :] * per_tap, axis=0)
+    d_taps = jnp.sum(input_table.astype(jnp.float32)[None] * per_tap, axis=1)
+    d_shift = jnp.sum(d_conv, axis=0)
     parts_list = (
-        jnp.dot(wide_float.T, d_raw, precision=HIGH),
+        table_grad,
         jnp.dot(own_float.T, d_gate, precision=HIGH),
         jnp.dot(own_float.T, d_step_rows, precision=HIGH),
         d_decay,

time: 418 us -> 412 us (0.986)
  other arithmetic: 53.7 us -> 47.3 us
    reduce_sum x1 -> x2, other arithmetic: 11.2 us -> 3.42 us  [the longest x1 3.32 us: local(): d_shift = jnp.sum(d_conv, axis=0)]
    unnamed x55 -> x81, local copies, waits for them, and re-layouts: 21.3 us -> 21.3 us
  transfers between devices with their start and end apart: 6 -> 6, of which waited for: 5 -> 5; matrix products, arithmetic and copies ran while one was open for 17% -> 18% of each run, Pallas kernels for 0% -> 0%
where the time goes in v2:
time: 412 us; the launch traced here: 404 us
  waiting for transfers between devices  141 us (34%)
  local copies, waits for them, and re-layouts  85.5 us (21%)
  matrix products  53.8 us (13%)
  other arithmetic  47.3 us (11%)
  starting transfers between devices  42.8 us (10%)
  blocking collectives  32.5 us (8%)
    all_to_all x1, waiting for transfers between devices, settle_forward(): lax.all_to_all(settled, 'seq', split_axis=1, concat_axis=1, tiled=True)  42.1 us
    all_to_all x1, blocking collectives, spread_sum(): lax.all_to_all(padded, axes, split_axis=0, concat_axis=0, tiled=True)  32.5 us
    all_to_all x1, waiting for transfers between devices, settle_backward(): lax.all_to_all(settled, 'seq', split_axis=1, concat_axis=1, tiled=True)  30.9 us
    all_to_all x1, waiting for transfers between devices, local(): lax.all_to_all(outgoing, 'seq', split_axis=1, concat_axis=1, tiled=True)  30 us
    all_to_all x1, waiting for transfers between devices, local(): lax.all_to_all(back_flat.reshape(heads, parts, span), 'seq', split_axis=1...  25.9 us
    unnamed x81, local copies, waits for them, and re-layouts  21.3 us
    dot_general x3, matrix products, intra(): jnp.einsum('chts,cshp->cthp', mixing, blocked, preferred_element_type=jnp...  17.4 us
    all_to_all x1, starting transfers between devices, local(): lax.all_to_all(outgoing, 'seq', split_axis=1, concat_axis=1, tiled=True)  12.9 us
  transfers between devices with their start and end apart: 6, of which 5 were waited for; matrix products, arithmetic and copies ran while one was open for 18% of the time, Pallas kernels for 0%

profile of v2, /device:TPU:1, one launch (start us, length us, event | category | flops | bytes accessed | tf_op | source)
XLA Modules:
  0.0 404.4 jit_solution(8753085387050339238)
XLA Ops:
  1.4 4.9 %collective-permute-start = (s32[3]{0:T(128)S(1)}, s32[3]{0:T(128)S(1)}, u32[]{:S(2)}, u32[]{:S(2)}) collective-permute-start(s32[3]{0:T(128)S(1)} %add_bitcast_fusion.1), channel_id=1, source_target_pairs={{0,4},{4,8},{8,12},{12,16},{16,20},{20,24},{24,28},{28,32},{32,36}... | collective-permute-start | bytes 44 | tf_op jit(solution)/shard_map/ppermute | solution.py:18
  10.7 3.8 multiply_convert_fusion.1
  17.0 3.5 reshape.362
  20.5 5.8 %copy.241 = bf16[2,128,56,64]{1,3,2,0:T(8,128)(2,1)S(1)} copy(bf16[2,128,56,64]{3,2,1,0:T(8,128)(2,1)} %reshape.362) | data formatting | bytes 3670016 | tf_op jit(solution)/shard_map/jvp()/reshape;jvp()/reshape | solution.py:51
  29.1 2.4 copy.245
  31.5 12.9 %all-to-all-start = ((f32[57,64,128]{2,0,1:T(8,128)}), f32[57,64,128]{2,0,1:T(8,128)}, u32[]{:S(2)}, u32[]{:S(2)}) async-start(f32[57,64,128]{2,0,1:T(8,128)} %copy.245), calls=%async_computation | async-start | bytes 4194304 | tf_op jit(solution)/shard_map/all_to_all | solution.py:208
  44.4 3.8 copy.251
  48.2 4.6 %reshape_squeeze.3 = bf16[2,128,56,64]{1,0,3,2:T(2,128)(2,1)} reshape(bf16[1,256,3584]{1,2,0:T(8,128)(2,1)} %copy.251) | data formatting | bytes 3670016 | tf_op jit(solution)/shard_map/reshape;squeeze | solution.py:212
  52.9 2.5 fusion.124
  55.4 5.4 %reshape.330 = f32[2,128,56,64]{1,0,3,2:T(2,128)} reshape(f32[256,3584]{0,1:T(8,128)} %fusion.124) | data formatting | bytes 7340032 | tf_op jit(solution)/shard_map/reshape | solution.py:211
  61.0 4.4 %fusion.46 = f32[2,128,56,64]{1,3,2,0:T(8,128)} fusion(bf16[2,128,56,64]{1,3,2,0:T(8,128)(2,1)S(1)} %copy.241, f32[2,56,128]{2,1,0:T(8,128)S(1)} %copy.248, f32[2,56,128]{2,1,0:T(8,128)S(1)} %copy.246, f32[2,128,128]{2,1,0:T(8,128)S(1)} %fusion.165, pred[128,128]{1,0:T(8,128)(4,1)S(1)} %iota_compare_fusion.2), kind=kOutput, calls=%fused_computation.73 | convolution fusion | flops 245891072 | bytes 5767168 | tf_op jit(solution)/shard_map/jvp(chts,cshp->cthp)/dot_general | solution.py:91
  65.4 30.0 %all-to-all-done = f32[57,64,128]{2,0,1:T(8,128)} async-done(((f32[57,64,128]{2,0,1:T(8,128)}), f32[57,64,128]{2,0,1:T(8,128)}, u32[]{:S(2)}, u32[]{:S(2)}) %all-to-all-start) | async-done | bytes 1867808 | tf_op jit(solution)/shard_map/all_to_all | solution.py:208
  95.4 3.7 copy.253
  99.1 3.9 copy.254
  104.7 3.8 fusion.50
  108.5 2.3 copy.255
  110.9 6.4 %all-to-all-start.1 = ((f32[56,64,128]{2,0,1:T(8,128)}), f32[56,64,128]{2,0,1:T(8,128)}, u32[]{:S(2)}, u32[]{:S(2)}) async-start(f32[56,64,128]{2,0,1:T(8,128)} %copy.255), calls=%async_computation.1 | async-start | bytes 3670016 | tf_op jit(solution)/shard_map/all_to_all | solution.py:141
  117.5 2.9 slice_add_fusion
  120.4 42.1 %all-to-all-done.1 = f32[56,64,128]{2,0,1:T(8,128)} async-done(((f32[56,64,128]{2,0,1:T(8,128)}), f32[56,64,128]{2,0,1:T(8,128)}, u32[]{:S(2)}, u32[]{:S(2)}) %all-to-all-start.1) | async-done | bytes 1835040 | tf_op jit(solution)/shard_map/all_to_all | solution.py:141
  165.0 4.9 %multiply_reduce_fusion.3 = (f32[2,128]{1,0:T(2,128)S(1)}, f32[2,128,56,64]{1,3,2,0:T(8,128)S(1)}, f32[2,128,56,64]{1,3,2,0:T(8,128)S(1)}) fusion(f32[2,128,56,64]{1,0,3,2:T(2,128)S(1)} %copy-done.11, bf16[2,128,56,64]{1,3,2,0:T(8,128)(2,1)S(1)} %copy.241, f32[56]{0:T(128)S(1)} %copy-done.32, f32[2,128,56,64]{1,3,2,0:T(8,128)} %fusion.46, ...), kind=kOutput, calls=%fused_computation.61 | convolution fusion | flops 248643328 | bytes 20309664 | tf_op jit(solution)/shard_map/jvp(ctn,chpn->cthp)/dot_general | solution.py:113
  173.3 5.6 %fusion.47 = (bf16[2,56,8,8,128]{4,3,2,1,0:T(8,128)(2,1)}, f32[2,128,56,64]{1,3,2,0:T(8,128)S(1)}, f32[2,128,56,64]{1,3,2,0:T(8,128)}, bf16[2,128,56,64]{1,3,2,0:T(8,128)(2,1)}) fusion(f32[56]{0:T(128)S(1)} %copy-done.32, f32[2,128,56,64]{1,0,3,2:T(2,128)S(1)} %copy-done.11, f32[2,128,56,64]{1,3,2,0:T(8,128)S(1)} %get-tuple-element.112, ...), kind=kLoop, calls=%fused_computation.75 | loop fusion | flops 25690112 | bytes 29434080
  178.9 2.5 multiply_reduce_fusion
  181.4 2.3 copy.261
  183.7 6.7 %all-to-all-start.2 = ((f32[56,64,128]{2,0,1:T(8,128)}), f32[56,64,128]{2,0,1:T(8,128)}, u32[]{:S(2)}, u32[]{:S(2)}) async-start(f32[56,64,128]{2,0,1:T(8,128)} %copy.261), calls=%async_computation.2 | async-start | bytes 3670016 | tf_op jit(solution)/shard_map/all_to_all | solution.py:235
  190.4 8.5 %fusion.10 = (f32[2,56,128]{2,1,0:T(8,128)S(1)}, f32[2,56,128]{2,1,0:T(8,128)S(1)}, f32[2,56,128]{2,1,0:T(8,128)S(1)}, bf16[2,128,128]{2,1,0:T(8,128)(2,1)S(1)}) fusion(f32[2,56,128]{2,1,0:T(8,128)S(1)} %copy.248, f32[2,56,128]{2,1,0:T(8,128)S(1)} %copy.246, f32[2,128,128]{2,1,0:T(8,128)S(1)} %fusion.165, pred[128,128]{1,0:T(8,128)(4,1)S(1)} %iota_compare_fusion.2, ...), kind=kOutput, calls=%fused_computation.19 | convolution fusion | flops 264165376 | bytes 6004736 | tf_op jit(solution)/shard_map/transpose(jvp(chts,cshp->cthp))/dot_general | solution.py:91
  199.1 2.2 reduce_window_sum.75
  202.0 4.5 %convert_bitcast_fusion = bf16[2,56,8,8,128]{4,3,2,1,0:T(8,128)(2,1)S(1)} fusion(f32[2,56,128]{2,1,0:T(8,128)S(1)} %copy.248, f32[2,56,128]{2,1,0:T(8,128)S(1)} %copy.246, f32[2,128,128]{2,1,0:T(8,128)S(1)} %fusion.165, pred[128,128]{1,0:T(8,128)(4,1)S(1)} %iota_compare_fusion.2, f32[2,128,56,64]{1,3,2,0:T(8,128)} %copy-done.2), kind=kOutput, calls=%fused_computation.96 | convolution fusion | flops 245891072 | bytes 5767168 | tf_op jit(solution)/shard_map/transpose(jvp(chts,cshp->cthp))/dot_general | solution.py:91
  209.7 25.9 %all-to-all-done.2 = f32[56,64,128]{2,0,1:T(8,128)} async-done(((f32[56,64,128]{2,0,1:T(8,128)}), f32[56,64,128]{2,0,1:T(8,128)}, u32[]{:S(2)}, u32[]{:S(2)}) %all-to-all-start.2) | async-done | bytes 1835040 | tf_op jit(solution)/shard_map/all_to_all | solution.py:235
  235.6 3.9 fusion.53
  239.6 2.3 copy.269
  241.9 6.2 %all-to-all-start.3 = ((f32[56,64,128]{2,0,1:T(8,128)}), f32[56,64,128]{2,0,1:T(8,128)S(1)}, u32[]{:S(2)}, u32[]{:S(2)}) async-start(f32[56,64,128]{2,0,1:T(8,128)} %copy.269), calls=%async_computation.3 | async-start | bytes 3670016 | tf_op jit(solution)/shard_map/all_to_all | solution.py:148
  248.9 4.1 %convert_element_type.92 = f32[2,56,64,128]{3,2,1,0:T(8,128)} convert(bf16[2,56,64,128]{3,2,1,0:T(8,128)(2,1)} %get-tuple-element.141) | non-fusion elementwise | flops 917504 | bytes 5505024 | tf_op jit(solution)/shard_map/transpose(jvp())/convert_element_type | solution.py:114
  253.0 3.3 copy.276
  258.3 4.2 %fusion.81 = bf16[2,128,128]{2,1,0:T(8,128)(2,1)S(1)} fusion(f32[2,128,56,64]{1,3,2,0:T(8,128)} %copy-done.2, f32[2,128,56]{1,2,0:T(8,128)S(1)} %copy.252, f32[1,56,64,128]{3,2,1,0:T(8,128)} %slice_add_fusion, f32[56,64,128]{2,1,0:T(8,128)} %copy-done.6, f32[2,56]{1,0:T(2,128)S(1)} %subtract_exponential_fusion.1), kind=kOutput, calls=%fused_computation.111 | convolution fusion | flops 238583808 | bytes 7463360 | tf_op jit(solution)/shard_map/transpose(jvp(ctn,chpn->cthp))/dot_general | solution.py:113
  262.5 30.9 %all-to-all-done.3 = f32[56,64,128]{2,0,1:T(8,128)S(1)} async-done(((f32[56,64,128]{2,0,1:T(8,128)}), f32[56,64,128]{2,0,1:T(8,128)S(1)}, u32[]{:S(2)}, u32[]{:S(2)}) %all-to-all-start.3) | async-done | bytes 1835040 | tf_op jit(solution)/shard_map/all_to_all | solution.py:148
  293.4 2.5 fusion.121
  296.5 4.6 %fusion.27 = (f32[56]{0:T(128)S(1)}, f32[2,128,56]{1,2,0:T(8,128)S(1)}, f32[2,128,56]{1,2,0:T(8,128)S(1)}, bf16[2,56,8,8,128]{4,3,2,1,0:T(8,128)(2,1)}) fusion(f32[2,128,56,64]{1,3,2,0:T(8,128)S(1)} %copy-done.3, bf16[2,128,56,64]{1,3,2,0:T(8,128)(2,1)S(1)} %copy-done.8, f32[2,128,56,64]{1,3,2,0:T(8,128)} %copy-done.12, f32[2,128,56]{1,2,0:T(8,128)S(1)} %copy.244, ...), kind=kOutput, calls=%fused_computation.47 | convolution fusion | flops 247697344 | bytes 13082848 | tf_op jit(solution)/shard_map/transpose(jvp(cshp,csn->chpn))/dot_general | solution.py:52
  309.7 3.1 multiply_reduce_fusion.5
  313.7 4.3 %bitcast_add_fusion = bf16[256,56,64]{0,2,1:T(8,128)(2,1)} fusion(bf16[2,56,8,8,128]{4,3,2,1,0:T(8,128)(2,1)} %get-tuple-element.121, bf16[256,56,64]{0,2,1:T(8,128)(2,1)} %bitcast.185, bf16[2,56,8,8,128]{4,3,2,1,0:T(8,128)(2,1)} %get-tuple-element.109), kind=kLoop, calls=%fused_computation.77 | loop fusion | flops 1835008 | bytes 7340032 | tf_op jit(solution)/shard_map/add | solution.py:246
  318.0 2.8 copy.274
  320.8 3.3 fusion.150
  324.2 2.6 multiply_reduce_fusion.7
  327.0 3.1 concatenate.29
  333.0 32.5 %all_to_all.36 = f32[256,1,557]{2,1,0:T(1,128)S(1)} all-to-all(f32[256,1,557]{2,1,0:T(1,128)S(1)} %all_to_all.29), channel_id=1, replica_groups=mesh['seq'=64,'batch'=4] {'seq','batch'}, dimensions={0} | all-to-all | bytes 1140736 | tf_op jit(solution)/shard_map/all_to_all | solution.py:158
  367.2 5.7 %all-to-all-start.5 = ((f32[256,1,557]{2,1,0:T(1,128)}), f32[256,1,557]{2,1,0:T(1,128)S(1)}, u32[]{:S(2)}, u32[]{:S(2)}) async-start(f32[256,1,557]{2,1,0:T(1,128)} %broadcast_in_dim.121), calls=%async_computation.5 | async-start | bytes 1310720 | tf_op jit(solution)/shard_map/all_to_all | solution.py:161
  372.9 6.7 %copy.297 = bf16[2,128,56,64]{3,2,1,0:T(8,128)(2,1)} copy(bf16[2,128,56,64]{1,3,2,0:T(8,128)(2,1)S(1)} %copy-done.13) | data formatting | bytes 3670016
  379.6 5.8 %reshape.361 = bf16[1,256,3584]{2,1,0:T(8,128)(2,1)} reshape(bf16[2,128,56,64]{3,2,1,0:T(8,128)(2,1)} %copy.297) | data formatting | bytes 3670016
  385.4 11.7 %all-to-all-done.5 = f32[256,1,557]{2,1,0:T(1,128)S(1)} async-done(((f32[256,1,557]{2,1,0:T(1,128)}), f32[256,1,557]{2,1,0:T(1,128)S(1)}, u32[]{:S(2)}, u32[]{:S(2)}) %all-to-all-start.5) | async-done | bytes 570400 | tf_op jit(solution)/shard_map/all_to_all | solution.py:161
  (178 shorter events, 46.6 us)
Async XLA Ops:
  0.6 52.2 %copy-start = (bf16[16,3584]{1,0:T(8,128)(2,1)S(1)}, bf16[16,3584]{1,0:T(8,128)(2,1)}, u32[]{:S(2)}) copy-start(bf16[16,3584]{1,0:T(8,128)(2,1)} %param.14) | copy-start | bytes 344068
  1.4 6.7 %collective-permute-start = (s32[3]{0:T(128)S(1)}, s32[3]{0:T(128)S(1)}, u32[]{:S(2)}, u32[]{:S(2)}) collective-permute-start(s32[3]{0:T(128)S(1)} %add_bitcast_fusion.1), channel_id=1, source_target_pairs={{0,4},{4,8},{8,12},{12,16},{16,20},{20,24},{24,28},{28,32},{32,36}... | collective-permute-start | bytes 44 | tf_op jit(solution)/shard_map/ppermute | solution.py:18
  7.0 7.7 %copy-start.36 = (f32[56]{0:T(128)}, f32[56]{0:T(128)S(1)}, u32[]{:S(2)}) copy-start(f32[56]{0:T(128)S(1)} %exponential_negate_fusion) | copy-start | bytes 676
  9.1 247.3 %copy-start.19 = (pred[259,16]{1,0:T(8,128)(4,1)}, pred[259,16]{1,0:T(8,128)(4,1)S(1)}, u32[]{:S(2)}) copy-start(pred[259,16]{1,0:T(8,128)(4,1)S(1)} %get-tuple-element.138) | copy-start | bytes 12436
  9.1 1.7 copy-start.26
  14.6 0.7 copy-start.33
  16.2 10.3 %copy-start.35 = (f32[56]{0:T(128)}, f32[56]{0:T(128)S(1)}, u32[]{:S(2)}) copy-start(f32[56]{0:T(128)S(1)} %get-tuple-element.115) | copy-start | bytes 676
  26.3 164.1 %copy-start.7 = (bf16[2,128,56,64]{1,3,2,0:T(8,128)(2,1)}, bf16[2,128,56,64]{1,3,2,0:T(8,128)(2,1)S(1)}, u32[]{:S(2)}) copy-start(bf16[2,128,56,64]{1,3,2,0:T(8,128)(2,1)S(1)} %copy.241) | copy-start | bytes 5505028
  26.5 1.3 copy-start.28
  26.6 0.9 copy-start.30
  27.2 1.8 copy-start.4
  31.5 63.9 %all-to-all-start = ((f32[57,64,128]{2,0,1:T(8,128)}), f32[57,64,128]{2,0,1:T(8,128)}, u32[]{:S(2)}, u32[]{:S(2)}) async-start(f32[57,64,128]{2,0,1:T(8,128)} %copy.245), calls=%async_computation | async-start | bytes 4194304 | tf_op jit(solution)/shard_map/all_to_all | solution.py:208
  108.5 8.7 %copy-start.27 = (f32[3584]{0:T(1024)S(1)}, f32[3584]{0:T(1024)}, u32[]{:S(2)}) copy-start(f32[3584]{0:T(1024)} %param.20) | copy-start | bytes 43012
  110.9 51.6 %all-to-all-start.1 = ((f32[56,64,128]{2,0,1:T(8,128)}), f32[56,64,128]{2,0,1:T(8,128)}, u32[]{:S(2)}, u32[]{:S(2)}) async-start(f32[56,64,128]{2,0,1:T(8,128)} %copy.255), calls=%async_computation.1 | async-start | bytes 3670016 | tf_op jit(solution)/shard_map/all_to_all | solution.py:141
  117.4 47.0 %copy-start.32 = (f32[56]{0:T(128)S(1)}, f32[56]{0:T(128)}, u32[]{:S(2)}) copy-start(f32[56]{0:T(128)} %param.19) | copy-start | bytes 676
  162.4 2.6 copy-start.11
  164.4 14.5 %copy-start.6 = (f32[56,64,128]{2,1,0:T(8,128)}, f32[56,64,128]{2,1,0:T(8,128)S(1)}, u32[]{:S(2)}) copy-start(f32[56,64,128]{2,1,0:T(8,128)S(1)} %copy.256) | copy-start | bytes 5505028
  165.0 4.9 %copy-start.9 = (bf16[2,128,56,64]{1,0,3,2:T(2,128)(2,1)S(1)}, bf16[2,128,56,64]{1,0,3,2:T(2,128)(2,1)}, u32[]{:S(2)}) copy-start(bf16[2,128,56,64]{1,0,3,2:T(2,128)(2,1)} %reshape_squeeze.3) | copy-start | bytes 5505028
  169.9 9.0 %copy-start.12 = (f32[2,128,56,64]{1,3,2,0:T(8,128)}, f32[2,128,56,64]{1,3,2,0:T(8,128)S(1)}, u32[]{:S(2)}) copy-start(f32[2,128,56,64]{1,3,2,0:T(8,128)S(1)} %get-tuple-element.140) | copy-start | bytes 11010052
  169.9 3.4 copy-start.14
  178.9 2.5 copy-start.2
  183.7 52.0 %all-to-all-start.2 = ((f32[56,64,128]{2,0,1:T(8,128)}), f32[56,64,128]{2,0,1:T(8,128)}, u32[]{:S(2)}, u32[]{:S(2)}) async-start(f32[56,64,128]{2,0,1:T(8,128)} %copy.261), calls=%async_computation.2 | async-start | bytes 3670016 | tf_op jit(solution)/shard_map/all_to_all | solution.py:235
  239.6 8.5 %copy-start.18 = (bf16[16,3840]{1,0:T(8,128)(2,1)S(1)}, bf16[16,3840]{1,0:T(8,128)(2,1)}, u32[]{:S(2)}) copy-start(bf16[16,3840]{1,0:T(8,128)(2,1)} %param.13) | copy-start | bytes 368644
  241.9 51.5 %all-to-all-start.3 = ((f32[56,64,128]{2,0,1:T(8,128)}), f32[56,64,128]{2,0,1:T(8,128)S(1)}, u32[]{:S(2)}, u32[]{:S(2)}) async-start(f32[56,64,128]{2,0,1:T(8,128)} %copy.269), calls=%async_computation.3 | async-start | bytes 3670016 | tf_op jit(solution)/shard_map/all_to_all | solution.py:148
  248.1 4.9 %copy-start.10 = (f32[2,128,56,64]{1,3,2,0:T(8,128)S(1)}, f32[2,128,56,64]{1,3,2,0:T(8,128)}, u32[]{:S(2)}) copy-start(f32[2,128,56,64]{1,3,2,0:T(8,128)} %get-tuple-element.117) | copy-start | bytes 11010052
  293.4 2.6 copy-start.3
  293.4 3.2 copy-start.8
  307.0 2.8 copy-start.5
  308.9 3.9 copy-start.31
  308.9 3.9 copy-start.29
  308.9 4.2 %copy-start.23 = (f32[256,56]{0,1:T(8,128)S(1)}, f32[256,56]{0,1:T(8,128)}, u32[]{:S(2)}) copy-start(f32[256,56]{0,1:T(8,128)} %copy.298) | copy-start | bytes 172036
  309.0 4.2 %copy-start.25 = (f32[256,56]{0,1:T(8,128)S(1)}, f32[256,56]{0,1:T(8,128)}, u32[]{:S(2)}) copy-start(f32[256,56]{0,1:T(8,128)} %get-tuple-element.139) | copy-start | bytes 172036
  309.0 4.3 %copy-start.20 = (pred[259,16]{1,0:T(8,128)(4,1)S(1)}, pred[259,16]{1,0:T(8,128)(4,1)}, u32[]{:S(2)}) copy-start(pred[259,16]{1,0:T(8,128)(4,1)} %copy-done.19) | copy-start | bytes 12436
  309.0 4.3 %copy-start.24 = (f32[256,56]{0,1:T(8,128)S(1)}, f32[256,56]{0,1:T(8,128)}, u32[]{:S(2)}) copy-start(f32[256,56]{0,1:T(8,128)} %copy_bitcast_fusion.2) | copy-start | bytes 172036
  309.0 4.3 %copy-start.37 = (f32[56]{0:T(128)S(1)}, f32[56]{0:T(128)}, u32[]{:S(2)}) copy-start(f32[56]{0:T(128)} %copy-done.36) | copy-start | bytes 676
  309.0 4.7 %copy-start.34 = (f32[56]{0:T(128)S(1)}, f32[56]{0:T(128)}, u32[]{:S(2)}) copy-start(f32[56]{0:T(128)} %param.16) | copy-start | bytes 676
  318.0 2.8 copy-start.21
  320.8 3.4 copy-start.15
  320.8 3.4 copy-start.16
  320.8 3.4 copy-start.17
  324.2 2.7 copy-start.22
  327.0 45.9 %copy-start.13 = (bf16[2,128,56,64]{1,3,2,0:T(8,128)(2,1)S(1)}, bf16[2,128,56,64]{1,3,2,0:T(8,128)(2,1)}, u32[]{:S(2)}) copy-start(bf16[2,128,56,64]{1,3,2,0:T(8,128)(2,1)} %get-tuple-element.118) | copy-start | bytes 5505028
  367.2 29.9 %all-to-all-start.5 = ((f32[256,1,557]{2,1,0:T(1,128)}), f32[256,1,557]{2,1,0:T(1,128)S(1)}, u32[]{:S(2)}, u32[]{:S(2)}) async-start(f32[256,1,557]{2,1,0:T(1,128)} %broadcast_in_dim.121), calls=%async_computation.5 | async-start | bytes 1310720 | tf_op jit(solution)/shard_map/all_to_all | solution.py:161
  379.6 24.4 %copy-start.1 = (bf16[16,3584]{1,0:T(8,128)(2,1)S(1)}, bf16[16,3584]{1,0:T(8,128)(2,1)}, u32[]{:S(2)}) copy-start(bf16[16,3584]{1,0:T(8,128)(2,1)} %param.14) | copy-start | bytes 344068

commit v3 on v2

--- a/solution.py
+++ b/solution.py
@@ -9,7 +9,7 @@
 
 
 EPS = 1e-05
-HIGH = lax.Precision.HIGHEST
+HIGH = lax.Precision.HIGH
 
 
 def shifted(value, axis, steps):

time: 412 us -> 409 us (level)
  no operation moved by 1% of the time
where the time goes in v3:
time: 409 us; the launch traced here: 401 us
  waiting for transfers between devices  141 us (34%)
  local copies, waits for them, and re-layouts  85.4 us (21%)
  matrix products  49.9 us (12%)
  other arithmetic  47.3 us (12%)
  starting transfers between devices  42.8 us (10%)
  blocking collectives  32.5 us (8%)
    all_to_all x1, waiting for transfers between devices, settle_forward(): lax.all_to_all(settled, 'seq', split_axis=1, concat_axis=1, tiled=True)  42.1 us
    all_to_all x1, blocking collectives, spread_sum(): lax.all_to_all(padded, axes, split_axis=0, concat_axis=0, tiled=True)  32.5 us
    all_to_all x1, waiting for transfers between devices, settle_backward(): lax.all_to_all(settled, 'seq', split_axis=1, concat_axis=1, tiled=True)  31.6 us
    all_to_all x1, waiting for transfers between devices, local(): lax.all_to_all(outgoing, 'seq', split_axis=1, concat_axis=1, tiled=True)  30 us
    all_to_all x1, waiting for transfers between devices, local(): lax.all_to_all(back_flat.reshape(heads, parts, span), 'seq', split_axis=1...  25.9 us
    unnamed x81, local copies, waits for them, and re-layouts  21.3 us
    dot_general x3, matrix products, intra(): jnp.einsum('chts,cshp->cthp', mixing, blocked, preferred_element_type=jnp...  17.4 us
    all_to_all x1, starting transfers between devices, local(): lax.all_to_all(outgoing, 'seq', split_axis=1, concat_axis=1, tiled=True)  12.9 us
  transfers between devices with their start and end apart: 6, of which 5 were waited for; matrix products, arithmetic and copies ran while one was open for 18% of the time, Pallas kernels for 0%

profile of v3, /device:TPU:1, one launch (start us, length us, event | category | flops | bytes accessed | tf_op | source)
XLA Modules:
  0.0 401.2 jit_solution(1217067777258442909)
XLA Ops:
  1.4 4.9 %collective-permute-start = (s32[3]{0:T(128)S(1)}, s32[3]{0:T(128)S(1)}, u32[]{:S(2)}, u32[]{:S(2)}) collective-permute-start(s32[3]{0:T(128)S(1)} %add_bitcast_fusion.1), channel_id=1, source_target_pairs={{0,4},{4,8},{8,12},{12,16},{16,20},{20,24},{24,28},{28,32},{32,36}... | collective-permute-start | bytes 44 | tf_op jit(solution)/shard_map/ppermute | solution.py:18
  10.7 3.8 multiply_convert_fusion.1
  16.9 3.5 reshape.362
  20.5 5.8 %copy.241 = bf16[2,128,56,64]{1,3,2,0:T(8,128)(2,1)S(1)} copy(bf16[2,128,56,64]{3,2,1,0:T(8,128)(2,1)} %reshape.362) | data formatting | bytes 3670016 | tf_op jit(solution)/shard_map/jvp()/reshape;jvp()/reshape | solution.py:51
  29.0 2.4 copy.245
  31.4 12.9 %all-to-all-start = ((f32[57,64,128]{2,0,1:T(8,128)}), f32[57,64,128]{2,0,1:T(8,128)}, u32[]{:S(2)}, u32[]{:S(2)}) async-start(f32[57,64,128]{2,0,1:T(8,128)} %copy.245), calls=%async_computation | async-start | bytes 4194304 | tf_op jit(solution)/shard_map/all_to_all | solution.py:208
  44.3 3.8 copy.251
  48.1 4.6 %reshape_squeeze.3 = bf16[2,128,56,64]{1,0,3,2:T(2,128)(2,1)} reshape(bf16[1,256,3584]{1,2,0:T(8,128)(2,1)} %copy.251) | data formatting | bytes 3670016 | tf_op jit(solution)/shard_map/reshape;squeeze | solution.py:212
  52.9 2.5 fusion.124
  55.4 5.4 %reshape.330 = f32[2,128,56,64]{1,0,3,2:T(2,128)} reshape(f32[256,3584]{0,1:T(8,128)} %fusion.124) | data formatting | bytes 7340032 | tf_op jit(solution)/shard_map/reshape | solution.py:211
  60.9 4.4 %fusion.46 = f32[2,128,56,64]{1,3,2,0:T(8,128)} fusion(bf16[2,128,56,64]{1,3,2,0:T(8,128)(2,1)S(1)} %copy.241, f32[2,56,128]{2,1,0:T(8,128)S(1)} %copy.248, f32[2,56,128]{2,1,0:T(8,128)S(1)} %copy.246, f32[2,128,128]{2,1,0:T(8,128)S(1)} %fusion.165, pred[128,128]{1,0:T(8,128)(4,1)S(1)} %iota_compare_fusion.2), kind=kOutput, calls=%fused_computation.73 | convolution fusion | flops 245891072 | bytes 5767168 | tf_op jit(solution)/shard_map/jvp(chts,cshp->cthp)/dot_general | solution.py:91
  65.3 30.0 %all-to-all-done = f32[57,64,128]{2,0,1:T(8,128)} async-done(((f32[57,64,128]{2,0,1:T(8,128)}), f32[57,64,128]{2,0,1:T(8,128)}, u32[]{:S(2)}, u32[]{:S(2)}) %all-to-all-start) | async-done | bytes 1867808 | tf_op jit(solution)/shard_map/all_to_all | solution.py:208
  95.3 3.7 copy.253
  99.0 3.9 copy.254
  104.7 2.7 fusion.50
  107.4 2.3 copy.255
  109.7 6.4 %all-to-all-start.1 = ((f32[56,64,128]{2,0,1:T(8,128)}), f32[56,64,128]{2,0,1:T(8,128)}, u32[]{:S(2)}, u32[]{:S(2)}) async-start(f32[56,64,128]{2,0,1:T(8,128)} %copy.255), calls=%async_computation.1 | async-start | bytes 3670016 | tf_op jit(solution)/shard_map/all_to_all | solution.py:141
  116.3 2.9 slice_add_fusion
  119.2 42.1 %all-to-all-done.1 = f32[56,64,128]{2,0,1:T(8,128)} async-done(((f32[56,64,128]{2,0,1:T(8,128)}), f32[56,64,128]{2,0,1:T(8,128)}, u32[]{:S(2)}, u32[]{:S(2)}) %all-to-all-start.1) | async-done | bytes 1835040 | tf_op jit(solution)/shard_map/all_to_all | solution.py:141
  163.8 4.9 %multiply_reduce_fusion.3 = (f32[2,128]{1,0:T(2,128)S(1)}, f32[2,128,56,64]{1,3,2,0:T(8,128)S(1)}, f32[2,128,56,64]{1,3,2,0:T(8,128)S(1)}) fusion(f32[2,128,56,64]{1,0,3,2:T(2,128)S(1)} %copy-done.11, bf16[2,128,56,64]{1,3,2,0:T(8,128)(2,1)S(1)} %copy.241, f32[56]{0:T(128)S(1)} %copy-done.32, f32[2,128,56,64]{1,3,2,0:T(8,128)} %fusion.46, ...), kind=kOutput, calls=%fused_computation.61 | convolution fusion | flops 248643328 | bytes 20309664 | tf_op jit(solution)/shard_map/jvp(ctn,chpn->cthp)/dot_general | solution.py:113
  172.1 5.6 %fusion.47 = (bf16[2,56,8,8,128]{4,3,2,1,0:T(8,128)(2,1)}, f32[2,128,56,64]{1,3,2,0:T(8,128)S(1)}, f32[2,128,56,64]{1,3,2,0:T(8,128)}, bf16[2,128,56,64]{1,3,2,0:T(8,128)(2,1)}) fusion(f32[56]{0:T(128)S(1)} %copy-done.32, f32[2,128,56,64]{1,0,3,2:T(2,128)S(1)} %copy-done.11, f32[2,128,56,64]{1,3,2,0:T(8,128)S(1)} %get-tuple-element.112, ...), kind=kLoop, calls=%fused_computation.75 | loop fusion | flops 25690112 | bytes 29434080
  177.7 2.5 multiply_reduce_fusion
  180.2 2.3 copy.261
  182.5 6.7 %all-to-all-start.2 = ((f32[56,64,128]{2,0,1:T(8,128)}), f32[56,64,128]{2,0,1:T(8,128)}, u32[]{:S(2)}, u32[]{:S(2)}) async-start(f32[56,64,128]{2,0,1:T(8,128)} %copy.261), calls=%async_computation.2 | async-start | bytes 3670016 | tf_op jit(solution)/shard_map/all_to_all | solution.py:235
  189.3 8.5 %fusion.10 = (f32[2,56,128]{2,1,0:T(8,128)S(1)}, f32[2,56,128]{2,1,0:T(8,128)S(1)}, f32[2,56,128]{2,1,0:T(8,128)S(1)}, bf16[2,128,128]{2,1,0:T(8,128)(2,1)S(1)}) fusion(f32[2,56,128]{2,1,0:T(8,128)S(1)} %copy.248, f32[2,56,128]{2,1,0:T(8,128)S(1)} %copy.246, f32[2,128,128]{2,1,0:T(8,128)S(1)} %fusion.165, pred[128,128]{1,0:T(8,128)(4,1)S(1)} %iota_compare_fusion.2, ...), kind=kOutput, calls=%fused_computation.19 | convolution fusion | flops 264165376 | bytes 6004736 | tf_op jit(solution)/shard_map/transpose(jvp(chts,cshp->cthp))/dot_general | solution.py:91
  197.9 2.2 reduce_window_sum.75
  200.8 4.5 %convert_bitcast_fusion = bf16[2,56,8,8,128]{4,3,2,1,0:T(8,128)(2,1)S(1)} fusion(f32[2,56,128]{2,1,0:T(8,128)S(1)} %copy.248, f32[2,56,128]{2,1,0:T(8,128)S(1)} %copy.246, f32[2,128,128]{2,1,0:T(8,128)S(1)} %fusion.165, pred[128,128]{1,0:T(8,128)(4,1)S(1)} %iota_compare_fusion.2, f32[2,128,56,64]{1,3,2,0:T(8,128)} %copy-done.2), kind=kOutput, calls=%fused_computation.96 | convolution fusion | flops 245891072 | bytes 5767168 | tf_op jit(solution)/shard_map/transpose(jvp(chts,cshp->cthp))/dot_general | solution.py:91
  208.6 25.9 %all-to-all-done.2 = f32[56,64,128]{2,0,1:T(8,128)} async-done(((f32[56,64,128]{2,0,1:T(8,128)}), f32[56,64,128]{2,0,1:T(8,128)}, u32[]{:S(2)}, u32[]{:S(2)}) %all-to-all-start.2) | async-done | bytes 1835040 | tf_op jit(solution)/shard_map/all_to_all | solution.py:235
  234.4 2.9 fusion.53
  237.4 2.3 copy.269
  239.7 6.2 %all-to-all-start.3 = ((f32[56,64,128]{2,0,1:T(8,128)}), f32[56,64,128]{2,0,1:T(8,128)S(1)}, u32[]{:S(2)}, u32[]{:S(2)}) async-start(f32[56,64,128]{2,0,1:T(8,128)} %copy.269), calls=%async_computation.3 | async-start | bytes 3670016 | tf_op jit(solution)/shard_map/all_to_all | solution.py:148
  246.7 4.1 %convert_element_type.92 = f32[2,56,64,128]{3,2,1,0:T(8,128)} convert(bf16[2,56,64,128]{3,2,1,0:T(8,128)(2,1)} %get-tuple-element.141) | non-fusion elementwise | flops 917504 | bytes 5505024 | tf_op jit(solution)/shard_map/transpose(jvp())/convert_element_type | solution.py:114
  250.9 3.3 copy.276
  255.4 4.2 %fusion.81 = bf16[2,128,128]{2,1,0:T(8,128)(2,1)S(1)} fusion(f32[2,128,56,64]{1,3,2,0:T(8,128)} %copy-done.2, f32[2,128,56]{1,2,0:T(8,128)S(1)} %copy.252, f32[1,56,64,128]{3,2,1,0:T(8,128)} %slice_add_fusion, f32[56,64,128]{2,1,0:T(8,128)} %copy-done.6, f32[2,56]{1,0:T(2,128)S(1)} %subtract_exponential_fusion.1), kind=kOutput, calls=%fused_computation.111 | convolution fusion | flops 238583808 | bytes 7463360 | tf_op jit(solution)/shard_map/transpose(jvp(ctn,chpn->cthp))/dot_general | solution.py:113
  259.6 31.6 %all-to-all-done.3 = f32[56,64,128]{2,0,1:T(8,128)S(1)} async-done(((f32[56,64,128]{2,0,1:T(8,128)}), f32[56,64,128]{2,0,1:T(8,128)S(1)}, u32[]{:S(2)}, u32[]{:S(2)}) %all-to-all-start.3) | async-done | bytes 1835040 | tf_op jit(solution)/shard_map/all_to_all | solution.py:148
  291.2 2.5 fusion.121
  294.4 4.6 %fusion.27 = (f32[56]{0:T(128)S(1)}, f32[2,128,56]{1,2,0:T(8,128)S(1)}, f32[2,128,56]{1,2,0:T(8,128)S(1)}, bf16[2,56,8,8,128]{4,3,2,1,0:T(8,128)(2,1)}) fusion(f32[2,128,56,64]{1,3,2,0:T(8,128)S(1)} %copy-done.3, bf16[2,128,56,64]{1,3,2,0:T(8,128)(2,1)S(1)} %copy-done.8, f32[2,128,56,64]{1,3,2,0:T(8,128)} %copy-done.12, f32[2,128,56]{1,2,0:T(8,128)S(1)} %copy.244, ...), kind=kOutput, calls=%fused_computation.47 | convolution fusion | flops 247697344 | bytes 13082848 | tf_op jit(solution)/shard_map/transpose(jvp(cshp,csn->chpn))/dot_general | solution.py:52
  300.2 2.2 reduce_window_sum.79
  307.5 3.1 multiply_reduce_fusion.5
  311.5 4.3 %bitcast_add_fusion = bf16[256,56,64]{0,2,1:T(8,128)(2,1)} fusion(bf16[2,56,8,8,128]{4,3,2,1,0:T(8,128)(2,1)} %get-tuple-element.121, bf16[256,56,64]{0,2,1:T(8,128)(2,1)} %bitcast.185, bf16[2,56,8,8,128]{4,3,2,1,0:T(8,128)(2,1)} %get-tuple-element.109), kind=kLoop, calls=%fused_computation.77 | loop fusion | flops 1835008 | bytes 7340032 | tf_op jit(solution)/shard_map/add | solution.py:246
  315.8 2.8 copy.274
  318.6 3.3 fusion.150
  323.8 3.0 concatenate.29
  329.8 32.5 %all_to_all.36 = f32[256,1,557]{2,1,0:T(1,128)S(1)} all-to-all(f32[256,1,557]{2,1,0:T(1,128)S(1)} %all_to_all.29), channel_id=1, replica_groups=mesh['seq'=64,'batch'=4] {'seq','batch'}, dimensions={0} | all-to-all | bytes 1140736 | tf_op jit(solution)/shard_map/all_to_all | solution.py:158
  364.0 5.7 %all-to-all-start.5 = ((f32[256,1,557]{2,1,0:T(1,128)}), f32[256,1,557]{2,1,0:T(1,128)S(1)}, u32[]{:S(2)}, u32[]{:S(2)}) async-start(f32[256,1,557]{2,1,0:T(1,128)} %broadcast_in_dim.121), calls=%async_computation.5 | async-start | bytes 1310720 | tf_op jit(solution)/shard_map/all_to_all | solution.py:161
  369.7 6.7 %copy.297 = bf16[2,128,56,64]{3,2,1,0:T(8,128)(2,1)} copy(bf16[2,128,56,64]{1,3,2,0:T(8,128)(2,1)S(1)} %copy-done.13) | data formatting | bytes 3670016
  376.4 5.8 %reshape.361 = bf16[1,256,3584]{2,1,0:T(8,128)(2,1)} reshape(bf16[2,128,56,64]{3,2,1,0:T(8,128)(2,1)} %copy.297) | data formatting | bytes 3670016
  382.2 11.7 %all-to-all-done.5 = f32[256,1,557]{2,1,0:T(1,128)S(1)} async-done(((f32[256,1,557]{2,1,0:T(1,128)}), f32[256,1,557]{2,1,0:T(1,128)S(1)}, u32[]{:S(2)}, u32[]{:S(2)}) %all-to-all-start.5) | async-done | bytes 570400 | tf_op jit(solution)/shard_map/all_to_all | solution.py:161
  (178 shorter events, 45.3 us)
Async XLA Ops:
  0.6 52.2 %copy-start = (bf16[16,3584]{1,0:T(8,128)(2,1)S(1)}, bf16[16,3584]{1,0:T(8,128)(2,1)}, u32[]{:S(2)}) copy-start(bf16[16,3584]{1,0:T(8,128)(2,1)} %param.14) | copy-start | bytes 344068
  1.4 6.7 %collective-permute-start = (s32[3]{0:T(128)S(1)}, s32[3]{0:T(128)S(1)}, u32[]{:S(2)}, u32[]{:S(2)}) collective-permute-start(s32[3]{0:T(128)S(1)} %add_bitcast_fusion.1), channel_id=1, source_target_pairs={{0,4},{4,8},{8,12},{12,16},{16,20},{20,24},{24,28},{28,32},{32,36}... | collective-permute-start | bytes 44 | tf_op jit(solution)/shard_map/ppermute | solution.py:18
  7.0 7.7 %copy-start.36 = (f32[56]{0:T(128)}, f32[56]{0:T(128)S(1)}, u32[]{:S(2)}) copy-start(f32[56]{0:T(128)S(1)} %exponential_negate_fusion) | copy-start | bytes 676
  9.1 245.1 %copy-start.19 = (pred[259,16]{1,0:T(8,128)(4,1)}, pred[259,16]{1,0:T(8,128)(4,1)S(1)}, u32[]{:S(2)}) copy-start(pred[259,16]{1,0:T(8,128)(4,1)S(1)} %get-tuple-element.138) | copy-start | bytes 12436
  9.1 1.7 copy-start.26
  14.6 0.7 copy-start.33
  16.2 10.3 %copy-start.35 = (f32[56]{0:T(128)}, f32[56]{0:T(128)S(1)}, u32[]{:S(2)}) copy-start(f32[56]{0:T(128)S(1)} %get-tuple-element.115) | copy-start | bytes 676
  26.3 163.0 %copy-start.7 = (bf16[2,128,56,64]{1,3,2,0:T(8,128)(2,1)}, bf16[2,128,56,64]{1,3,2,0:T(8,128)(2,1)S(1)}, u32[]{:S(2)}) copy-start(bf16[2,128,56,64]{1,3,2,0:T(8,128)(2,1)S(1)} %copy.241) | copy-start | bytes 5505028
  26.4 1.3 copy-start.28
  26.5 0.9 copy-start.30
  27.2 1.8 copy-start.4
  31.4 63.9 %all-to-all-start = ((f32[57,64,128]{2,0,1:T(8,128)}), f32[57,64,128]{2,0,1:T(8,128)}, u32[]{:S(2)}, u32[]{:S(2)}) async-start(f32[57,64,128]{2,0,1:T(8,128)} %copy.245), calls=%async_computation | async-start | bytes 4194304 | tf_op jit(solution)/shard_map/all_to_all | solution.py:208
  107.3 8.7 %copy-start.27 = (f32[3584]{0:T(1024)S(1)}, f32[3584]{0:T(1024)}, u32[]{:S(2)}) copy-start(f32[3584]{0:T(1024)} %param.20) | copy-start | bytes 43012
  109.7 51.6 %all-to-all-start.1 = ((f32[56,64,128]{2,0,1:T(8,128)}), f32[56,64,128]{2,0,1:T(8,128)}, u32[]{:S(2)}, u32[]{:S(2)}) async-start(f32[56,64,128]{2,0,1:T(8,128)} %copy.255), calls=%async_computation.1 | async-start | bytes 3670016 | tf_op jit(solution)/shard_map/all_to_all | solution.py:141
  116.3 47.0 %copy-start.32 = (f32[56]{0:T(128)S(1)}, f32[56]{0:T(128)}, u32[]{:S(2)}) copy-start(f32[56]{0:T(128)} %param.19) | copy-start | bytes 676
  161.3 2.6 copy-start.11
  163.3 14.5 %copy-start.6 = (f32[56,64,128]{2,1,0:T(8,128)}, f32[56,64,128]{2,1,0:T(8,128)S(1)}, u32[]{:S(2)}) copy-start(f32[56,64,128]{2,1,0:T(8,128)S(1)} %copy.256) | copy-start | bytes 5505028
  163.8 4.9 %copy-start.9 = (bf16[2,128,56,64]{1,0,3,2:T(2,128)(2,1)S(1)}, bf16[2,128,56,64]{1,0,3,2:T(2,128)(2,1)}, u32[]{:S(2)}) copy-start(bf16[2,128,56,64]{1,0,3,2:T(2,128)(2,1)} %reshape_squeeze.3) | copy-start | bytes 5505028
  168.7 9.0 %copy-start.12 = (f32[2,128,56,64]{1,3,2,0:T(8,128)}, f32[2,128,56,64]{1,3,2,0:T(8,128)S(1)}, u32[]{:S(2)}) copy-start(f32[2,128,56,64]{1,3,2,0:T(8,128)S(1)} %get-tuple-element.140) | copy-start | bytes 11010052
  168.7 3.4 copy-start.14
  177.7 2.5 copy-start.2
  182.5 52.0 %all-to-all-start.2 = ((f32[56,64,128]{2,0,1:T(8,128)}), f32[56,64,128]{2,0,1:T(8,128)}, u32[]{:S(2)}, u32[]{:S(2)}) async-start(f32[56,64,128]{2,0,1:T(8,128)} %copy.261), calls=%async_computation.2 | async-start | bytes 3670016 | tf_op jit(solution)/shard_map/all_to_all | solution.py:235
  237.4 8.5 %copy-start.18 = (bf16[16,3840]{1,0:T(8,128)(2,1)S(1)}, bf16[16,3840]{1,0:T(8,128)(2,1)}, u32[]{:S(2)}) copy-start(bf16[16,3840]{1,0:T(8,128)(2,1)} %param.13) | copy-start | bytes 368644
  239.7 51.5 %all-to-all-start.3 = ((f32[56,64,128]{2,0,1:T(8,128)}), f32[56,64,128]{2,0,1:T(8,128)S(1)}, u32[]{:S(2)}, u32[]{:S(2)}) async-start(f32[56,64,128]{2,0,1:T(8,128)} %copy.269), calls=%async_computation.3 | async-start | bytes 3670016 | tf_op jit(solution)/shard_map/all_to_all | solution.py:148
  245.9 4.9 %copy-start.10 = (f32[2,128,56,64]{1,3,2,0:T(8,128)S(1)}, f32[2,128,56,64]{1,3,2,0:T(8,128)}, u32[]{:S(2)}) copy-start(f32[2,128,56,64]{1,3,2,0:T(8,128)} %get-tuple-element.117) | copy-start | bytes 11010052
  291.2 2.6 copy-start.3
  291.2 3.2 copy-start.8
  304.8 2.8 copy-start.5
  306.7 3.9 copy-start.31
  306.8 3.9 copy-start.29
  306.8 4.2 %copy-start.23 = (f32[256,56]{0,1:T(8,128)S(1)}, f32[256,56]{0,1:T(8,128)}, u32[]{:S(2)}) copy-start(f32[256,56]{0,1:T(8,128)} %copy.298) | copy-start | bytes 172036
  306.8 4.2 %copy-start.25 = (f32[256,56]{0,1:T(8,128)S(1)}, f32[256,56]{0,1:T(8,128)}, u32[]{:S(2)}) copy-start(f32[256,56]{0,1:T(8,128)} %get-tuple-element.139) | copy-start | bytes 172036
  306.8 4.3 %copy-start.20 = (pred[259,16]{1,0:T(8,128)(4,1)S(1)}, pred[259,16]{1,0:T(8,128)(4,1)}, u32[]{:S(2)}) copy-start(pred[259,16]{1,0:T(8,128)(4,1)} %copy-done.19) | copy-start | bytes 12436
  306.8 4.3 %copy-start.24 = (f32[256,56]{0,1:T(8,128)S(1)}, f32[256,56]{0,1:T(8,128)}, u32[]{:S(2)}) copy-start(f32[256,56]{0,1:T(8,128)} %copy_bitcast_fusion.2) | copy-start | bytes 172036
  306.8 4.3 %copy-start.37 = (f32[56]{0:T(128)S(1)}, f32[56]{0:T(128)}, u32[]{:S(2)}) copy-start(f32[56]{0:T(128)} %copy-done.36) | copy-start | bytes 676
  306.8 4.6 %copy-start.34 = (f32[56]{0:T(128)S(1)}, f32[56]{0:T(128)}, u32[]{:S(2)}) copy-start(f32[56]{0:T(128)} %param.16) | copy-start | bytes 676
  315.8 2.8 copy-start.21
  318.6 3.4 copy-start.15
  318.6 3.4 copy-start.16
  318.6 3.4 copy-start.17
  321.9 1.7 copy-start.22
  323.8 45.9 %copy-start.13 = (bf16[2,128,56,64]{1,3,2,0:T(8,128)(2,1)S(1)}, bf16[2,128,56,64]{1,3,2,0:T(8,128)(2,1)}, u32[]{:S(2)}) copy-start(bf16[2,128,56,64]{1,3,2,0:T(8,128)(2,1)} %get-tuple-element.118) | copy-start | bytes 5505028
  364.0 29.9 %all-to-all-start.5 = ((f32[256,1,557]{2,1,0:T(1,128)}), f32[256,1,557]{2,1,0:T(1,128)S(1)}, u32[]{:S(2)}, u32[]{:S(2)}) async-start(f32[256,1,557]{2,1,0:T(1,128)} %broadcast_in_dim.121), calls=%async_computation.5 | async-start | bytes 1310720 | tf_op jit(solution)/shard_map/all_to_all | solution.py:161
  376.4 24.4 %copy-start.1 = (bf16[16,3584]{1,0:T(8,128)(2,1)S(1)}, bf16[16,3584]{1,0:T(8,128)(2,1)}, u32[]{:S(2)}) copy-start(bf16[16,3584]{1,0:T(8,128)(2,1)} %param.14) | copy-start | bytes 344068

commit v4 on v3

--- a/solution.py
+++ b/solution.py
@@ -149,17 +149,21 @@
 
 
 def spread_sum(flat, axes):
+    sizes = [lax.axis_size(axis) for axis in axes]
     count = 1
-    for axis in axes:
-        count *= lax.axis_size(axis)
+    for size_of in sizes:
+        count *= size_of
     size = flat.shape[0]
     chunk = -(-size // count)
-    padded = jnp.pad(flat, (0, chunk * count - size)).reshape(count, chunk)
-    gathered = lax.all_to_all(padded, axes, split_axis=0, concat_axis=0, tiled=True)
-    reduced = jnp.sum(gathered, axis=0, keepdims=True)
-    spread = jnp.broadcast_to(reduced, (count, chunk))
-    whole = lax.all_to_all(spread, axes, split_axis=0, concat_axis=0, tiled=True)
-    return whole.reshape(-1)[:size]
+    piece = jnp.pad(flat, (0, chunk * count - size))
+    for axis, parts in zip(axes, sizes):
+        rows = piece.reshape(parts, -1)
+        gathered = lax.all_to_all(rows, axis, split_axis=0, concat_axis=0, tiled=True)
+        piece = jnp.sum(gathered, axis=0)
+    for axis, parts in reversed(list(zip(axes, sizes))):
+        spread = jnp.broadcast_to(piece[None], (parts, piece.shape[0]))
+        piece = lax.all_to_all(spread, axis, split_axis=0, concat_axis=0, tiled=True).reshape(-1)
+    return piece[:size]
 
 
 def local(

time: 409 us -> 411 us (level)
  blocking collectives: 32.5 us -> 39.1 us
  waiting for transfers between devices: 141 us -> 136 us
    all_to_all x1 -> x3, blocking collectives: 32.5 us -> 39.1 us  [the longest x2 32.6 us: spread_sum(): lax.all_to_all(rows, axis, split_axis=0, concat_axis=0, tiled=True)]
    all_to_all x1, waiting for transfers between devices: 11.7 us -> 6.24 us  [spread_sum(): lax.all_to_all(spread, axis, split_axis=0, concat_axis=0, tiled=True)]
where the time goes in v4:
time: 411 us; the launch traced here: 403 us
  waiting for transfers between devices  136 us (33%)
  local copies, waits for them, and re-layouts  83.4 us (20%)
  matrix products  49.8 us (12%)
  other arithmetic  47.1 us (11%)
  starting transfers between devices  46 us (11%)
  blocking collectives  39.1 us (10%)
    all_to_all x1, waiting for transfers between devices, settle_forward(): lax.all_to_all(settled, 'seq', split_axis=1, concat_axis=1, tiled=True)  42.1 us
    all_to_all x2, blocking collectives, spread_sum(): lax.all_to_all(rows, axis, split_axis=0, concat_axis=0, tiled=True)  32.6 us
    all_to_all x1, waiting for transfers between devices, settle_backward(): lax.all_to_all(settled, 'seq', split_axis=1, concat_axis=1, tiled=True)  31.6 us
    all_to_all x1, waiting for transfers between devices, local(): lax.all_to_all(outgoing, 'seq', split_axis=1, concat_axis=1, tiled=True)  30 us
    all_to_all x1, waiting for transfers between devices, local(): lax.all_to_all(back_flat.reshape(heads, parts, span), 'seq', split_axis=1...  25.9 us
    unnamed x81, local copies, waits for them, and re-layouts  21.3 us
    dot_general x3, matrix products, intra(): jnp.einsum('chts,cshp->cthp', mixing, blocked, preferred_element_type=jnp...  17.4 us
    all_to_all x1, starting transfers between devices, local(): lax.all_to_all(outgoing, 'seq', split_axis=1, concat_axis=1, tiled=True)  12.8 us
  transfers between devices with their start and end apart: 6, of which 5 were waited for; matrix products, arithmetic and copies ran while one was open for 18% of the time, Pallas kernels for 0%

profile of v4, /device:TPU:1, one launch (start us, length us, event | category | flops | bytes accessed | tf_op | source)
XLA Modules:
  0.0 403.0 jit_solution(4831211650492860749)
XLA Ops:
  1.4 4.9 %collective-permute-start = (s32[3]{0:T(128)S(1)}, s32[3]{0:T(128)S(1)}, u32[]{:S(2)}, u32[]{:S(2)}) collective-permute-start(s32[3]{0:T(128)S(1)} %add_bitcast_fusion.1), channel_id=1, source_target_pairs={{0,4},{4,8},{8,12},{12,16},{16,20},{20,24},{24,28},{28,32},{32,36}... | collective-permute-start | bytes 44 | tf_op jit(solution)/shard_map/ppermute | solution.py:18
  10.7 3.8 multiply_convert_fusion.1
  16.9 3.5 reshape.375
  20.5 5.8 %copy.348 = bf16[2,128,56,64]{1,3,2,0:T(8,128)(2,1)S(1)} copy(bf16[2,128,56,64]{3,2,1,0:T(8,128)(2,1)} %reshape.375) | data formatting | bytes 3670016 | tf_op jit(solution)/shard_map/jvp()/reshape;jvp()/reshape | solution.py:51
  29.0 2.4 copy.352
  31.4 12.8 %all-to-all-start = ((f32[57,64,128]{2,0,1:T(8,128)}), f32[57,64,128]{2,0,1:T(8,128)}, u32[]{:S(2)}, u32[]{:S(2)}) async-start(f32[57,64,128]{2,0,1:T(8,128)} %copy.352), calls=%async_computation | async-start | bytes 4194304 | tf_op jit(solution)/shard_map/all_to_all | solution.py:212
  44.3 3.8 copy.358
  48.1 4.6 %reshape_squeeze.3 = bf16[2,128,56,64]{1,0,3,2:T(2,128)(2,1)} reshape(bf16[1,256,3584]{1,2,0:T(8,128)(2,1)} %copy.358) | data formatting | bytes 3670016 | tf_op jit(solution)/shard_map/reshape;squeeze | solution.py:216
  52.8 2.5 fusion.124
  55.3 5.4 %reshape.343 = f32[2,128,56,64]{1,0,3,2:T(2,128)} reshape(f32[256,3584]{0,1:T(8,128)} %fusion.124) | data formatting | bytes 7340032 | tf_op jit(solution)/shard_map/reshape | solution.py:215
  60.9 4.4 %fusion.46 = f32[2,128,56,64]{1,3,2,0:T(8,128)} fusion(bf16[2,128,56,64]{1,3,2,0:T(8,128)(2,1)S(1)} %copy.348, f32[2,56,128]{2,1,0:T(8,128)S(1)} %copy.355, f32[2,56,128]{2,1,0:T(8,128)S(1)} %copy.353, f32[2,128,128]{2,1,0:T(8,128)S(1)} %fusion.165, pred[128,128]{1,0:T(8,128)(4,1)S(1)} %iota_compare_fusion.2), kind=kOutput, calls=%fused_computation.73 | convolution fusion | flops 245891072 | bytes 5767168 | tf_op jit(solution)/shard_map/jvp(chts,cshp->cthp)/dot_general | solution.py:91
  65.3 30.0 %all-to-all-done = f32[57,64,128]{2,0,1:T(8,128)} async-done(((f32[57,64,128]{2,0,1:T(8,128)}), f32[57,64,128]{2,0,1:T(8,128)}, u32[]{:S(2)}, u32[]{:S(2)}) %all-to-all-start) | async-done | bytes 1867808 | tf_op jit(solution)/shard_map/all_to_all | solution.py:212
  95.3 3.7 copy.360
  99.0 3.9 copy.361
  104.6 2.7 fusion.50
  107.3 2.3 copy.362
  109.7 6.3 %all-to-all-start.1 = ((f32[56,64,128]{2,0,1:T(8,128)}), f32[56,64,128]{2,0,1:T(8,128)}, u32[]{:S(2)}, u32[]{:S(2)}) async-start(f32[56,64,128]{2,0,1:T(8,128)} %copy.362), calls=%async_computation.1 | async-start | bytes 3670016 | tf_op jit(solution)/shard_map/all_to_all | solution.py:141
  116.2 2.9 slice_add_fusion
  119.1 42.1 %all-to-all-done.1 = f32[56,64,128]{2,0,1:T(8,128)} async-done(((f32[56,64,128]{2,0,1:T(8,128)}), f32[56,64,128]{2,0,1:T(8,128)}, u32[]{:S(2)}, u32[]{:S(2)}) %all-to-all-start.1) | async-done | bytes 1835040 | tf_op jit(solution)/shard_map/all_to_all | solution.py:141
  163.8 4.9 %multiply_reduce_fusion.3 = (f32[2,128]{1,0:T(2,128)S(1)}, f32[2,128,56,64]{1,3,2,0:T(8,128)S(1)}, f32[2,128,56,64]{1,3,2,0:T(8,128)S(1)}) fusion(f32[2,128,56,64]{1,0,3,2:T(2,128)S(1)} %copy-done.11, bf16[2,128,56,64]{1,3,2,0:T(8,128)(2,1)S(1)} %copy.348, f32[56]{0:T(128)S(1)} %copy-done.32, f32[2,128,56,64]{1,3,2,0:T(8,128)} %fusion.46, ...), kind=kOutput, calls=%fused_computation.61 | convolution fusion | flops 248643328 | bytes 20309664 | tf_op jit(solution)/shard_map/jvp(ctn,chpn->cthp)/dot_general | solution.py:113
  172.0 5.6 %fusion.47 = (bf16[2,56,8,8,128]{4,3,2,1,0:T(8,128)(2,1)}, f32[2,128,56,64]{1,3,2,0:T(8,128)S(1)}, f32[2,128,56,64]{1,3,2,0:T(8,128)}, bf16[2,128,56,64]{1,3,2,0:T(8,128)(2,1)}) fusion(f32[56]{0:T(128)S(1)} %copy-done.32, f32[2,128,56,64]{1,0,3,2:T(2,128)S(1)} %copy-done.11, f32[2,128,56,64]{1,3,2,0:T(8,128)S(1)} %get-tuple-element.130, ...), kind=kLoop, calls=%fused_computation.75 | loop fusion | flops 25690112 | bytes 29434080
  177.6 2.5 multiply_reduce_fusion
  180.1 2.3 copy.368
  182.4 6.5 %all-to-all-start.2 = ((f32[56,64,128]{2,0,1:T(8,128)}), f32[56,64,128]{2,0,1:T(8,128)}, u32[]{:S(2)}, u32[]{:S(2)}) async-start(f32[56,64,128]{2,0,1:T(8,128)} %copy.368), calls=%async_computation.2 | async-start | bytes 3670016 | tf_op jit(solution)/shard_map/all_to_all | solution.py:239
  189.0 8.5 %fusion.10 = (f32[2,56,128]{2,1,0:T(8,128)S(1)}, f32[2,56,128]{2,1,0:T(8,128)S(1)}, f32[2,56,128]{2,1,0:T(8,128)S(1)}, bf16[2,128,128]{2,1,0:T(8,128)(2,1)S(1)}) fusion(f32[2,56,128]{2,1,0:T(8,128)S(1)} %copy.355, f32[2,56,128]{2,1,0:T(8,128)S(1)} %copy.353, f32[2,128,128]{2,1,0:T(8,128)S(1)} %fusion.165, pred[128,128]{1,0:T(8,128)(4,1)S(1)} %iota_compare_fusion.2, ...), kind=kOutput, calls=%fused_computation.19 | convolution fusion | flops 264165376 | bytes 6004736 | tf_op jit(solution)/shard_map/transpose(jvp(chts,cshp->cthp))/dot_general | solution.py:91
  200.5 4.5 %convert_bitcast_fusion = bf16[2,56,8,8,128]{4,3,2,1,0:T(8,128)(2,1)S(1)} fusion(f32[2,56,128]{2,1,0:T(8,128)S(1)} %copy.355, f32[2,56,128]{2,1,0:T(8,128)S(1)} %copy.353, f32[2,128,128]{2,1,0:T(8,128)S(1)} %fusion.165, pred[128,128]{1,0:T(8,128)(4,1)S(1)} %iota_compare_fusion.2, f32[2,128,56,64]{1,3,2,0:T(8,128)} %copy-done.2), kind=kOutput, calls=%fused_computation.96 | convolution fusion | flops 245891072 | bytes 5767168 | tf_op jit(solution)/shard_map/transpose(jvp(chts,cshp->cthp))/dot_general | solution.py:91
  208.3 25.9 %all-to-all-done.2 = f32[56,64,128]{2,0,1:T(8,128)} async-done(((f32[56,64,128]{2,0,1:T(8,128)}), f32[56,64,128]{2,0,1:T(8,128)}, u32[]{:S(2)}, u32[]{:S(2)}) %all-to-all-start.2) | async-done | bytes 1835040 | tf_op jit(solution)/shard_map/all_to_all | solution.py:239
  234.2 2.9 fusion.53
  237.1 2.3 copy.376
  239.4 6.5 %all-to-all-start.3 = ((f32[56,64,128]{2,0,1:T(8,128)}), f32[56,64,128]{2,0,1:T(8,128)S(1)}, u32[]{:S(2)}, u32[]{:S(2)}) async-start(f32[56,64,128]{2,0,1:T(8,128)} %copy.376), calls=%async_computation.3 | async-start | bytes 3670016 | tf_op jit(solution)/shard_map/all_to_all | solution.py:148
  246.7 4.1 %convert_element_type.92 = f32[2,56,64,128]{3,2,1,0:T(8,128)} convert(bf16[2,56,64,128]{3,2,1,0:T(8,128)(2,1)} %get-tuple-element.159) | non-fusion elementwise | flops 917504 | bytes 5505024 | tf_op jit(solution)/shard_map/transpose(jvp())/convert_element_type | solution.py:114
  250.9 3.3 copy.383
  255.4 4.2 %fusion.81 = bf16[2,128,128]{2,1,0:T(8,128)(2,1)S(1)} fusion(f32[2,128,56,64]{1,3,2,0:T(8,128)} %copy-done.2, f32[2,128,56]{1,2,0:T(8,128)S(1)} %copy.359, f32[1,56,64,128]{3,2,1,0:T(8,128)} %slice_add_fusion, f32[56,64,128]{2,1,0:T(8,128)} %copy-done.6, f32[2,56]{1,0:T(2,128)S(1)} %subtract_exponential_fusion.1), kind=kOutput, calls=%fused_computation.111 | convolution fusion | flops 238583808 | bytes 7463360 | tf_op jit(solution)/shard_map/transpose(jvp(ctn,chpn->cthp))/dot_general | solution.py:113
  259.6 31.6 %all-to-all-done.3 = f32[56,64,128]{2,0,1:T(8,128)S(1)} async-done(((f32[56,64,128]{2,0,1:T(8,128)}), f32[56,64,128]{2,0,1:T(8,128)S(1)}, u32[]{:S(2)}, u32[]{:S(2)}) %all-to-all-start.3) | async-done | bytes 1835040 | tf_op jit(solution)/shard_map/all_to_all | solution.py:148
  291.2 2.5 fusion.121
  294.4 4.6 %fusion.27 = (f32[56]{0:T(128)S(1)}, f32[2,128,56]{1,2,0:T(8,128)S(1)}, f32[2,128,56]{1,2,0:T(8,128)S(1)}, bf16[2,56,8,8,128]{4,3,2,1,0:T(8,128)(2,1)}) fusion(f32[2,128,56,64]{1,3,2,0:T(8,128)S(1)} %copy-done.3, bf16[2,128,56,64]{1,3,2,0:T(8,128)(2,1)S(1)} %copy-done.8, f32[2,128,56,64]{1,3,2,0:T(8,128)} %copy-done.12, f32[2,128,56]{1,2,0:T(8,128)S(1)} %copy.351, ...), kind=kOutput, calls=%fused_computation.47 | convolution fusion | flops 247697344 | bytes 13082848 | tf_op jit(solution)/shard_map/transpose(jvp(cshp,csn->chpn))/dot_general | solution.py:52
  307.5 3.1 multiply_reduce_fusion.5
  311.4 4.3 %bitcast_add_fusion = bf16[256,56,64]{0,2,1:T(8,128)(2,1)} fusion(bf16[2,56,8,8,128]{4,3,2,1,0:T(8,128)(2,1)} %get-tuple-element.139, bf16[256,56,64]{0,2,1:T(8,128)(2,1)} %bitcast.185, bf16[2,56,8,8,128]{4,3,2,1,0:T(8,128)(2,1)} %get-tuple-element.127), kind=kLoop, calls=%fused_computation.77 | loop fusion | flops 1835008 | bytes 7340032 | tf_op jit(solution)/shard_map/add | solution.py:250
  315.7 2.8 copy.381
  318.6 3.3 fusion.150
  323.8 3.0 concatenate.29
  327.7 24.5 %all_to_all.50 = f32[64,1,2228]{2,1,0:T(1,128)S(1)} all-to-all(f32[64,1,2228]{2,1,0:T(1,128)S(1)} %all_to_all.36), channel_id=1, replica_groups=mesh['seq'=64,'batch'=4] {'seq'}, dimensions={0} | all-to-all | bytes 1140736 | tf_op jit(solution)/shard_map/all_to_all | solution.py:161
  352.6 8.2 %all_to_all.51 = f32[4,1,557]{2,1,0:T(1,128)S(1)} all-to-all(f32[4,1,557]{2,1,0:T(1,128)S(1)} %all_to_all.38), channel_id=1, replica_groups=mesh['seq'=64,'batch'=4] {'batch'}, dimensions={0} | all-to-all | bytes 17824 | tf_op jit(solution)/shard_map/all_to_all | solution.py:161
  360.8 6.5 %all_to_all.52 = f32[4,1,557]{2,1,0:T(1,128)S(1)} all-to-all(f32[4,1,557]{2,1,0:T(1,128)S(1)} %broadcast_in_dim.128), channel_id=1, replica_groups=mesh['seq'=64,'batch'=4] {'batch'}, dimensions={0} | all-to-all | bytes 17824 | tf_op jit(solution)/shard_map/all_to_all | solution.py:165
  368.6 8.9 %all-to-all-start.7 = ((f32[64,1,2228]{2,1,0:T(1,128)}), f32[64,1,2228]{2,1,0:T(1,128)S(1)}, u32[]{:S(2)}, u32[]{:S(2)}) async-start(f32[64,1,2228]{2,1,0:T(1,128)} %broadcast_in_dim.130), calls=%async_computation.7 | async-start | bytes 1179648 | tf_op jit(solution)/shard_map/all_to_all | solution.py:165
  377.5 6.7 %copy.405 = bf16[2,128,56,64]{3,2,1,0:T(8,128)(2,1)} copy(bf16[2,128,56,64]{1,3,2,0:T(8,128)(2,1)S(1)} %copy-done.13) | data formatting | bytes 3670016
  384.2 5.8 %reshape.374 = bf16[1,256,3584]{2,1,0:T(8,128)(2,1)} reshape(bf16[2,128,56,64]{3,2,1,0:T(8,128)(2,1)} %copy.405) | data formatting | bytes 3670016
  389.9 6.2 %all-to-all-done.7 = f32[64,1,2228]{2,1,0:T(1,128)S(1)} async-done(((f32[64,1,2228]{2,1,0:T(1,128)}), f32[64,1,2228]{2,1,0:T(1,128)S(1)}, u32[]{:S(2)}, u32[]{:S(2)}) %all-to-all-start.7) | async-done | bytes 570400 | tf_op jit(solution)/shard_map/all_to_all | solution.py:165
  (185 shorter events, 47.5 us)
Async XLA Ops:
  0.6 52.2 %copy-start = (bf16[16,3584]{1,0:T(8,128)(2,1)S(1)}, bf16[16,3584]{1,0:T(8,128)(2,1)}, u32[]{:S(2)}) copy-start(bf16[16,3584]{1,0:T(8,128)(2,1)} %param.14) | copy-start | bytes 344068
  1.4 6.7 %collective-permute-start = (s32[3]{0:T(128)S(1)}, s32[3]{0:T(128)S(1)}, u32[]{:S(2)}, u32[]{:S(2)}) collective-permute-start(s32[3]{0:T(128)S(1)} %add_bitcast_fusion.1), channel_id=1, source_target_pairs={{0,4},{4,8},{8,12},{12,16},{16,20},{20,24},{24,28},{28,32},{32,36}... | collective-permute-start | bytes 44 | tf_op jit(solution)/shard_map/ppermute | solution.py:18
  7.0 7.7 %copy-start.36 = (f32[56]{0:T(128)}, f32[56]{0:T(128)S(1)}, u32[]{:S(2)}) copy-start(f32[56]{0:T(128)S(1)} %exponential_negate_fusion) | copy-start | bytes 676
  9.1 245.1 %copy-start.19 = (pred[259,16]{1,0:T(8,128)(4,1)}, pred[259,16]{1,0:T(8,128)(4,1)S(1)}, u32[]{:S(2)}) copy-start(pred[259,16]{1,0:T(8,128)(4,1)S(1)} %get-tuple-element.156) | copy-start | bytes 12436
  9.1 1.7 copy-start.26
  14.6 0.7 copy-start.33
  16.2 10.3 %copy-start.35 = (f32[56]{0:T(128)}, f32[56]{0:T(128)S(1)}, u32[]{:S(2)}) copy-start(f32[56]{0:T(128)S(1)} %get-tuple-element.133) | copy-start | bytes 676
  26.3 162.7 %copy-start.7 = (bf16[2,128,56,64]{1,3,2,0:T(8,128)(2,1)}, bf16[2,128,56,64]{1,3,2,0:T(8,128)(2,1)S(1)}, u32[]{:S(2)}) copy-start(bf16[2,128,56,64]{1,3,2,0:T(8,128)(2,1)S(1)} %copy.348) | copy-start | bytes 5505028
  26.4 1.3 copy-start.28
  26.5 0.9 copy-start.30
  27.2 1.8 copy-start.4
  31.4 63.9 %all-to-all-start = ((f32[57,64,128]{2,0,1:T(8,128)}), f32[57,64,128]{2,0,1:T(8,128)}, u32[]{:S(2)}, u32[]{:S(2)}) async-start(f32[57,64,128]{2,0,1:T(8,128)} %copy.352), calls=%async_computation | async-start | bytes 4194304 | tf_op jit(solution)/shard_map/all_to_all | solution.py:212
  107.3 8.7 %copy-start.27 = (f32[3584]{0:T(1024)S(1)}, f32[3584]{0:T(1024)}, u32[]{:S(2)}) copy-start(f32[3584]{0:T(1024)} %param.20) | copy-start | bytes 43012
  109.7 51.5 %all-to-all-start.1 = ((f32[56,64,128]{2,0,1:T(8,128)}), f32[56,64,128]{2,0,1:T(8,128)}, u32[]{:S(2)}, u32[]{:S(2)}) async-start(f32[56,64,128]{2,0,1:T(8,128)} %copy.362), calls=%async_computation.1 | async-start | bytes 3670016 | tf_op jit(solution)/shard_map/all_to_all | solution.py:141
  116.2 47.0 %copy-start.32 = (f32[56]{0:T(128)S(1)}, f32[56]{0:T(128)}, u32[]{:S(2)}) copy-start(f32[56]{0:T(128)} %param.19) | copy-start | bytes 676
  161.2 2.6 copy-start.11
  163.2 14.5 %copy-start.6 = (f32[56,64,128]{2,1,0:T(8,128)}, f32[56,64,128]{2,1,0:T(8,128)S(1)}, u32[]{:S(2)}) copy-start(f32[56,64,128]{2,1,0:T(8,128)S(1)} %copy.363) | copy-start | bytes 5505028
  163.8 4.9 %copy-start.9 = (bf16[2,128,56,64]{1,0,3,2:T(2,128)(2,1)S(1)}, bf16[2,128,56,64]{1,0,3,2:T(2,128)(2,1)}, u32[]{:S(2)}) copy-start(bf16[2,128,56,64]{1,0,3,2:T(2,128)(2,1)} %reshape_squeeze.3) | copy-start | bytes 5505028
  168.7 9.0 %copy-start.12 = (f32[2,128,56,64]{1,3,2,0:T(8,128)}, f32[2,128,56,64]{1,3,2,0:T(8,128)S(1)}, u32[]{:S(2)}) copy-start(f32[2,128,56,64]{1,3,2,0:T(8,128)S(1)} %get-tuple-element.158) | copy-start | bytes 11010052
  168.7 3.4 copy-start.14
  177.6 2.5 copy-start.2
  182.4 51.7 %all-to-all-start.2 = ((f32[56,64,128]{2,0,1:T(8,128)}), f32[56,64,128]{2,0,1:T(8,128)}, u32[]{:S(2)}, u32[]{:S(2)}) async-start(f32[56,64,128]{2,0,1:T(8,128)} %copy.368), calls=%async_computation.2 | async-start | bytes 3670016 | tf_op jit(solution)/shard_map/all_to_all | solution.py:239
  237.1 8.8 %copy-start.18 = (bf16[16,3840]{1,0:T(8,128)(2,1)S(1)}, bf16[16,3840]{1,0:T(8,128)(2,1)}, u32[]{:S(2)}) copy-start(bf16[16,3840]{1,0:T(8,128)(2,1)} %param.13) | copy-start | bytes 368644
  239.4 51.8 %all-to-all-start.3 = ((f32[56,64,128]{2,0,1:T(8,128)}), f32[56,64,128]{2,0,1:T(8,128)S(1)}, u32[]{:S(2)}, u32[]{:S(2)}) async-start(f32[56,64,128]{2,0,1:T(8,128)} %copy.376), calls=%async_computation.3 | async-start | bytes 3670016 | tf_op jit(solution)/shard_map/all_to_all | solution.py:148
  245.9 4.9 %copy-start.10 = (f32[2,128,56,64]{1,3,2,0:T(8,128)S(1)}, f32[2,128,56,64]{1,3,2,0:T(8,128)}, u32[]{:S(2)}) copy-start(f32[2,128,56,64]{1,3,2,0:T(8,128)} %get-tuple-element.135) | copy-start | bytes 11010052
  291.2 2.6 copy-start.3
  291.2 3.2 copy-start.8
  304.7 2.8 copy-start.5
  306.7 3.9 copy-start.31
  306.7 3.9 copy-start.29
  306.7 4.2 %copy-start.23 = (f32[256,56]{0,1:T(8,128)S(1)}, f32[256,56]{0,1:T(8,128)}, u32[]{:S(2)}) copy-start(f32[256,56]{0,1:T(8,128)} %copy.406) | copy-start | bytes 172036
  306.7 4.2 %copy-start.25 = (f32[256,56]{0,1:T(8,128)S(1)}, f32[256,56]{0,1:T(8,128)}, u32[]{:S(2)}) copy-start(f32[256,56]{0,1:T(8,128)} %get-tuple-element.157) | copy-start | bytes 172036
  306.8 4.3 %copy-start.20 = (pred[259,16]{1,0:T(8,128)(4,1)S(1)}, pred[259,16]{1,0:T(8,128)(4,1)}, u32[]{:S(2)}) copy-start(pred[259,16]{1,0:T(8,128)(4,1)} %copy-done.19) | copy-start | bytes 12436
  306.8 4.3 %copy-start.24 = (f32[256,56]{0,1:T(8,128)S(1)}, f32[256,56]{0,1:T(8,128)}, u32[]{:S(2)}) copy-start(f32[256,56]{0,1:T(8,128)} %copy_bitcast_fusion.2) | copy-start | bytes 172036
  306.8 4.3 %copy-start.37 = (f32[56]{0:T(128)S(1)}, f32[56]{0:T(128)}, u32[]{:S(2)}) copy-start(f32[56]{0:T(128)} %copy-done.36) | copy-start | bytes 676
  306.8 4.6 %copy-start.34 = (f32[56]{0:T(128)S(1)}, f32[56]{0:T(128)}, u32[]{:S(2)}) copy-start(f32[56]{0:T(128)} %param.16) | copy-start | bytes 676
  315.7 2.8 copy-start.21
  318.6 3.4 copy-start.15
  318.6 3.4 copy-start.16
  318.6 3.4 copy-start.17
  321.9 1.7 copy-start.22
  323.8 53.7 %copy-start.13 = (bf16[2,128,56,64]{1,3,2,0:T(8,128)(2,1)S(1)}, bf16[2,128,56,64]{1,3,2,0:T(8,128)(2,1)}, u32[]{:S(2)}) copy-start(bf16[2,128,56,64]{1,3,2,0:T(8,128)(2,1)} %get-tuple-element.136) | copy-start | bytes 5505028
  368.6 27.6 %all-to-all-start.7 = ((f32[64,1,2228]{2,1,0:T(1,128)}), f32[64,1,2228]{2,1,0:T(1,128)S(1)}, u32[]{:S(2)}, u32[]{:S(2)}) async-start(f32[64,1,2228]{2,1,0:T(1,128)} %broadcast_in_dim.130), calls=%async_computation.7 | async-start | bytes 1179648 | tf_op jit(solution)/shard_map/all_to_all | solution.py:165
  377.5 25.3 %copy-start.1 = (bf16[16,3584]{1,0:T(8,128)(2,1)S(1)}, bf16[16,3584]{1,0:T(8,128)(2,1)}, u32[]{:S(2)}) copy-start(bf16[16,3584]{1,0:T(8,128)(2,1)} %param.14) | copy-start | bytes 344068

commit v5 on v3

--- a/solution.py
+++ b/solution.py
@@ -46,15 +46,22 @@
 def group_states(values, write_keys, steps, log_decay):
     tokens, heads, head = values.shape
     count = tokens // BLOCK
+    inner = heads * head
     cum = jnp.cumsum(log_decay.reshape(count, BLOCK, heads), axis=1)
     factor = jnp.exp(cum[:, -1:, :] - cum) * steps.reshape(count, BLOCK, heads)
-    weighted = (values.reshape(count, BLOCK, heads, head) * factor[..., None]).astype(jnp.bfloat16)
-    return jnp.einsum(
-        "cshp,csn->chpn",
+    expand = (
+        lax.broadcasted_iota(jnp.int32, (heads, inner), 1) // head
+        == lax.broadcasted_iota(jnp.int32, (heads, inner), 0)
+    ).astype(jnp.float32)
+    wide = jnp.einsum("csh,hk->csk", factor, expand, precision=HIGH)
+    weighted = (values.reshape(count, BLOCK, inner) * wide).astype(jnp.bfloat16)
+    pieces = jnp.einsum(
+        "csk,csn->ckn",
         weighted,
         write_keys.reshape(count, BLOCK, -1),
         preferred_element_type=jnp.float32,
     )
+    return pieces.reshape(count, heads, head, -1)
 
 
 def local_states(pieces, log_decay):

time: 409 us -> 416 us (1.017)
  waiting for transfers between devices: 141 us -> 126 us
  local copies, waits for them, and re-layouts: 85.4 us -> 99 us
  other arithmetic: 47.3 us -> 52.2 us
    all_to_all x1, waiting for transfers between devices: 30 us -> 18.6 us  [local(): lax.all_to_all(outgoing, 'seq', split_axis=1, concat_axis=1, tiled=True)]
    reshape x1 -> x3, local copies, waits for them, and re-layouts: 1.58 us -> 11.5 us  [intra(): blocked = values.reshape(count, BLOCK, heads, head)]
    reduce_sum x1 -> x2, other arithmetic: 0.08 us -> 9.02 us  [the longest x1 8.84 us: mixer_output(): mixed = within + across + skip_gain[None, None, :, None] * blocked]
    convert_element_type x0 -> x1, local copies, waits for them, and re-layouts: none -> 5.66 us  [group_states(): weighted = (values.reshape(count, BLOCK, inner) * wide).astype(jnp.bfloat16)]
    unnamed x1 -> x0, other arithmetic: 5.6 us -> none
    reshape x2 -> x1, local copies, waits for them, and re-layouts: 9.32 us -> 5.28 us  [group_states(): weighted = (values.reshape(count, BLOCK, inner) * wide).astype(jnp.bfloat16)]
    unnamed x81 -> x117, local copies, waits for them, and re-layouts: 21.3 us -> 19.1 us
  transfers between devices with their start and end apart: 6 -> 6, of which waited for: 5 -> 5; matrix products, arithmetic and copies ran while one was open for 18% -> 21% of each run, Pallas kernels for 0% -> 0%
where the time goes in v5:
time: 416 us; the launch traced here: 408 us
  waiting for transfers between devices  126 us (30%)
  local copies, waits for them, and re-layouts  99 us (24%)
  matrix products  53.3 us (13%)
  other arithmetic  52.2 us (13%)
  starting transfers between devices  42.9 us (10%)
  blocking collectives  32.5 us (8%)
    all_to_all x1, waiting for transfers between devices, settle_forward(): lax.all_to_all(settled, 'seq', split_axis=1, concat_axis=1, tiled=True)  42 us
    all_to_all x1, blocking collectives, spread_sum(): lax.all_to_all(padded, axes, split_axis=0, concat_axis=0, tiled=True)  32.5 us
    all_to_all x1, waiting for transfers between devices, settle_backward(): lax.all_to_all(settled, 'seq', split_axis=1, concat_axis=1, tiled=True)  28.7 us
    all_to_all x1, waiting for transfers between devices, local(): lax.all_to_all(back_flat.reshape(heads, parts, span), 'seq', split_axis=1...  25.3 us
    unnamed x117, local copies, waits for them, and re-layouts  19.1 us
    dot_general x3, matrix products, intra(): jnp.einsum('chts,cshp->cthp', mixing, blocked, preferred_element_type=jnp...  18.8 us
    all_to_all x1, waiting for transfers between devices, local(): lax.all_to_all(outgoing, 'seq', split_axis=1, concat_axis=1, tiled=True)  18.6 us
    all_to_all x1, starting transfers between devices, local(): lax.all_to_all(outgoing, 'seq', split_axis=1, concat_axis=1, tiled=True)  12.9 us
  transfers between devices with their start and end apart: 6, of which 5 were waited for; matrix products, arithmetic and copies ran while one was open for 21% of the time, Pallas kernels for 0%

profile of v5, /device:TPU:1, one launch (start us, length us, event | category | flops | bytes accessed | tf_op | source)
XLA Modules:
  0.0 408.2 jit_solution(7811511238726940429)
XLA Ops:
  1.4 4.9 %collective-permute-start = (s32[3]{0:T(128)S(1)}, s32[3]{0:T(128)S(1)}, u32[]{:S(2)}, u32[]{:S(2)}) collective-permute-start(s32[3]{0:T(128)S(1)} %add_bitcast_fusion.1), channel_id=1, source_target_pairs={{0,4},{4,8},{8,12},{12,16},{16,20},{20,24},{24,28},{28,32},{32,36}... | collective-permute-start | bytes 44 | tf_op jit(solution)/shard_map/ppermute | solution.py:18
  12.4 3.8 multiply_convert_fusion.1
  22.4 2.3 multiply_add_fusion
  24.9 2.4 copy.248
  27.3 12.9 %all-to-all-start = ((f32[57,64,128]{2,0,1:T(8,128)}), f32[57,64,128]{2,0,1:T(8,128)}, u32[]{:S(2)}, u32[]{:S(2)}) async-start(f32[57,64,128]{2,0,1:T(8,128)} %copy.248), calls=%async_computation | async-start | bytes 4194304 | tf_op jit(solution)/shard_map/all_to_all | solution.py:215
  40.2 3.8 copy.255
  44.0 4.6 %reshape_squeeze.3 = bf16[2,128,56,64]{1,0,3,2:T(2,128)(2,1)} reshape(bf16[1,256,3584]{1,2,0:T(8,128)(2,1)} %copy.255) | data formatting | bytes 3670016 | tf_op jit(solution)/shard_map/reshape;squeeze | solution.py:219
  48.6 3.5 reshape.369
  52.1 6.4 %copy.253 = bf16[2,128,56,64]{1,3,2,0:T(8,128)(2,1)} copy(bf16[2,128,56,64]{3,2,1,0:T(8,128)(2,1)} %reshape.369) | data formatting | bytes 3670016 | tf_op jit(solution)/shard_map/jvp()/reshape;jvp()/reshape | solution.py:97
  58.7 2.5 fusion.123
  61.2 5.5 %reshape.336 = f32[2,128,56,64]{1,0,3,2:T(2,128)} reshape(f32[256,3584]{0,1:T(8,128)} %fusion.123) | data formatting | bytes 7340032 | tf_op jit(solution)/shard_map/reshape | solution.py:218
  66.9 5.7 %fusion.45 = f32[2,128,56,64]{1,3,2,0:T(8,128)} fusion(bf16[2,128,56,64]{1,3,2,0:T(8,128)(2,1)} %copy.253, f32[2,56,128]{2,1,0:T(8,128)S(1)} %copy.252, f32[2,56,128]{2,1,0:T(8,128)S(1)} %copy.250, f32[2,128,128]{2,1,0:T(8,128)S(1)} %fusion.176, pred[128,128]{1,0:T(8,128)(4,1)S(1)} %iota_compare_fusion.3), kind=kOutput, calls=%fused_computation.73 | convolution fusion | flops 245891072 | bytes 5767168 | tf_op jit(solution)/shard_map/jvp(chts,cshp->cthp)/dot_general | solution.py:98
  72.6 18.6 %all-to-all-done = f32[57,64,128]{2,0,1:T(8,128)} async-done(((f32[57,64,128]{2,0,1:T(8,128)}), f32[57,64,128]{2,0,1:T(8,128)}, u32[]{:S(2)}, u32[]{:S(2)}) %all-to-all-start) | async-done | bytes 1867808 | tf_op jit(solution)/shard_map/all_to_all | solution.py:215
  91.2 3.7 copy.257
  95.0 3.9 copy.258
  100.6 2.7 fusion.49
  105.6 6.6 %all-to-all-start.1 = ((f32[56,64,128]{2,0,1:T(8,128)}), f32[56,64,128]{2,0,1:T(8,128)}, u32[]{:S(2)}, u32[]{:S(2)}) async-start(f32[56,64,128]{2,0,1:T(8,128)} %copy.259), calls=%async_computation.1 | async-start | bytes 3670016 | tf_op jit(solution)/shard_map/all_to_all | solution.py:148
  112.5 2.9 broadcast_add_fusion
  115.4 42.0 %all-to-all-done.1 = f32[56,64,128]{2,0,1:T(8,128)} async-done(((f32[56,64,128]{2,0,1:T(8,128)}), f32[56,64,128]{2,0,1:T(8,128)}, u32[]{:S(2)}, u32[]{:S(2)}) %all-to-all-start.1) | async-done | bytes 1835040 | tf_op jit(solution)/shard_map/all_to_all | solution.py:148
  160.0 5.4 %multiply_reduce_fusion.3 = (f32[2,128]{1,0:T(2,128)S(1)}, f32[2,128,56,64]{1,3,2,0:T(8,128)S(1)}, f32[2,128,56,64]{1,3,2,0:T(8,128)S(1)}) fusion(f32[2,128,56,64]{1,0,3,2:T(2,128)S(1)} %copy-done.9, bf16[2,128,56,64]{1,3,2,0:T(8,128)(2,1)} %copy.253, f32[56]{0:T(128)S(1)} %copy-done.42, f32[2,128,56,64]{1,3,2,0:T(8,128)} %fusion.45, ...), kind=kOutput, calls=%fused_computation.62 | convolution fusion | flops 248643328 | bytes 20309664 | tf_op jit(solution)/shard_map/jvp(ctn,chpn->cthp)/dot_general | solution.py:120
  165.5 2.3 fusion.23
  168.0 8.8 %fusion.22 = (f32[56]{0:T(128)}, f32[2,128,56]{1,2,0:T(8,128)S(1)}, f32[2,128,56,64]{1,3,2,0:T(8,128)S(1)}, f32[2,128,56,64]{1,3,2,0:T(8,128)}, bf16[2,128,56,64]{1,3,2,0:T(8,128)(2,1)}) fusion(bf16[2,128,56,64]{1,3,2,0:T(8,128)(2,1)S(1)} %copy-done.12, f32[2,128,56,64]{1,3,2,0:T(8,128)S(1)} %get-tuple-element.135, f32[2,128,56,64]{1,0,3,2:T(2,128)S(1)} %copy-done.9, ...), kind=kLoop, calls=%fused_computation.42 | loop fusion | flops 27510728 | bytes 27656640 | tf_op jit(solution)/shard_map/transpose(jvp())/reduce_sum | solution.py:123
  176.9 2.6 multiply_reduce_fusion
  179.5 2.3 copy.266
  181.8 6.4 %all-to-all-start.2 = ((f32[56,64,128]{2,0,1:T(8,128)}), f32[56,64,128]{2,0,1:T(8,128)}, u32[]{:S(2)}, u32[]{:S(2)}) async-start(f32[56,64,128]{2,0,1:T(8,128)} %copy.266), calls=%async_computation.2 | async-start | bytes 3670016 | tf_op jit(solution)/shard_map/all_to_all | solution.py:242
  188.2 8.5 %fusion.10 = (f32[2,56,128]{2,1,0:T(8,128)S(1)}, f32[2,56,128]{2,1,0:T(8,128)S(1)}, f32[2,56,128]{2,1,0:T(8,128)S(1)}, bf16[2,128,128]{2,1,0:T(8,128)(2,1)S(1)}) fusion(f32[2,56,128]{2,1,0:T(8,128)S(1)} %copy.252, f32[2,56,128]{2,1,0:T(8,128)S(1)} %copy.250, f32[2,128,128]{2,1,0:T(8,128)S(1)} %fusion.176, pred[128,128]{1,0:T(8,128)(4,1)S(1)} %iota_compare_fusion.3, ...), kind=kOutput, calls=%fused_computation.15 | convolution fusion | flops 264165376 | bytes 6004736 | tf_op jit(solution)/shard_map/transpose(jvp(chts,cshp->cthp))/dot_general | solution.py:98
  199.8 4.5 %convert_bitcast_fusion = bf16[2,56,8,8,128]{4,3,2,1,0:T(8,128)(2,1)S(1)} fusion(f32[2,56,128]{2,1,0:T(8,128)S(1)} %copy.252, f32[2,56,128]{2,1,0:T(8,128)S(1)} %copy.250, f32[2,128,128]{2,1,0:T(8,128)S(1)} %fusion.176, pred[128,128]{1,0:T(8,128)(4,1)S(1)} %iota_compare_fusion.3, f32[2,128,56,64]{1,3,2,0:T(8,128)} %copy-done.4), kind=kOutput, calls=%fused_computation.92 | convolution fusion | flops 245891072 | bytes 5767168 | tf_op jit(solution)/shard_map/transpose(jvp(chts,cshp->cthp))/dot_general | solution.py:98
  208.1 25.3 %all-to-all-done.2 = f32[56,64,128]{2,0,1:T(8,128)} async-done(((f32[56,64,128]{2,0,1:T(8,128)}), f32[56,64,128]{2,0,1:T(8,128)}, u32[]{:S(2)}, u32[]{:S(2)}) %all-to-all-start.2) | async-done | bytes 1835040 | tf_op jit(solution)/shard_map/all_to_all | solution.py:242
  233.4 2.9 fusion.51
  236.4 2.3 copy.274
  238.7 6.3 %all-to-all-start.3 = ((f32[56,64,128]{2,0,1:T(8,128)}), f32[56,64,128]{2,0,1:T(8,128)}, u32[]{:S(2)}, u32[]{:S(2)}) async-start(f32[56,64,128]{2,0,1:T(8,128)} %copy.274), calls=%async_computation.3 | async-start | bytes 3670016 | tf_op jit(solution)/shard_map/all_to_all | solution.py:155
  248.2 3.8 convert_element_type.100
  252.0 3.3 copy.281
  257.1 4.2 %fusion.72 = bf16[2,128,128]{2,1,0:T(8,128)(2,1)S(1)} fusion(f32[2,128,56,64]{1,3,2,0:T(8,128)} %copy-done.4, f32[2,128,56]{1,2,0:T(8,128)S(1)} %copy.256, f32[1,56,64,128]{3,2,1,0:T(8,128)} %broadcast_add_fusion, f32[56,64,128]{2,1,0:T(8,128)} %copy-done.6, f32[2,56]{1,0:T(2,128)S(1)} %copy-done.36), kind=kOutput, calls=%fused_computation.103 | convolution fusion | flops 238583808 | bytes 7463360 | tf_op jit(solution)/shard_map/transpose(jvp(ctn,chpn->cthp))/dot_general | solution.py:120
  261.4 28.7 %all-to-all-done.3 = f32[56,64,128]{2,0,1:T(8,128)} async-done(((f32[56,64,128]{2,0,1:T(8,128)}), f32[56,64,128]{2,0,1:T(8,128)}, u32[]{:S(2)}, u32[]{:S(2)}) %all-to-all-start.3) | async-done | bytes 1835040 | tf_op jit(solution)/shard_map/all_to_all | solution.py:155
  292.1 4.2 %multiply_reduce_fusion.5 = (f32[56]{0:T(128)}, bf16[56,64,128]{2,1,0:T(8,128)(2,1)S(1)}, f32[56]{0:T(128)}) fusion(f32[56,64,128]{2,0,1:T(8,128)} %all-to-all-done.3, f32[56]{0:T(128)S(1)} %copy-done.41, f32[2,56,64,128]{3,2,1,0:T(8,128)} %convert_element_type.100, f32[56,64,128]{2,1,0:T(8,128)S(1)} %bitcast.190, f32[56]{0:T(128)S(1)} %copy-done.39), kind=kLoop, calls=%fused_computation.86 | loop fusion | flops 3669904 | bytes 6423424 | tf_op jit(solution)/shard_map/transpose(jvp())/eval_jaxpr/reduce_sum | solution.py:73
  304.1 2.4 multiply_reduce_fusion.6
  307.3 5.7 %copy.278 = bf16[2,128,3584]{1,0,2:T(2,128)(2,1)} copy(bf16[2,128,3584]{2,1,0:T(8,128)(2,1)} %get-tuple-element.137) | data formatting | bytes 3670016 | tf_op jit(solution)/shard_map/transpose(jvp())/convert_element_type | solution.py:57
  313.0 5.3 %reshape.346 = bf16[256,56,64]{0,2,1:T(8,128)(2,1)} reshape(bf16[2,128,3584]{1,0,2:T(2,128)(2,1)} %copy.278) | data formatting | bytes 3670016 | tf_op jit(solution)/shard_map/transpose(jvp())/reshape | solution.py:57
  318.2 5.1 %fusion.47 = bf16[256,56,64]{0,2,1:T(8,128)(2,1)} fusion(bf16[256,56,64]{0,2,1:T(8,128)(2,1)} %reshape.346, bf16[256,56,64]{0,2,1:T(8,128)(2,1)S(1)} %bitcast.196, f32[2,128,56,64]{1,3,2,0:T(8,128)} %copy-done.4, f32[56]{0:T(128)S(1)} %copy-done.43), kind=kLoop, calls=%fused_computation.77 | loop fusion | flops 7340032 | bytes 9175264 | tf_op jit(solution)/shard_map/add | solution.py:253
  323.3 2.8 copy.279
  326.2 3.3 fusion.157
  331.3 2.8 concatenate.36
  337.0 32.5 %all_to_all.36 = f32[256,1,557]{2,1,0:T(1,128)S(1)} all-to-all(f32[256,1,557]{2,1,0:T(1,128)S(1)} %all_to_all.29), channel_id=1, replica_groups=mesh['seq'=64,'batch'=4] {'seq','batch'}, dimensions={0} | all-to-all | bytes 1140736 | tf_op jit(solution)/shard_map/all_to_all | solution.py:165
  371.3 5.7 %all-to-all-start.5 = ((f32[256,1,557]{2,1,0:T(1,128)}), f32[256,1,557]{2,1,0:T(1,128)S(1)}, u32[]{:S(2)}, u32[]{:S(2)}) async-start(f32[256,1,557]{2,1,0:T(1,128)} %broadcast_in_dim.114), calls=%async_computation.5 | async-start | bytes 1310720 | tf_op jit(solution)/shard_map/all_to_all | solution.py:168
  377.0 6.7 %copy.300 = bf16[2,128,56,64]{3,2,1,0:T(8,128)(2,1)} copy(bf16[2,128,56,64]{1,3,2,0:T(8,128)(2,1)S(1)} %copy-done.10) | data formatting | bytes 3670016
  383.7 5.8 %reshape.368 = bf16[1,256,3584]{2,1,0:T(8,128)(2,1)} reshape(bf16[2,128,56,64]{3,2,1,0:T(8,128)(2,1)} %copy.300) | data formatting | bytes 3670016
  389.5 11.7 %all-to-all-done.5 = f32[256,1,557]{2,1,0:T(1,128)S(1)} async-done(((f32[256,1,557]{2,1,0:T(1,128)}), f32[256,1,557]{2,1,0:T(1,128)S(1)}, u32[]{:S(2)}, u32[]{:S(2)}) %all-to-all-start.5) | async-done | bytes 570400 | tf_op jit(solution)/shard_map/all_to_all | solution.py:168
  (221 shorter events, 55.7 us)
Async XLA Ops:
  0.6 58.0 %copy-start = (bf16[16,3584]{1,0:T(8,128)(2,1)S(1)}, bf16[16,3584]{1,0:T(8,128)(2,1)}, u32[]{:S(2)}) copy-start(bf16[16,3584]{1,0:T(8,128)(2,1)} %param.14) | copy-start | bytes 344068
  1.4 6.8 %collective-permute-start = (s32[3]{0:T(128)S(1)}, s32[3]{0:T(128)S(1)}, u32[]{:S(2)}, u32[]{:S(2)}) collective-permute-start(s32[3]{0:T(128)S(1)} %add_bitcast_fusion.1), channel_id=1, source_target_pairs={{0,4},{4,8},{8,12},{12,16},{16,20},{20,24},{24,28},{28,32},{32,36}... | collective-permute-start | bytes 44 | tf_op jit(solution)/shard_map/ppermute | solution.py:18
  6.4 10.1 %copy-start.30 = (pred[3584]{0:T(1024)(128)(4,1)}, pred[3584]{0:T(1024)(128)(4,1)S(1)}, u32[]{:S(2)}) copy-start(pred[3584]{0:T(1024)(128)(4,1)S(1)} %fusion.133) | copy-start | bytes 10756
  7.0 3.2 copy-start.49
  9.1 246.2 %copy-start.17 = (pred[259,16]{1,0:T(8,128)(4,1)}, pred[259,16]{1,0:T(8,128)(4,1)S(1)}, u32[]{:S(2)}) copy-start(pred[259,16]{1,0:T(8,128)(4,1)S(1)} %get-tuple-element.134) | copy-start | bytes 12436
  10.2 11.6 %copy-start.51 = (f32[56]{0:T(128)}, f32[56]{0:T(128)S(1)}, u32[]{:S(2)}) copy-start(f32[56]{0:T(128)S(1)} %get-tuple-element.113) | copy-start | bytes 676
  10.6 101.9 %copy-start.32 = (f32[2,1,56]{2,1,0:T(1,128)}, f32[2,1,56]{2,1,0:T(1,128)S(1)}, u32[]{:S(2)}) copy-start(f32[2,1,56]{2,1,0:T(1,128)S(1)} %slice.180) | copy-start | bytes 1348
  10.7 5.8 %copy-start.14 = (f32[2,128,56]{1,2,0:T(8,128)}, f32[2,128,56]{1,2,0:T(8,128)S(1)}, u32[]{:S(2)}) copy-start(f32[2,128,56]{1,2,0:T(8,128)S(1)} %copy.245) | copy-start | bytes 172036
  21.8 3.1 copy-start.47
  21.8 3.1 copy-start.45
  21.9 90.6 %copy-start.38 = (f32[56]{0:T(128)}, f32[56]{0:T(128)S(1)}, u32[]{:S(2)}) copy-start(f32[56]{0:T(128)S(1)} %get-tuple-element.143) | copy-start | bytes 676
  27.3 63.9 %all-to-all-start = ((f32[57,64,128]{2,0,1:T(8,128)}), f32[57,64,128]{2,0,1:T(8,128)}, u32[]{:S(2)}, u32[]{:S(2)}) async-start(f32[57,64,128]{2,0,1:T(8,128)} %copy.248), calls=%async_computation | async-start | bytes 4194304 | tf_op jit(solution)/shard_map/all_to_all | solution.py:215
  103.3 8.9 %copy-start.37 = (f32[3584]{0:T(1024)S(1)}, f32[3584]{0:T(1024)}, u32[]{:S(2)}) copy-start(f32[3584]{0:T(1024)} %param.20) | copy-start | bytes 43012
  105.6 51.8 %all-to-all-start.1 = ((f32[56,64,128]{2,0,1:T(8,128)}), f32[56,64,128]{2,0,1:T(8,128)}, u32[]{:S(2)}, u32[]{:S(2)}) async-start(f32[56,64,128]{2,0,1:T(8,128)} %copy.259), calls=%async_computation.1 | async-start | bytes 3670016 | tf_op jit(solution)/shard_map/all_to_all | solution.py:148
  112.5 64.4 %copy-start.35 = (f32[2,56]{1,0:T(2,128)}, f32[2,56]{1,0:T(2,128)S(1)}, u32[]{:S(2)}) copy-start(f32[2,56]{1,0:T(2,128)S(1)} %subtract_exponential_fusion.2) | copy-start | bytes 1348
  112.5 47.0 %copy-start.42 = (f32[56]{0:T(128)S(1)}, f32[56]{0:T(128)}, u32[]{:S(2)}) copy-start(f32[56]{0:T(128)} %param.19) | copy-start | bytes 676
  157.4 2.6 copy-start.9
  159.4 17.5 %copy-start.6 = (f32[56,64,128]{2,1,0:T(8,128)}, f32[56,64,128]{2,1,0:T(8,128)S(1)}, u32[]{:S(2)}) copy-start(f32[56,64,128]{2,1,0:T(8,128)S(1)} %copy.260) | copy-start | bytes 5505028
  160.0 5.5 %copy-start.7 = (bf16[2,128,56,64]{1,0,3,2:T(2,128)(2,1)S(1)}, bf16[2,128,56,64]{1,0,3,2:T(2,128)(2,1)}, u32[]{:S(2)}) copy-start(bf16[2,128,56,64]{1,0,3,2:T(2,128)(2,1)} %reshape_squeeze.3) | copy-start | bytes 5505028
  165.4 2.6 copy-start.13
  176.9 2.6 copy-start.4
  181.8 51.7 %all-to-all-start.2 = ((f32[56,64,128]{2,0,1:T(8,128)}), f32[56,64,128]{2,0,1:T(8,128)}, u32[]{:S(2)}, u32[]{:S(2)}) async-start(f32[56,64,128]{2,0,1:T(8,128)} %copy.266), calls=%async_computation.2 | async-start | bytes 3670016 | tf_op jit(solution)/shard_map/all_to_all | solution.py:242
  236.4 8.6 %copy-start.16 = (bf16[16,3840]{1,0:T(8,128)(2,1)S(1)}, bf16[16,3840]{1,0:T(8,128)(2,1)}, u32[]{:S(2)}) copy-start(bf16[16,3840]{1,0:T(8,128)(2,1)} %param.13) | copy-start | bytes 368644
  238.7 51.4 %all-to-all-start.3 = ((f32[56,64,128]{2,0,1:T(8,128)}), f32[56,64,128]{2,0,1:T(8,128)}, u32[]{:S(2)}, u32[]{:S(2)}) async-start(f32[56,64,128]{2,0,1:T(8,128)} %copy.274), calls=%async_computation.3 | async-start | bytes 3670016 | tf_op jit(solution)/shard_map/all_to_all | solution.py:155
  248.1 3.8 copy-start.8
  257.1 4.2 %copy-start.20 = (bf16[2,128,128]{2,1,0:T(8,128)(2,1)S(1)}, bf16[2,128,128]{2,1,0:T(8,128)(2,1)}, u32[]{:S(2)}) copy-start(bf16[2,128,128]{2,1,0:T(8,128)(2,1)} %fusion.177) | copy-start | bytes 196612
  257.1 35.0 %copy-start.39 = (f32[56]{0:T(128)S(1)}, f32[56]{0:T(128)}, u32[]{:S(2)}) copy-start(f32[56]{0:T(128)} %copy-done.38) | copy-start | bytes 676
  257.1 35.0 %copy-start.41 = (f32[56]{0:T(128)S(1)}, f32[56]{0:T(128)}, u32[]{:S(2)}) copy-start(f32[56]{0:T(128)} %copy-done.40) | copy-start | bytes 676
  292.1 4.2 %copy-start.3 = (f32[2,128,3584]{2,1,0:T(8,128)S(1)}, f32[2,128,3584]{2,1,0:T(8,128)}, u32[]{:S(2)}) copy-start(f32[2,128,3584]{2,1,0:T(8,128)} %copy-done.2) | copy-start | bytes 11010052
  301.3 5.1 %copy-start.52 = (f32[56]{0:T(128)S(1)}, f32[56]{0:T(128)}, u32[]{:S(2)}) copy-start(f32[56]{0:T(128)} %copy-done.51) | copy-start | bytes 676
  301.3 5.1 %copy-start.48 = (f32[1,56]{1,0:T(1,128)S(1)}, f32[1,56]{1,0:T(1,128)}, u32[]{:S(2)}) copy-start(f32[1,56]{1,0:T(1,128)} %copy-done.47) | copy-start | bytes 676
  301.4 5.1 %copy-start.54 = (f32[56]{0:T(128)S(1)}, f32[56]{0:T(128)}, u32[]{:S(2)}) copy-start(f32[56]{0:T(128)} %get-tuple-element.121) | copy-start | bytes 676
  301.4 5.1 %copy-start.46 = (f32[1,56]{1,0:T(1,128)S(1)}, f32[1,56]{1,0:T(1,128)}, u32[]{:S(2)}) copy-start(f32[1,56]{1,0:T(1,128)} %copy-done.45) | copy-start | bytes 676
  301.4 5.1 %copy-start.53 = (f32[56]{0:T(128)S(1)}, f32[56]{0:T(128)}, u32[]{:S(2)}) copy-start(f32[56]{0:T(128)} %get-tuple-element.107) | copy-start | bytes 676
  301.4 5.4 %copy-start.23 = (f32[256,56]{0,1:T(8,128)S(1)}, f32[256,56]{0,1:T(8,128)}, u32[]{:S(2)}) copy-start(f32[256,56]{0,1:T(8,128)} %copy-done.22) | copy-start | bytes 172036
  301.4 5.4 %copy-start.24 = (f32[256,56]{0,1:T(8,128)S(1)}, f32[256,56]{0,1:T(8,128)}, u32[]{:S(2)}) copy-start(f32[256,56]{0,1:T(8,128)} %copy.301) | copy-start | bytes 172036
  301.4 5.4 %copy-start.25 = (f32[256,56]{0,1:T(8,128)S(1)}, f32[256,56]{0,1:T(8,128)}, u32[]{:S(2)}) copy-start(f32[256,56]{0,1:T(8,128)} %copy.302) | copy-start | bytes 172036
  301.4 5.5 %copy-start.18 = (pred[259,16]{1,0:T(8,128)(4,1)S(1)}, pred[259,16]{1,0:T(8,128)(4,1)}, u32[]{:S(2)}) copy-start(pred[259,16]{1,0:T(8,128)(4,1)} %copy-done.17) | copy-start | bytes 12436
  301.4 5.5 %copy-start.28 = (f32[2,7,8,128]{3,2,1,0:T(8,128)S(1)}, f32[2,7,8,128]{3,2,1,0:T(8,128)}, u32[]{:S(2)}) copy-start(f32[2,7,8,128]{3,2,1,0:T(8,128)} %get-tuple-element.128) | copy-start | bytes 172036
  301.4 5.5 %copy-start.29 = (f32[256,56]{0,1:T(8,128)S(1)}, f32[256,56]{0,1:T(8,128)}, u32[]{:S(2)}) copy-start(f32[256,56]{0,1:T(8,128)} %copy_bitcast_fusion.1) | copy-start | bytes 172036
  301.4 5.5 %copy-start.50 = (f32[56]{0:T(128)S(1)}, f32[56]{0:T(128)}, u32[]{:S(2)}) copy-start(f32[56]{0:T(128)} %copy-done.49) | copy-start | bytes 676
  301.4 5.8 %copy-start.55 = (f32[56]{0:T(128)S(1)}, f32[56]{0:T(128)}, u32[]{:S(2)}) copy-start(f32[56]{0:T(128)} %param.16) | copy-start | bytes 676
  307.3 11.0 %copy-start.11 = (bf16[2,56,8,8,128]{4,3,0,2,1:T(8,128)(2,1)S(1)}, bf16[2,56,8,8,128]{4,3,0,2,1:T(8,128)(2,1)}, u32[]{:S(2)}) copy-start(bf16[2,56,8,8,128]{4,3,0,2,1:T(8,128)(2,1)} %copy.353) | copy-start | bytes 5505028
  307.3 11.0 %copy-start.43 = (f32[56]{0:T(128)S(1)}, f32[56]{0:T(128)}, u32[]{:S(2)}) copy-start(f32[56]{0:T(128)} %param.19) | copy-start | bytes 676
  323.3 2.8 copy-start.19
  331.3 45.7 %copy-start.10 = (bf16[2,128,56,64]{1,3,2,0:T(8,128)(2,1)S(1)}, bf16[2,128,56,64]{1,3,2,0:T(8,128)(2,1)}, u32[]{:S(2)}) copy-start(bf16[2,128,56,64]{1,3,2,0:T(8,128)(2,1)} %get-tuple-element.116) | copy-start | bytes 5505028
  371.3 29.9 %all-to-all-start.5 = ((f32[256,1,557]{2,1,0:T(1,128)}), f32[256,1,557]{2,1,0:T(1,128)S(1)}, u32[]{:S(2)}, u32[]{:S(2)}) async-start(f32[256,1,557]{2,1,0:T(1,128)} %broadcast_in_dim.114), calls=%async_computation.5 | async-start | bytes 1310720 | tf_op jit(solution)/shard_map/all_to_all | solution.py:168
  383.7 24.4 %copy-start.1 = (bf16[16,3584]{1,0:T(8,128)(2,1)S(1)}, bf16[16,3584]{1,0:T(8,128)(2,1)}, u32[]{:S(2)}) copy-start(bf16[16,3584]{1,0:T(8,128)(2,1)} %param.14) | copy-start | bytes 344068
  (14 other events, 21.6 us)

commit v6 on v3

--- a/solution.py
+++ b/solution.py
@@ -154,6 +154,7 @@
         count *= lax.axis_size(axis)
     size = flat.shape[0]
     chunk = -(-size // count)
+    chunk = -(-chunk // 128) * 128
     padded = jnp.pad(flat, (0, chunk * count - size)).reshape(count, chunk)
     gathered = lax.all_to_all(padded, axes, split_axis=0, concat_axis=0, tiled=True)
     reduced = jnp.sum(gathered, axis=0, keepdims=True)

time: 409 us -> 404 us (0.988)
  no operation moved by 1% of the time
where the time goes in v6:
time: 404 us; the launch traced here: 397 us
  waiting for transfers between devices  141 us (35%)
  local copies, waits for them, and re-layouts  82.5 us (20%)
  matrix products  49.8 us (12%)
  other arithmetic  45.7 us (11%)
  starting transfers between devices  43 us (11%)
  blocking collectives  32.5 us (8%)
    all_to_all x1, waiting for transfers between devices, settle_forward(): lax.all_to_all(settled, 'seq', split_axis=1, concat_axis=1, tiled=True)  42.1 us
    all_to_all x1, blocking collectives, spread_sum(): lax.all_to_all(padded, axes, split_axis=0, concat_axis=0, tiled=True)  32.5 us
    all_to_all x1, waiting for transfers between devices, settle_backward(): lax.all_to_all(settled, 'seq', split_axis=1, concat_axis=1, tiled=True)  31.6 us
    all_to_all x1, waiting for transfers between devices, local(): lax.all_to_all(outgoing, 'seq', split_axis=1, concat_axis=1, tiled=True)  30 us
    all_to_all x1, waiting for transfers between devices, local(): lax.all_to_all(back_flat.reshape(heads, parts, span), 'seq', split_axis=1...  25.9 us
    unnamed x81, local copies, waits for them, and re-layouts  21.3 us
    dot_general x3, matrix products, intra(): jnp.einsum('chts,cshp->cthp', mixing, blocked, preferred_element_type=jnp...  17.4 us
    all_to_all x1, starting transfers between devices, local(): lax.all_to_all(outgoing, 'seq', split_axis=1, concat_axis=1, tiled=True)  13.2 us
  transfers between devices with their start and end apart: 6, of which 5 were waited for; matrix products, arithmetic and copies ran while one was open for 18% of the time, Pallas kernels for 0%

profile of v6, /device:TPU:1, one launch (start us, length us, event | category | flops | bytes accessed | tf_op | source)
XLA Modules:
  0.0 396.7 jit_solution(15463790658720853640)
XLA Ops:
  1.4 4.9 %collective-permute-start = (s32[3]{0:T(128)S(1)}, s32[3]{0:T(128)S(1)}, u32[]{:S(2)}, u32[]{:S(2)}) collective-permute-start(s32[3]{0:T(128)S(1)} %add_bitcast_fusion.1), channel_id=1, source_target_pairs={{0,4},{4,8},{8,12},{12,16},{16,20},{20,24},{24,28},{28,32},{32,36}... | collective-permute-start | bytes 44 | tf_op jit(solution)/shard_map/ppermute | solution.py:18
  10.7 3.8 multiply_convert_fusion.1
  16.9 3.5 reshape.364
  20.5 5.8 %copy.347 = bf16[2,128,56,64]{1,3,2,0:T(8,128)(2,1)S(1)} copy(bf16[2,128,56,64]{3,2,1,0:T(8,128)(2,1)} %reshape.364) | data formatting | bytes 3670016 | tf_op jit(solution)/shard_map/jvp()/reshape;jvp()/reshape | solution.py:51
  29.0 2.4 copy.351
  31.4 13.2 %all-to-all-start = ((f32[57,64,128]{2,0,1:T(8,128)}), f32[57,64,128]{2,0,1:T(8,128)}, u32[]{:S(2)}, u32[]{:S(2)}) async-start(f32[57,64,128]{2,0,1:T(8,128)} %copy.351), calls=%async_computation | async-start | bytes 4194304 | tf_op jit(solution)/shard_map/all_to_all | solution.py:209
  44.6 3.8 copy.357
  48.4 4.6 %reshape_squeeze.3 = bf16[2,128,56,64]{1,0,3,2:T(2,128)(2,1)} reshape(bf16[1,256,3584]{1,2,0:T(8,128)(2,1)} %copy.357) | data formatting | bytes 3670016 | tf_op jit(solution)/shard_map/reshape;squeeze | solution.py:213
  53.2 2.5 fusion.124
  55.7 5.4 %reshape.332 = f32[2,128,56,64]{1,0,3,2:T(2,128)} reshape(f32[256,3584]{0,1:T(8,128)} %fusion.124) | data formatting | bytes 7340032 | tf_op jit(solution)/shard_map/reshape | solution.py:212
  61.3 4.4 %fusion.46 = f32[2,128,56,64]{1,3,2,0:T(8,128)} fusion(bf16[2,128,56,64]{1,3,2,0:T(8,128)(2,1)S(1)} %copy.347, f32[2,56,128]{2,1,0:T(8,128)S(1)} %copy.354, f32[2,56,128]{2,1,0:T(8,128)S(1)} %copy.352, f32[2,128,128]{2,1,0:T(8,128)S(1)} %fusion.165, pred[128,128]{1,0:T(8,128)(4,1)S(1)} %iota_compare_fusion.2), kind=kOutput, calls=%fused_computation.73 | convolution fusion | flops 245891072 | bytes 5767168 | tf_op jit(solution)/shard_map/jvp(chts,cshp->cthp)/dot_general | solution.py:91
  65.7 30.0 %all-to-all-done = f32[57,64,128]{2,0,1:T(8,128)} async-done(((f32[57,64,128]{2,0,1:T(8,128)}), f32[57,64,128]{2,0,1:T(8,128)}, u32[]{:S(2)}, u32[]{:S(2)}) %all-to-all-start) | async-done | bytes 1867808 | tf_op jit(solution)/shard_map/all_to_all | solution.py:209
  95.6 3.7 copy.359
  99.3 3.9 copy.360
  105.0 2.7 fusion.50
  107.7 2.3 copy.361
  110.0 6.3 %all-to-all-start.1 = ((f32[56,64,128]{2,0,1:T(8,128)}), f32[56,64,128]{2,0,1:T(8,128)}, u32[]{:S(2)}, u32[]{:S(2)}) async-start(f32[56,64,128]{2,0,1:T(8,128)} %copy.361), calls=%async_computation.1 | async-start | bytes 3670016 | tf_op jit(solution)/shard_map/all_to_all | solution.py:141
  116.5 2.9 slice_add_fusion
  119.4 42.1 %all-to-all-done.1 = f32[56,64,128]{2,0,1:T(8,128)} async-done(((f32[56,64,128]{2,0,1:T(8,128)}), f32[56,64,128]{2,0,1:T(8,128)}, u32[]{:S(2)}, u32[]{:S(2)}) %all-to-all-start.1) | async-done | bytes 1835040 | tf_op jit(solution)/shard_map/all_to_all | solution.py:141
  164.1 4.9 %multiply_reduce_fusion.3 = (f32[2,128]{1,0:T(2,128)S(1)}, f32[2,128,56,64]{1,3,2,0:T(8,128)S(1)}, f32[2,128,56,64]{1,3,2,0:T(8,128)S(1)}) fusion(f32[2,128,56,64]{1,0,3,2:T(2,128)S(1)} %copy-done.11, bf16[2,128,56,64]{1,3,2,0:T(8,128)(2,1)S(1)} %copy.347, f32[56]{0:T(128)S(1)} %copy-done.32, f32[2,128,56,64]{1,3,2,0:T(8,128)} %fusion.46, ...), kind=kOutput, calls=%fused_computation.61 | convolution fusion | flops 248643328 | bytes 20309664 | tf_op jit(solution)/shard_map/jvp(ctn,chpn->cthp)/dot_general | solution.py:113
  172.4 5.6 %fusion.47 = (bf16[2,56,8,8,128]{4,3,2,1,0:T(8,128)(2,1)}, f32[2,128,56,64]{1,3,2,0:T(8,128)S(1)}, f32[2,128,56,64]{1,3,2,0:T(8,128)}, bf16[2,128,56,64]{1,3,2,0:T(8,128)(2,1)}) fusion(f32[56]{0:T(128)S(1)} %copy-done.32, f32[2,128,56,64]{1,0,3,2:T(2,128)S(1)} %copy-done.11, f32[2,128,56,64]{1,3,2,0:T(8,128)S(1)} %get-tuple-element.130, ...), kind=kLoop, calls=%fused_computation.75 | loop fusion | flops 25690112 | bytes 29434080
  178.0 2.5 multiply_reduce_fusion
  180.4 2.3 copy.367
  182.7 6.5 %all-to-all-start.2 = ((f32[56,64,128]{2,0,1:T(8,128)}), f32[56,64,128]{2,0,1:T(8,128)}, u32[]{:S(2)}, u32[]{:S(2)}) async-start(f32[56,64,128]{2,0,1:T(8,128)} %copy.367), calls=%async_computation.2 | async-start | bytes 3670016 | tf_op jit(solution)/shard_map/all_to_all | solution.py:236
  189.2 8.5 %fusion.10 = (f32[2,56,128]{2,1,0:T(8,128)S(1)}, f32[2,56,128]{2,1,0:T(8,128)S(1)}, f32[2,56,128]{2,1,0:T(8,128)S(1)}, bf16[2,128,128]{2,1,0:T(8,128)(2,1)S(1)}) fusion(f32[2,56,128]{2,1,0:T(8,128)S(1)} %copy.354, f32[2,56,128]{2,1,0:T(8,128)S(1)} %copy.352, f32[2,128,128]{2,1,0:T(8,128)S(1)} %fusion.165, pred[128,128]{1,0:T(8,128)(4,1)S(1)} %iota_compare_fusion.2, ...), kind=kOutput, calls=%fused_computation.19 | convolution fusion | flops 264165376 | bytes 6004736 | tf_op jit(solution)/shard_map/transpose(jvp(chts,cshp->cthp))/dot_general | solution.py:91
  197.9 2.2 reduce_window_sum.75
  200.8 4.5 %convert_bitcast_fusion = bf16[2,56,8,8,128]{4,3,2,1,0:T(8,128)(2,1)S(1)} fusion(f32[2,56,128]{2,1,0:T(8,128)S(1)} %copy.354, f32[2,56,128]{2,1,0:T(8,128)S(1)} %copy.352, f32[2,128,128]{2,1,0:T(8,128)S(1)} %fusion.165, pred[128,128]{1,0:T(8,128)(4,1)S(1)} %iota_compare_fusion.2, f32[2,128,56,64]{1,3,2,0:T(8,128)} %copy-done.2), kind=kOutput, calls=%fused_computation.96 | convolution fusion | flops 245891072 | bytes 5767168 | tf_op jit(solution)/shard_map/transpose(jvp(chts,cshp->cthp))/dot_general | solution.py:91
  208.5 25.9 %all-to-all-done.2 = f32[56,64,128]{2,0,1:T(8,128)} async-done(((f32[56,64,128]{2,0,1:T(8,128)}), f32[56,64,128]{2,0,1:T(8,128)}, u32[]{:S(2)}, u32[]{:S(2)}) %all-to-all-start.2) | async-done | bytes 1835040 | tf_op jit(solution)/shard_map/all_to_all | solution.py:236
  234.4 2.9 fusion.53
  237.4 2.3 copy.375
  239.7 6.5 %all-to-all-start.3 = ((f32[56,64,128]{2,0,1:T(8,128)}), f32[56,64,128]{2,0,1:T(8,128)S(1)}, u32[]{:S(2)}, u32[]{:S(2)}) async-start(f32[56,64,128]{2,0,1:T(8,128)} %copy.375), calls=%async_computation.3 | async-start | bytes 3670016 | tf_op jit(solution)/shard_map/all_to_all | solution.py:148
  247.0 4.1 %convert_element_type.92 = f32[2,56,64,128]{3,2,1,0:T(8,128)} convert(bf16[2,56,64,128]{3,2,1,0:T(8,128)(2,1)} %get-tuple-element.159) | non-fusion elementwise | flops 917504 | bytes 5505024 | tf_op jit(solution)/shard_map/transpose(jvp())/convert_element_type | solution.py:114
  251.1 3.3 copy.382
  255.6 4.2 %fusion.81 = bf16[2,128,128]{2,1,0:T(8,128)(2,1)S(1)} fusion(f32[2,128,56,64]{1,3,2,0:T(8,128)} %copy-done.2, f32[2,128,56]{1,2,0:T(8,128)S(1)} %copy.358, f32[1,56,64,128]{3,2,1,0:T(8,128)} %slice_add_fusion, f32[56,64,128]{2,1,0:T(8,128)} %copy-done.6, f32[2,56]{1,0:T(2,128)S(1)} %subtract_exponential_fusion.1), kind=kOutput, calls=%fused_computation.111 | convolution fusion | flops 238583808 | bytes 7463360 | tf_op jit(solution)/shard_map/transpose(jvp(ctn,chpn->cthp))/dot_general | solution.py:113
  259.8 31.6 %all-to-all-done.3 = f32[56,64,128]{2,0,1:T(8,128)S(1)} async-done(((f32[56,64,128]{2,0,1:T(8,128)}), f32[56,64,128]{2,0,1:T(8,128)S(1)}, u32[]{:S(2)}, u32[]{:S(2)}) %all-to-all-start.3) | async-done | bytes 1835040 | tf_op jit(solution)/shard_map/all_to_all | solution.py:148
  291.4 2.5 fusion.121
  294.6 4.6 %fusion.27 = (f32[56]{0:T(128)S(1)}, f32[2,128,56]{1,2,0:T(8,128)S(1)}, f32[2,128,56]{1,2,0:T(8,128)S(1)}, bf16[2,56,8,8,128]{4,3,2,1,0:T(8,128)(2,1)}) fusion(f32[2,128,56,64]{1,3,2,0:T(8,128)S(1)} %copy-done.3, bf16[2,128,56,64]{1,3,2,0:T(8,128)(2,1)S(1)} %copy-done.8, f32[2,128,56,64]{1,3,2,0:T(8,128)} %copy-done.12, f32[2,128,56]{1,2,0:T(8,128)S(1)} %copy.350, ...), kind=kOutput, calls=%fused_computation.47 | convolution fusion | flops 247697344 | bytes 13082848 | tf_op jit(solution)/shard_map/transpose(jvp(cshp,csn->chpn))/dot_general | solution.py:52
  300.3 2.2 reduce_window_sum.79
  307.7 3.1 multiply_reduce_fusion.5
  311.7 4.3 %bitcast_add_fusion = bf16[256,56,64]{0,2,1:T(8,128)(2,1)} fusion(bf16[2,56,8,8,128]{4,3,2,1,0:T(8,128)(2,1)} %get-tuple-element.139, bf16[256,56,64]{0,2,1:T(8,128)(2,1)} %bitcast.187, bf16[2,56,8,8,128]{4,3,2,1,0:T(8,128)(2,1)} %get-tuple-element.127), kind=kLoop, calls=%fused_computation.77 | loop fusion | flops 1835008 | bytes 7340032 | tf_op jit(solution)/shard_map/add | solution.py:247
  315.9 2.8 copy.380
  318.8 3.3 fusion.150
  324.0 2.8 concatenate.29
  326.9 32.5 %all_to_all.35 = f32[256,1,640]{2,1,0:T(1,128)S(1)} all-to-all(f32[256,1,640]{2,1,0:T(1,128)S(1)} %bitcast.190), channel_id=1, replica_groups=mesh['seq'=64,'batch'=4] {'seq','batch'}, dimensions={0} | all-to-all | bytes 1310720 | tf_op jit(solution)/shard_map/all_to_all | solution.py:159
  361.1 5.7 %all-to-all-start.5 = ((f32[256,1,640]{2,1,0:T(1,128)}), f32[256,1,640]{2,1,0:T(1,128)S(1)}, u32[]{:S(2)}, u32[]{:S(2)}) async-start(f32[256,1,640]{2,1,0:T(1,128)} %broadcast_in_dim.121), calls=%async_computation.5 | async-start | bytes 1310720 | tf_op jit(solution)/shard_map/all_to_all | solution.py:162
  366.8 6.7 %copy.403 = bf16[2,128,56,64]{3,2,1,0:T(8,128)(2,1)} copy(bf16[2,128,56,64]{1,3,2,0:T(8,128)(2,1)S(1)} %copy-done.13) | data formatting | bytes 3670016
  373.5 5.8 %reshape.363 = bf16[1,256,3584]{2,1,0:T(8,128)(2,1)} reshape(bf16[2,128,56,64]{3,2,1,0:T(8,128)(2,1)} %copy.403) | data formatting | bytes 3670016
  379.2 11.7 %all-to-all-done.5 = f32[256,1,640]{2,1,0:T(1,128)S(1)} async-done(((f32[256,1,640]{2,1,0:T(1,128)}), f32[256,1,640]{2,1,0:T(1,128)S(1)}, u32[]{:S(2)}, u32[]{:S(2)}) %all-to-all-start.5) | async-done | bytes 655392 | tf_op jit(solution)/shard_map/all_to_all | solution.py:162
  (175 shorter events, 41.0 us)
Async XLA Ops:
  0.6 52.5 %copy-start = (bf16[16,3584]{1,0:T(8,128)(2,1)S(1)}, bf16[16,3584]{1,0:T(8,128)(2,1)}, u32[]{:S(2)}) copy-start(bf16[16,3584]{1,0:T(8,128)(2,1)} %param.14) | copy-start | bytes 344068
  1.4 6.7 %collective-permute-start = (s32[3]{0:T(128)S(1)}, s32[3]{0:T(128)S(1)}, u32[]{:S(2)}, u32[]{:S(2)}) collective-permute-start(s32[3]{0:T(128)S(1)} %add_bitcast_fusion.1), channel_id=1, source_target_pairs={{0,4},{4,8},{8,12},{12,16},{16,20},{20,24},{24,28},{28,32},{32,36}... | collective-permute-start | bytes 44 | tf_op jit(solution)/shard_map/ppermute | solution.py:18
  7.0 7.7 %copy-start.36 = (f32[56]{0:T(128)}, f32[56]{0:T(128)S(1)}, u32[]{:S(2)}) copy-start(f32[56]{0:T(128)S(1)} %exponential_negate_fusion) | copy-start | bytes 676
  9.1 245.4 %copy-start.19 = (pred[259,16]{1,0:T(8,128)(4,1)}, pred[259,16]{1,0:T(8,128)(4,1)S(1)}, u32[]{:S(2)}) copy-start(pred[259,16]{1,0:T(8,128)(4,1)S(1)} %get-tuple-element.156) | copy-start | bytes 12436
  9.1 1.7 copy-start.26
  14.6 0.7 copy-start.33
  16.2 10.3 %copy-start.35 = (f32[56]{0:T(128)}, f32[56]{0:T(128)S(1)}, u32[]{:S(2)}) copy-start(f32[56]{0:T(128)S(1)} %get-tuple-element.133) | copy-start | bytes 676
  26.3 163.0 %copy-start.7 = (bf16[2,128,56,64]{1,3,2,0:T(8,128)(2,1)}, bf16[2,128,56,64]{1,3,2,0:T(8,128)(2,1)S(1)}, u32[]{:S(2)}) copy-start(bf16[2,128,56,64]{1,3,2,0:T(8,128)(2,1)S(1)} %copy.347) | copy-start | bytes 5505028
  26.4 1.3 copy-start.28
  26.5 0.9 copy-start.30
  27.2 1.8 copy-start.4
  31.4 64.2 %all-to-all-start = ((f32[57,64,128]{2,0,1:T(8,128)}), f32[57,64,128]{2,0,1:T(8,128)}, u32[]{:S(2)}, u32[]{:S(2)}) async-start(f32[57,64,128]{2,0,1:T(8,128)} %copy.351), calls=%async_computation | async-start | bytes 4194304 | tf_op jit(solution)/shard_map/all_to_all | solution.py:209
  107.7 8.6 %copy-start.27 = (f32[3584]{0:T(1024)S(1)}, f32[3584]{0:T(1024)}, u32[]{:S(2)}) copy-start(f32[3584]{0:T(1024)} %param.20) | copy-start | bytes 43012
  110.0 51.5 %all-to-all-start.1 = ((f32[56,64,128]{2,0,1:T(8,128)}), f32[56,64,128]{2,0,1:T(8,128)}, u32[]{:S(2)}, u32[]{:S(2)}) async-start(f32[56,64,128]{2,0,1:T(8,128)} %copy.361), calls=%async_computation.1 | async-start | bytes 3670016 | tf_op jit(solution)/shard_map/all_to_all | solution.py:141
  116.5 47.0 %copy-start.32 = (f32[56]{0:T(128)S(1)}, f32[56]{0:T(128)}, u32[]{:S(2)}) copy-start(f32[56]{0:T(128)} %param.19) | copy-start | bytes 676
  161.5 2.6 copy-start.11
  163.5 14.5 %copy-start.6 = (f32[56,64,128]{2,1,0:T(8,128)}, f32[56,64,128]{2,1,0:T(8,128)S(1)}, u32[]{:S(2)}) copy-start(f32[56,64,128]{2,1,0:T(8,128)S(1)} %copy.362) | copy-start | bytes 5505028
  164.1 4.9 %copy-start.9 = (bf16[2,128,56,64]{1,0,3,2:T(2,128)(2,1)S(1)}, bf16[2,128,56,64]{1,0,3,2:T(2,128)(2,1)}, u32[]{:S(2)}) copy-start(bf16[2,128,56,64]{1,0,3,2:T(2,128)(2,1)} %reshape_squeeze.3) | copy-start | bytes 5505028
  169.0 9.0 %copy-start.12 = (f32[2,128,56,64]{1,3,2,0:T(8,128)}, f32[2,128,56,64]{1,3,2,0:T(8,128)S(1)}, u32[]{:S(2)}) copy-start(f32[2,128,56,64]{1,3,2,0:T(8,128)S(1)} %get-tuple-element.158) | copy-start | bytes 11010052
  169.0 3.4 copy-start.14
  178.0 2.5 copy-start.2
  182.7 51.7 %all-to-all-start.2 = ((f32[56,64,128]{2,0,1:T(8,128)}), f32[56,64,128]{2,0,1:T(8,128)}, u32[]{:S(2)}, u32[]{:S(2)}) async-start(f32[56,64,128]{2,0,1:T(8,128)} %copy.367), calls=%async_computation.2 | async-start | bytes 3670016 | tf_op jit(solution)/shard_map/all_to_all | solution.py:236
  237.4 8.8 %copy-start.18 = (bf16[16,3840]{1,0:T(8,128)(2,1)S(1)}, bf16[16,3840]{1,0:T(8,128)(2,1)}, u32[]{:S(2)}) copy-start(bf16[16,3840]{1,0:T(8,128)(2,1)} %param.13) | copy-start | bytes 368644
  239.7 51.7 %all-to-all-start.3 = ((f32[56,64,128]{2,0,1:T(8,128)}), f32[56,64,128]{2,0,1:T(8,128)S(1)}, u32[]{:S(2)}, u32[]{:S(2)}) async-start(f32[56,64,128]{2,0,1:T(8,128)} %copy.375), calls=%async_computation.3 | async-start | bytes 3670016 | tf_op jit(solution)/shard_map/all_to_all | solution.py:148
  246.1 4.9 %copy-start.10 = (f32[2,128,56,64]{1,3,2,0:T(8,128)S(1)}, f32[2,128,56,64]{1,3,2,0:T(8,128)}, u32[]{:S(2)}) copy-start(f32[2,128,56,64]{1,3,2,0:T(8,128)} %get-tuple-element.135) | copy-start | bytes 11010052
  291.4 2.6 copy-start.3
  291.4 3.2 copy-start.8
  305.0 2.8 copy-start.5
  306.9 3.9 copy-start.31
  306.9 3.9 copy-start.29
  306.9 4.2 %copy-start.23 = (f32[256,56]{0,1:T(8,128)S(1)}, f32[256,56]{0,1:T(8,128)}, u32[]{:S(2)}) copy-start(f32[256,56]{0,1:T(8,128)} %copy.404) | copy-start | bytes 172036
  306.9 4.2 %copy-start.25 = (f32[256,56]{0,1:T(8,128)S(1)}, f32[256,56]{0,1:T(8,128)}, u32[]{:S(2)}) copy-start(f32[256,56]{0,1:T(8,128)} %get-tuple-element.157) | copy-start | bytes 172036
  307.0 4.3 %copy-start.20 = (pred[259,16]{1,0:T(8,128)(4,1)S(1)}, pred[259,16]{1,0:T(8,128)(4,1)}, u32[]{:S(2)}) copy-start(pred[259,16]{1,0:T(8,128)(4,1)} %copy-done.19) | copy-start | bytes 12436
  307.0 4.3 %copy-start.24 = (f32[256,56]{0,1:T(8,128)S(1)}, f32[256,56]{0,1:T(8,128)}, u32[]{:S(2)}) copy-start(f32[256,56]{0,1:T(8,128)} %copy_bitcast_fusion.2) | copy-start | bytes 172036
  307.0 4.3 %copy-start.37 = (f32[56]{0:T(128)S(1)}, f32[56]{0:T(128)}, u32[]{:S(2)}) copy-start(f32[56]{0:T(128)} %copy-done.36) | copy-start | bytes 676
  307.0 4.6 %copy-start.34 = (f32[56]{0:T(128)S(1)}, f32[56]{0:T(128)}, u32[]{:S(2)}) copy-start(f32[56]{0:T(128)} %param.16) | copy-start | bytes 676
  315.9 2.8 copy-start.21
  318.8 3.4 copy-start.15
  318.8 3.4 copy-start.16
  318.8 3.4 copy-start.17
  322.1 1.7 copy-start.22
  323.9 42.8 %copy-start.13 = (bf16[2,128,56,64]{1,3,2,0:T(8,128)(2,1)S(1)}, bf16[2,128,56,64]{1,3,2,0:T(8,128)(2,1)}, u32[]{:S(2)}) copy-start(bf16[2,128,56,64]{1,3,2,0:T(8,128)(2,1)} %get-tuple-element.136) | copy-start | bytes 5505028
  361.1 29.9 %all-to-all-start.5 = ((f32[256,1,640]{2,1,0:T(1,128)}), f32[256,1,640]{2,1,0:T(1,128)S(1)}, u32[]{:S(2)}, u32[]{:S(2)}) async-start(f32[256,1,640]{2,1,0:T(1,128)} %broadcast_in_dim.121), calls=%async_computation.5 | async-start | bytes 1310720 | tf_op jit(solution)/shard_map/all_to_all | solution.py:162
  366.8 29.7 %copy-start.1 = (bf16[16,3584]{1,0:T(8,128)(2,1)S(1)}, bf16[16,3584]{1,0:T(8,128)(2,1)}, u32[]{:S(2)}) copy-start(bf16[16,3584]{1,0:T(8,128)(2,1)} %param.14) | copy-start | bytes 344068
